TPU v7x, 32 devices: a whole 2x2x4 slice. The times are simulated.
32 devices in a mesh: img: 4 (over z), ref: 8 (over y, x, core).
Axes of the slice: x: 2, y: 2, z: 4, core: 2. Of those that a mesh axis runs over, the one named last changes fastest.
Arguments:
- images: bfloat16 [2048, 9216], P(('img', 'ref')), may hold values from -96 to 96
- references: bfloat16 [6912, 9216], P('ref'), may hold values from -0.5 to 0.5
- class_prior: float32 [192], P('ref'), may hold values from 0.2 to 5
Outputs:
- class_sums: float32 [192, 9216], P('ref', 'img')
- class_weights: float32 [192], P('ref')
All inputs are finite; a program needn't handle non-finite values.
Results may differ from a plain program's by a relative error of at most 0.0021.
Values may be sent and summed in bfloat16 or wider, within the bound.
No kernel may reach another device: no remote copies, remote signals or barrier semaphores. Data moves between devices by JAX's collectives and lax.ppermute only.
A program may use at most 128 MiB of HBM per device.

v0:
```python
import jax
import jax.numpy as jnp
from jax import lax
from jax.sharding import PartitionSpec as P

ANG = 144


def unturn(stacked, shift_size):
    classes_here, rotations, columns = stacked.shape
    cycles = stacked.reshape(classes_here, rotations, columns // ANG, ANG)
    doubled = jnp.concatenate([cycles, cycles], axis=3)
    result = doubled[:, 0, :, 0:ANG]
    for turn_index in range(1, rotations):
        start_col = turn_index * shift_size
        result = result + doubled[:, turn_index, :, start_col : start_col + ANG]
    return result.reshape(classes_here, columns)


def per_device(images, references, class_prior):
    local_refs, pixels = references.shape
    classes_here = class_prior.shape[0]
    rotations = local_refs // classes_here
    shift_size = ANG // rotations
    half_norm = 0.5 * jnp.einsum(
        "jp,jp->j", references, references, preferred_element_type=jnp.float32
    )
    offsets = (jnp.log(class_prior)[:, None] - half_norm.reshape(classes_here, rotations)).reshape(
        local_refs
    )
    gathered = lax.all_gather(images, "ref", axis=0, tiled=True)
    products = lax.dot_general(
        gathered, references, (((1,), (1,)), ((), ())), preferred_element_type=jnp.float32
    )
    scores = products + offsets
    local_max = jnp.max(scores, axis=1)
    top_score = lax.pmax(local_max, "ref")
    denominator = lax.psum(jnp.sum(jnp.exp(scores - top_score[:, None]), axis=1), "ref")
    weights = (jnp.exp(scores - top_score[:, None]) / denominator[:, None]).astype(jnp.bfloat16)
    local_mass = (
        jnp.sum(weights.astype(jnp.float32), axis=0).reshape(classes_here, rotations).sum(axis=1)
    )
    class_weights = lax.psum(local_mass, "img")
    sums = lax.dot_general(
        weights, gathered, (((0,), (0,)), ((), ())), preferred_element_type=jnp.float32
    )
    reduced = lax.psum_scatter(sums, "img", scatter_dimension=1, tiled=True)
    class_sums = unturn(reduced.reshape(classes_here, rotations, -1), shift_size)
    return (class_sums, class_weights)


def solution(mesh):
    placed = (P(("img", "ref"), None), P("ref", None), P("ref"))
    return jax.shard_map(
        per_device,
        mesh=mesh,
        in_specs=placed,
        out_specs=(P("ref", "img"), P("ref")),
        check_vma=False,
    )
```

profile of v0, /device:TPU:0, one launch (start us, length us, event | category | flops | bytes accessed | tf_op | source)
XLA Modules:
  0.0 719.0 jit_solution(10911316544609606139)
XLA Ops:
  7.2 0.7 all-gather.2.cloned.1.call-update
  7.9 0.7 log.3
  8.8 7.0 fusion
  15.8 55.7 %all-gather.2.cloned.1.call-done = bf16[512,9216]{1,0:T(8,128)(2,1)} async-done(((bf16[64,9216]{1,0:T(8,128)(2,1)}), bf16[512,9216]{1,0:T(8,128)(2,1)}) %all-gather.2.cloned.1.call-update) | async-done | bytes 9437200 | tf_op jit(solution)/shard_map/all_gather | solution.py:31
  71.4 14.2 %add_reduce_fusion = (f32[512]{0:T(512)S(1)}, f32[512,864]{0,1:T(8,128)S(1)}) fusion(f32[864]{0:T(1024)S(1)} %multiply_subtract_fusion, bf16[512,9216]{1,0:T(8,128)(2,1)} %all-gather.2.cloned.1.call-done, bf16[864,9216]{1,0:T(8,128)(2,1)} %param.4), kind=kOutput, calls=%fused_computation.5 | convolution fusion | flops 8154611200 | bytes 27137408 | tf_op jit(solution)/shard_map/dot_general | solution.py:32
  85.6 13.1 %pmax.7 = f32[512]{0:T(512)S(1)} all-reduce(f32[512]{0:T(512)S(1)} %get-tuple-element.22), channel_id=1, replica_groups=mesh['img'=4,'ref'=8] {'ref'}, use_global_device_ids=true, to_apply=%region_1.0 | all-reduce | flops 512 | bytes 4096 | tf_op jit(solution)/shard_map/pmax | solution.py:37
  98.7 0.4 fusion.1
  99.1 11.8 %psum.14 = f32[512]{0:T(512)S(1)} all-reduce(f32[512]{0:T(512)S(1)} %fusion.1), channel_id=1, replica_groups=mesh['img'=4,'ref'=8] {'ref'}, use_global_device_ids=true, to_apply=%region_3.0 | all-reduce | flops 512 | bytes 4096 | tf_op jit(solution)/shard_map/psum | solution.py:38
  110.9 0.5 convert_reduce_fusion
  111.4 17.6 %fusion.2 = f32[864,9216]{1,0:T(8,128)} fusion(bf16[512,864]{0,1:T(8,128)(2,1)S(1)} %get-tuple-element.3, bf16[512,9216]{1,0:T(8,128)(2,1)} %all-gather.2.cloned.1.call-done), kind=kOutput, calls=%fused_computation.44 | convolution fusion | flops 8153726976 | bytes 42172416 | tf_op jit(solution)/shard_map/dot_general | solution.py:44
  129.2 12.4 %psum.15 = f32[24]{0:T(128)} all-reduce(f32[24]{0:T(128)S(1)} %reduce_sum.29), channel_id=1, replica_groups=mesh['img'=4,'ref'=8] {'img'}, use_global_device_ids=true, to_apply=%region_7.0 | all-reduce | flops 24 | bytes 192 | tf_op jit(solution)/shard_map/psum | solution.py:43
  141.6 513.8 %reduce-scatter.2.cloned.1.call-done = f32[864,2304]{1,0:T(8,128)} async-done(((f32[864,9216]{1,0:T(8,128)}), f32[864,2304]{1,0:T(8,128)}) %reduce-scatter.2.cloned.1.call-update) | async-done | bytes 7962640 | tf_op jit(solution)/shard_map/reduce_scatter | solution.py:47
  655.4 15.2 %reshape_reshape.3 = f32[24,36,16,144]{3,2,1,0:T(8,128)} reshape(f32[864,2304]{1,0:T(8,128)} %reduce-scatter.2.cloned.1.call-done) | data formatting | bytes 15925248 | tf_op jit(solution)/shard_map/reshape;reshape | solution.py:11
  670.6 8.5 %maximum_add_fusion = f32[24,1,16,144]{3,2,1,0:T(8,128)} fusion(f32[24,36,16,144]{3,2,1,0:T(8,128)} %reshape_reshape.3), kind=kLoop, calls=%fused_computation.26 | loop fusion | flops 1769472 | bytes 14770176 | tf_op jit(solution)/shard_map/add | solution.py:16
  679.3 1.0 pad_maximum_fusion
  680.2 3.5 pad_maximum_fusion.18
  683.7 2.5 pad_maximum_fusion.17
  686.2 1.9 reshape.71
  688.1 1.9 squeeze.128
  690.0 1.9 squeeze.111
  691.9 1.9 squeeze.110
  693.8 1.9 squeeze.126
  695.6 1.9 squeeze.118
  697.5 1.9 squeeze.122
  699.4 1.9 squeeze.117
  701.3 1.9 squeeze.124
  703.2 1.9 squeeze.116
  705.1 1.9 squeeze.121
  707.0 0.9 squeeze.115
  708.5 0.2 squeeze.113
  708.7 0.2 squeeze.123
  709.5 2.7 add_add_fusion
  (16 shorter events, 1.9 us)
Async XLA Ops:
  7.2 64.3 %all-gather.2.cloned.1.call-start = ((), (), s32[]{:S(2)}) async-start(), calls=%async_computation.1 | async-start | bytes 10616832 | tf_op jit(solution)/shard_map/all_gather | solution.py:31
  7.9 647.5 %reduce-scatter.2.cloned.1.call-start = ((), (), s32[]{:S(2)}) async-start(), calls=%async_computation.2 | async-start | bytes 39813120 | tf_op jit(solution)/shard_map/reduce_scatter | solution.py:47
  670.6 8.6 %copy-start = (f32[24,36,16,144]{3,2,1,0:T(8,128)S(1)}, f32[24,36,16,144]{3,2,1,0:T(8,128)}, u32[]{:S(2)}) copy-start(f32[24,36,16,144]{3,2,1,0:T(8,128)} %reshape_reshape.3) | copy-start | bytes 23887876
Sparse Core Ops, SparseCore 0:
  9.9 61.5 all-gather.1
  129.1 526.1 reduce-scatter.1
where the time goes:
time: 720 us; the launch traced here: 719 us
  waiting for transfers between devices  570 us (79%)
  local copies, waits for them, and re-layouts  39.7 us (6%)
  blocking collectives  37.3 us (5%)
  matrix products  31.7 us (4%)
  other arithmetic  26.1 us (4%)
  between operations  14.1 us (2%)
    reduce_scatter x1, waiting for transfers between devices, per_device(): reduced = lax.psum_scatter(sums, 'img', scatter_dimension=1, tiled=True)  514 us
    all_gather x1, waiting for transfers between devices, per_device(): gathered = lax.all_gather(images, 'ref', axis=0, tiled=True)  55.7 us
    squeeze x19, local copies, waits for them, and re-layouts, unturn(): result = result + doubled[:, turn_index, :, start_col:start_col + ANG]  21.4 us
    dot_general x1, matrix products, per_device(): lax.dot_general(weights, gathered, (((0,), (0,)), ((), ())), preferred_el...  17.6 us
    another operation x1, local copies, waits for them, and re-layouts, unturn(): cycles = stacked.reshape(classes_here, rotations, columns // ANG, ANG)  15.2 us
  transfers between devices with their start and end apart: 2, of which 2 were waited for; matrix products, arithmetic and copies ran while one was open for 1% of the time, Pallas kernels for 0%

commit v1 on v0

v1 whole, which is shorter than its diff:
```python
import functools

import jax
import jax.numpy as jnp
from jax import lax
from jax.experimental import pallas as pl
from jax.experimental.pallas import tpu as pltpu
from jax.sharding import PartitionSpec as P

ANG = 144
LANES = 128


def pixel_dims(pixels, rotations):
    shift = ANG // rotations
    cycles = pixels // ANG
    per_lane_block = LANES // shift
    halves = cycles // per_lane_block
    return shift, per_lane_block, halves


def to_turn_layout(x, rotations):
    rows, pixels = x.shape
    shift, per_lane_block, halves = pixel_dims(pixels, rotations)
    x = x.reshape(rows, halves, per_lane_block, rotations, shift)
    return x.transpose(0, 1, 3, 2, 4).reshape(rows, pixels)


def from_turn_layout(x, rotations):
    rows, pixels = x.shape
    shift, per_lane_block, halves = pixel_dims(pixels, rotations)
    x = x.reshape(rows, halves, rotations, per_lane_block, shift)
    return x.transpose(0, 1, 3, 2, 4).reshape(rows, pixels)


def turn_sum_kernel(classes_here, rotations, by_turn_ref, images_ref, out_ref, products_ref):
    products_ref[...] = jnp.dot(
        by_turn_ref[...], images_ref[...], preferred_element_type=jnp.float32
    )
    for b in range(rotations):
        total = None
        for turn_index in range(rotations):
            col = ((b + turn_index) % rotations) * LANES
            part = products_ref[
                turn_index * classes_here : (turn_index + 1) * classes_here, col : col + LANES
            ]
            total = part if total is None else total + part
        out_ref[:, b * LANES : (b + 1) * LANES] = total


def turn_and_sum(by_turn, gathered, classes_here, rotations, halves):
    local_refs, n = by_turn.shape
    pixels = gathered.shape[1]
    slab = pixels // halves
    return pl.pallas_call(
        functools.partial(turn_sum_kernel, classes_here, rotations),
        grid=(halves,),
        in_specs=[
            pl.BlockSpec((local_refs, n), lambda h: (0, 0)),
            pl.BlockSpec((n, slab), lambda h: (0, h)),
        ],
        out_specs=pl.BlockSpec((classes_here, slab), lambda h: (0, h)),
        out_shape=jax.ShapeDtypeStruct((classes_here, pixels), jnp.float32),
        scratch_shapes=[pltpu.VMEM((local_refs, slab), jnp.float32)],
        compiler_params=pltpu.CompilerParams(vmem_limit_bytes=60 * 1024 * 1024),
        cost_estimate=pl.CostEstimate(
            flops=2 * local_refs * n * pixels,
            bytes_accessed=2 * local_refs * n + 2 * n * pixels + 4 * classes_here * pixels,
            transcendentals=0,
        ),
    )(by_turn, gathered)


def per_device(images, references, class_prior):
    local_refs, pixels = references.shape
    classes_here = class_prior.shape[0]
    rotations = local_refs // classes_here
    shift, per_lane_block, halves = pixel_dims(pixels, rotations)

    half_norm = 0.5 * jnp.einsum(
        "jp,jp->j", references, references, preferred_element_type=jnp.float32
    )
    offsets = (jnp.log(class_prior)[:, None] - half_norm.reshape(classes_here, rotations)).reshape(
        local_refs
    )
    turned_images = to_turn_layout(images, rotations)
    gathered = lax.all_gather(turned_images, "ref", axis=0, tiled=True)
    turned_refs = to_turn_layout(references, rotations)
    products = lax.dot_general(
        gathered, turned_refs, (((1,), (1,)), ((), ())), preferred_element_type=jnp.float32
    )
    scores = products + offsets
    local_max = jnp.max(scores, axis=1)
    local_sum = jnp.sum(jnp.exp(scores - local_max[:, None]), axis=1)
    stats = lax.all_gather(jnp.stack([local_max, local_sum]), "ref", axis=0)
    top_score = jnp.max(stats[:, 0], axis=0)
    denominator = jnp.sum(stats[:, 1] * jnp.exp(stats[:, 0] - top_score[None, :]), axis=0)
    weights = (jnp.exp(scores - top_score[:, None]) / denominator[:, None]).astype(jnp.bfloat16)
    local_mass = (
        jnp.sum(weights.astype(jnp.float32), axis=0).reshape(classes_here, rotations).sum(axis=1)
    )
    class_weights = lax.psum(local_mass, "img")

    n = weights.shape[0]
    by_turn = weights.reshape(n, classes_here, rotations).transpose(2, 1, 0).reshape(local_refs, n)
    turned_sums = turn_and_sum(by_turn, gathered, classes_here, rotations, halves)
    local_sums = from_turn_layout(turned_sums, rotations)
    class_sums = lax.psum_scatter(local_sums, "img", scatter_dimension=1, tiled=True)
    return (class_sums, class_weights)


def solution(mesh):
    placed = (P(("img", "ref"), None), P("ref", None), P("ref"))
    return jax.shard_map(
        per_device,
        mesh=mesh,
        in_specs=placed,
        out_specs=(P("ref", "img"), P("ref")),
        check_vma=False,
    )
```

time: 720 us -> 255 us (0.35)
  waiting for transfers between devices: 570 us -> 73 us
  local copies, waits for them, and re-layouts: 39.7 us -> 108 us
  other arithmetic: 26.1 us -> 7.91 us
  matrix products: 31.7 us -> 13.7 us
  blocking collectives: 37.3 us -> 23.5 us
  Pallas kernels: 0 us -> 12.4 us
    reduce_scatter x1, waiting for transfers between devices: 514 us -> 72.9 us  [per_device(): lax.psum_scatter(local_sums, 'img', scatter_dimension=1, tiled=True)]
    reshape x0 -> x4, local copies, waits for them, and re-layouts: none -> 56.7 us  [the longest x2 28.7 us: to_turn_layout(): return x.transpose(0, 1, 3, 2, 4).reshape(rows, pixels)]
    all_gather x1, waiting for transfers between devices: 55.7 us -> 0.02 us  [per_device(): gathered = lax.all_gather(turned_images, 'ref', axis=0, tiled=True)]
    unnamed x2 -> x5, local copies, waits for them, and re-layouts: 0.17 us -> 26.2 us
    transpose x0 -> x4, local copies, waits for them, and re-layouts: none -> 21.5 us  [the longest x2 15 us: to_turn_layout(): return x.transpose(0, 1, 3, 2, 4).reshape(rows, pixels)]
    squeeze x19 -> x0, local copies, waits for them, and re-layouts: 21.4 us -> none  [unturn(): result = result + doubled[:, turn_index, :, start_col:start_col + ANG]]
    dot_general x2 -> x1, matrix products: 31.7 us -> 13.7 us  [per_device(): lax.dot_general(gathered, turned_refs, (((1,), (1,)), ((), ())), preferre...]
    another operation x1 -> x0, local copies, waits for them, and re-layouts: 15.2 us -> none  [unturn(): cycles = stacked.reshape(classes_here, rotations, columns // ANG, ANG)]
  transfers between devices with their start and end apart: 2 -> 2, of which waited for: 2 -> 1; matrix products, arithmetic and copies ran while one was open for 1% -> 37% of each run, Pallas kernels for 0% -> 0%
where the time goes in v1:
time: 255 us; the launch traced here: 253 us
  local copies, waits for them, and re-layouts  108 us (42%)
  waiting for transfers between devices  73 us (29%)
  blocking collectives  23.5 us (9%)
  between operations  14.1 us (6%)
  matrix products  13.7 us (5%)
  Pallas kernels  12.4 us (5%)
  other arithmetic  7.91 us (3%)
    reduce_scatter x1, waiting for transfers between devices, per_device(): lax.psum_scatter(local_sums, 'img', scatter_dimension=1, tiled=True)  72.9 us
    reshape x2, local copies, waits for them, and re-layouts, to_turn_layout(): return x.transpose(0, 1, 3, 2, 4).reshape(rows, pixels)  28.7 us
    reshape x1, local copies, waits for them, and re-layouts, to_turn_layout(): x = x.reshape(rows, halves, per_lane_block, rotations, shift)  27.8 us
    unnamed x5, local copies, waits for them, and re-layouts  26.2 us
    transpose x2, local copies, waits for them, and re-layouts, to_turn_layout(): return x.transpose(0, 1, 3, 2, 4).reshape(rows, pixels)  15 us
    dot_general x1, matrix products, per_device(): lax.dot_general(gathered, turned_refs, (((1,), (1,)), ((), ())), preferre...  13.7 us
    psum x1, blocking collectives, per_device(): class_weights = lax.psum(local_mass, 'img')  12.6 us
    pallas_call x1, Pallas kernels, turn_and_sum(): pl.pallas_call(functools.partial(turn_sum_kernel, classes_here, rotations...  12.4 us
  transfers between devices with their start and end apart: 2, of which 1 were waited for; matrix products, arithmetic and copies ran while one was open for 37% of the time, Pallas kernels for 0%

profile of v1, /device:TPU:0, one launch (start us, length us, event | category | flops | bytes accessed | tf_op | source)
XLA Modules:
  0.0 253.2 jit_solution(16367151426134609091)
XLA Ops:
  7.2 0.0 all-gather.4.cloned.1.call-start
  7.2 3.7 %copy.29 = bf16[64,9216]{0,1:T(8,128)(2,1)} copy(bf16[64,9216]{1,0:T(8,128)(2,1)} %param.3) | data formatting | bytes 2359296 | tf_op args[0]
  10.9 3.0 %copy.30 = bf16[64,2,36,32,4]{0,4,3,2,1:T(4,128)(2,1)S(1)} copy(bf16[64,2,36,32,4]{0,4,2,3,1:T(4,128)(2,1)} %bitcast.39) | data formatting | bytes 2359296 | tf_op jit(solution)/shard_map/transpose | solution.py:26
  13.9 2.2 copy.31
  16.1 0.0 all-gather.4.cloned.1.call-update
  16.1 0.0 reduce-scatter.2.cloned.1.call-start
  16.2 20.2 %copy.32 = bf16[864,9216]{0,1:T(8,128)(2,1)} copy(bf16[864,9216]{1,0:T(8,128)(2,1)} %param.4) | data formatting | bytes 31850496 | tf_op args[1]
  36.4 27.8 %reshape.46 = bf16[864,2,32,36,4]{0,4,3,2,1:T(4,128)(2,1)} reshape(bf16[864,9216]{0,1:T(8,128)(2,1)} %copy.32) | data formatting | bytes 31850496 | tf_op jit(solution)/shard_map/reshape | solution.py:25
  64.1 12.0 %copy.33 = bf16[864,2,36,32,4]{0,4,3,2,1:T(4,128)(2,1)} copy(bf16[864,2,36,32,4]{0,4,2,3,1:T(4,128)(2,1)} %bitcast.35) | data formatting | bytes 31850496 | tf_op jit(solution)/shard_map/transpose | solution.py:26
  76.2 0.0 copy-start
  76.2 26.5 %reshape.47 = bf16[864,9216]{0,1:T(8,128)(2,1)} reshape(bf16[864,2,36,32,4]{0,4,3,2,1:T(4,128)(2,1)} %copy.33) | data formatting | bytes 31850496 | tf_op jit(solution)/shard_map/reshape | solution.py:26
  102.7 0.0 copy-done
  102.7 0.1 sub.36
  102.8 0.1 sub.37
  102.9 7.0 %fusion = f32[864]{0:T(1024)S(1)} fusion(bf16[864,9216]{1,0:T(8,128)(2,1)} %param.4), kind=kLoop, calls=%fused_computation.1 | loop fusion | flops 23887008 | bytes 15928704 | tf_op jit(solution)/shard_map/jp,jp->j/dot_general | solution.py:80
  109.9 0.0 all-gather.4.cloned.1.call-done.images_ref
  109.9 13.7 %fusion.4 = (f32[512]{0:T(512)S(1)}, f32[512,864]{0,1:T(8,128)S(1)}) fusion(f32[864]{0:T(1024)S(1)} %multiply_subtract_fusion, bf16[512,9216]{1,0:T(8,128)(2,1)} %all-gather.4.cloned.1.call-done.images_ref, bf16[864,9216]{0,1:T(8,128)(2,1)} %reshape.47), kind=kOutput, calls=%fused_computation.14 | convolution fusion | flops 8154611200 | bytes 27137408 | tf_op jit(solution)/shard_map/dot_general | solution.py:89
  123.7 0.3 exponential_reduce_fusion
  124.0 11.0 %all-gather.1 = f32[8,2,512]{2,1,0:T(2,128)S(1)} all-gather(f32[1,2,512]{2,1,0:T(2,128)S(1)} %maximum_bitcast_fusion), channel_id=2, replica_groups=mesh['img'=4,'ref'=8] {'ref'}, dimensions={0}, use_global_device_ids=true | all-gather | bytes 36864 | tf_op jit(solution)/shard_map/all_gather | solution.py:95
  135.0 0.4 convert_reduce_fusion
  135.4 0.2 reshape.48
  135.6 1.2 copy.35
  136.8 12.4 %shard_map.50 = f32[24,9216]{1,0:T(8,128)} custom-call(bf16[864,512]{1,0:T(8,128)(2,1)} %bitcast.41, bf16[512,9216]{1,0:T(8,128)(2,1)} %all-gather.4.cloned.1.call-done.images_ref), custom_call_target="tpu_custom_call" | custom-call | flops 8153726976 | bytes 11206656 | tf_op jit(solution)/shard_map/pallas_call | solution.py:55
  149.2 3.8 %copy.36 = f32[24,9216]{0,1:T(8,128)} copy(f32[24,9216]{1,0:T(8,128)} %shard_map.50) | data formatting | bytes 1769472 | tf_op jit(solution)/shard_map/pallas_call | solution.py:55
  153.0 5.3 %copy.37 = f32[24,2,32,36,4]{0,4,3,2,1:T(4,128)} copy(f32[24,2,32,36,4]{0,4,2,3,1:T(4,128)} %bitcast.37) | data formatting | bytes 1769472 | tf_op jit(solution)/shard_map/transpose | solution.py:33
  158.3 0.0 reduce-scatter.2.cloned.1.call-update
  158.3 0.1 reshape.52
  158.4 0.1 reduce_sum.39
  158.5 12.6 %psum.7 = f32[24]{0:T(128)} all-reduce(f32[24]{0:T(128)S(1)} %reduce_sum.39), channel_id=1, replica_groups=mesh['img'=4,'ref'=8] {'img'}, use_global_device_ids=true, to_apply=%region_7.0 | all-reduce | flops 24 | bytes 192 | tf_op jit(solution)/shard_map/psum | solution.py:102
  171.1 72.9 %reduce-scatter.2.cloned.1.call-done = f32[24,2304]{0,1:T(8,128)} async-done(((f32[24,9216]{0,1:T(8,128)}), f32[24,2304]{0,1:T(8,128)}) %reduce-scatter.2.cloned.1.call-update) | async-done | bytes 221200 | tf_op jit(solution)/shard_map/reduce_scatter | solution.py:108
  244.0 2.3 copy.38
  (5 shorter events, 0.1 us)
Async XLA Ops:
  7.2 102.8 %all-gather.4.cloned.1.call-start = ((), (), s32[]{:S(2)}) async-start(), calls=%async_computation.1 | async-start | bytes 10616832 | tf_op jit(solution)/shard_map/all_gather | solution.py:87
  16.1 227.9 %reduce-scatter.2.cloned.1.call-start = ((), (), s32[]{:S(2)}) async-start(), calls=%async_computation.2 | async-start | bytes 5898240 | tf_op jit(solution)/shard_map/reduce_scatter | solution.py:108
  76.2 26.5 %copy-start = (f32[24]{0:T(128)S(1)}, f32[24]{0:T(128)}, u32[]{:S(2)}) copy-start(f32[24]{0:T(128)} %param.5) | copy-start | bytes 292
Sparse Core Ops, SparseCore 0:
  16.2 61.5 all-gather.3
  158.4 85.5 reduce-scatter.1

commit v2 on v0

v2 whole, which is shorter than its diff:
```python
import functools

import jax
import jax.numpy as jnp
from jax import lax
from jax.experimental import pallas as pl
from jax.experimental.pallas import tpu as pltpu
from jax.sharding import PartitionSpec as P

ANG = 144
LANES = 128
GROUP_COLS = 1152


def turn_sum_kernel(classes_here, rotations, by_turn_ref, images_ref, angle_ref, out_ref, products_ref):
    shift = ANG // rotations
    width = images_ref.shape[1]
    products_ref[...] = jnp.dot(
        by_turn_ref[...], images_ref[...], preferred_element_type=jnp.float32
    )
    rows = 8 if classes_here % 8 == 0 else classes_here
    cols = GROUP_COLS if width % GROUP_COLS == 0 else width
    for row0 in range(0, classes_here, rows):
        for col0 in range(0, width, cols):
            angle = angle_ref[:, col0 : col0 + cols]
            total = products_ref[row0 : row0 + rows, col0 : col0 + cols]
            for turn_index in range(1, rotations):
                start = turn_index * classes_here + row0
                part = products_ref[start : start + rows, col0 : col0 + cols]
                step = turn_index * shift
                ahead = pltpu.roll(part, cols - step, 1)
                behind = pltpu.roll(part, ANG - step, 1)
                total = total + jnp.where(angle < ANG - step, ahead, behind)
            out_ref[0, row0 : row0 + rows, col0 : col0 + cols] = total
    mass = jnp.sum(by_turn_ref[...].astype(jnp.float32), axis=1, keepdims=True)
    class_mass = mass[0:classes_here]
    for turn_index in range(1, rotations):
        class_mass = class_mass + mass[turn_index * classes_here : (turn_index + 1) * classes_here]
    out_ref[0, :, width:] = jnp.broadcast_to(class_mass, (classes_here, LANES))


def turn_and_sum(by_turn, gathered, classes_here, rotations, chunks):
    local_refs, n = by_turn.shape
    pixels = gathered.shape[1]
    width = pixels // chunks
    angle = (jnp.arange(width, dtype=jnp.int32) % ANG).reshape(1, width)
    return pl.pallas_call(
        functools.partial(turn_sum_kernel, classes_here, rotations),
        grid=(chunks,),
        in_specs=[
            pl.BlockSpec((local_refs, n), lambda t: (0, 0)),
            pl.BlockSpec((n, width), lambda t: (0, t)),
            pl.BlockSpec((1, width), lambda t: (0, 0)),
        ],
        out_specs=pl.BlockSpec((1, classes_here, width + LANES), lambda t: (t, 0, 0)),
        out_shape=jax.ShapeDtypeStruct((chunks, classes_here, width + LANES), jnp.float32),
        scratch_shapes=[pltpu.VMEM((local_refs, width), jnp.float32)],
        compiler_params=pltpu.CompilerParams(vmem_limit_bytes=60 * 1024 * 1024),
        cost_estimate=pl.CostEstimate(
            flops=2 * local_refs * n * pixels,
            bytes_accessed=2 * local_refs * n + 2 * n * pixels + 4 * classes_here * pixels,
            transcendentals=0,
        ),
    )(by_turn, gathered, angle)


def per_device(chunks, images, references, class_prior):
    local_refs, pixels = references.shape
    classes_here = class_prior.shape[0]
    rotations = local_refs // classes_here

    half_norm = 0.5 * jnp.einsum(
        "jp,jp->j", references, references, preferred_element_type=jnp.float32
    )
    offsets = (jnp.log(class_prior)[:, None] - half_norm.reshape(classes_here, rotations)).reshape(
        local_refs
    )
    gathered = lax.all_gather(images, "ref", axis=0, tiled=True)
    products = lax.dot_general(
        gathered, references, (((1,), (1,)), ((), ())), preferred_element_type=jnp.float32
    )
    scores = products + offsets
    local_max = jnp.max(scores, axis=1)
    local_sum = jnp.sum(jnp.exp(scores - local_max[:, None]), axis=1)
    stats = lax.all_gather(jnp.stack([local_max, local_sum]), "ref", axis=0)
    top_score = jnp.max(stats[:, 0], axis=0)
    denominator = jnp.sum(stats[:, 1] * jnp.exp(stats[:, 0] - top_score[None, :]), axis=0)
    weights = (jnp.exp(scores - top_score[:, None]) / denominator[:, None]).astype(jnp.bfloat16)

    n = weights.shape[0]
    by_turn = weights.reshape(n, classes_here, rotations).transpose(2, 1, 0).reshape(local_refs, n)
    chunked = turn_and_sum(by_turn, gathered, classes_here, rotations, chunks)
    reduced = lax.psum_scatter(chunked, "img", scatter_dimension=0, tiled=True)[0]
    width = pixels // chunks
    return (reduced[:, :width], reduced[:, width])


def solution(mesh):
    placed = (P(("img", "ref"), None), P("ref", None), P("ref"))
    return jax.shard_map(
        functools.partial(per_device, mesh.shape["img"]),
        mesh=mesh,
        in_specs=placed,
        out_specs=(P("ref", "img"), P("ref")),
        check_vma=False,
    )
```

time: 720 us -> 155 us (0.22)
  waiting for transfers between devices: 570 us -> 81.4 us
  local copies, waits for them, and re-layouts: 39.7 us -> 5.14 us
  blocking collectives: 37.3 us -> 9.02 us
  Pallas kernels: 0 us -> 22.5 us
  other arithmetic: 26.1 us -> 8.32 us
  matrix products: 31.7 us -> 14.1 us
    reduce_scatter x1 -> x0, waiting for transfers between devices: 514 us -> none  [per_device(): reduced = lax.psum_scatter(sums, 'img', scatter_dimension=1, tiled=True)]
    unnamed x2 -> x3, waiting for transfers between devices: 0.7 us -> 26.4 us
    psum x2 -> x0, blocking collectives: 24.2 us -> none  [the longest x1 12.4 us: per_device(): class_weights = lax.psum(local_mass, 'img')]
    pallas_call x0 -> x1, Pallas kernels: none -> 22.5 us  [turn_and_sum(): pl.pallas_call(functools.partial(turn_sum_kernel, classes_here, rotations...]
    squeeze x19 -> x0, local copies, waits for them, and re-layouts: 21.4 us -> none  [unturn(): result = result + doubled[:, turn_index, :, start_col:start_col + ANG]]
    dot_general x1 -> x0, matrix products: 17.6 us -> none  [per_device(): lax.dot_general(weights, gathered, (((0,), (0,)), ((), ())), preferred_el...]
    another operation x1 -> x0, local copies, waits for them, and re-layouts: 15.2 us -> none  [unturn(): cycles = stacked.reshape(classes_here, rotations, columns // ANG, ANG)]
    pmax x1 -> x0, blocking collectives: 13.1 us -> none  [per_device(): top_score = lax.pmax(local_max, 'ref')]
  transfers between devices with their start and end apart: 2 -> 2, of which waited for: 2 -> 2; matrix products, arithmetic and copies ran while one was open for 1% -> 5% of each run, Pallas kernels for 0% -> 0%
where the time goes in v2:
time: 155 us
  waiting for transfers between devices  81.4 us (53%)
  Pallas kernels  22.5 us (15%)
  matrix products  14.1 us (9%)
  between operations  14.1 us (9%)
  blocking collectives  9.02 us (6%)
  other arithmetic  8.32 us (5%)
  local copies, waits for them, and re-layouts  5.14 us (3%)
    all_gather x1, waiting for transfers between devices, per_device(): gathered = lax.all_gather(images, 'ref', axis=0, tiled=True)  55 us
    unnamed x3, waiting for transfers between devices  26.4 us
    pallas_call x1, Pallas kernels, turn_and_sum(): pl.pallas_call(functools.partial(turn_sum_kernel, classes_here, rotations...  22.5 us
    dot_general x1, matrix products, per_device(): lax.dot_general(gathered, references, (((1,), (1,)), ((), ())), preferred...  14.1 us
    all_gather x1, blocking collectives, per_device(): stats = lax.all_gather(jnp.stack([local_max, local_sum]), 'ref', axis=0)  9.02 us
    dot_general x1, other arithmetic, per_device(): jnp.einsum('jp,jp->j', references, references, preferred_element_type=jnp...  7 us
  transfers between devices with their start and end apart: 2, of which 2 were waited for; matrix products, arithmetic and copies ran while one was open for 5% of the time, Pallas kernels for 0%

profile of v2, /device:TPU:0, one launch (start us, length us, event | category | flops | bytes accessed | tf_op | source)
XLA Modules:
  0.0 154.7 jit_solution(406221096289238818)
XLA Ops:
  7.2 0.0 all-gather.4.cloned.1.call-start
  7.2 0.7 all-gather.4.cloned.1.call-update
  7.9 0.0 reduce-scatter.4.cloned.1.call-start
  7.9 0.7 log.3
  8.6 0.1 sub.36
  8.7 0.1 sub.37
  8.8 7.0 %fusion = f32[864]{0:T(1024)S(1)} fusion(bf16[864,9216]{1,0:T(8,128)(2,1)} %param.4), kind=kLoop, calls=%fused_computation.1 | loop fusion | flops 23887008 | bytes 15928704 | tf_op jit(solution)/shard_map/jp,jp->j/dot_general | solution.py:72
  15.8 0.6 and_select_fusion.angle_ref
  16.4 55.0 %all-gather.4.cloned.1.call-done.images_ref = bf16[512,9216]{1,0:T(8,128)(2,1)} async-done(((bf16[64,9216]{1,0:T(8,128)(2,1)}), bf16[512,9216]{1,0:T(8,128)(2,1)}) %all-gather.4.cloned.1.call-update) | async-done | bytes 9437200 | tf_op jit(solution)/shard_map/all_gather | solution.py:78
  71.4 14.1 %fusion.4 = (f32[512]{0:T(512)S(1)}, f32[512,864]{0,1:T(8,128)S(1)}) fusion(f32[864]{0:T(1024)S(1)} %multiply_subtract_fusion, bf16[512,9216]{1,0:T(8,128)(2,1)} %all-gather.4.cloned.1.call-done.images_ref, bf16[864,9216]{1,0:T(8,128)(2,1)} %param.4), kind=kOutput, calls=%fused_computation.15 | convolution fusion | flops 8154611200 | bytes 27137408 | tf_op jit(solution)/shard_map/dot_general | solution.py:79
  85.6 0.3 exponential_reduce_fusion
  85.9 9.0 %all-gather.1 = f32[8,2,512]{2,1,0:T(2,128)S(1)} all-gather(f32[1,2,512]{2,1,0:T(2,128)S(1)} %maximum_bitcast_fusion), channel_id=2, replica_groups=mesh['img'=4,'ref'=8] {'ref'}, dimensions={0}, use_global_device_ids=true | all-gather | bytes 36864 | tf_op jit(solution)/shard_map/all_gather | solution.py:85
  95.0 0.3 divide_convert_fusion
  95.3 0.2 reshape.46
  95.5 1.2 copy.10
  96.7 22.5 %shard_map.50 = f32[4,24,2432]{2,1,0:T(8,128)} custom-call(bf16[864,512]{1,0:T(8,128)(2,1)} %bitcast.25, bf16[512,9216]{1,0:T(8,128)(2,1)} %all-gather.4.cloned.1.call-done.images_ref, s32[1,2304]{1,0:T(1,128)} %and_select_fusion.angle_ref), custom_call_target="tpu_custom_call" | custom-call | flops 8153726976 | bytes 11206656 | tf_op jit(solution)/shard_map/pallas_call | solution.py:47
  119.2 0.0 reduce-scatter.4.cloned.1.call-update
  119.2 25.7 %reduce-scatter.4.cloned.1.call-done = f32[1,24,2432]{2,1,0:T(8,128)} async-done(((f32[4,24,2432]{2,1,0:T(8,128)}), f32[1,24,2432]{2,1,0:T(8,128)}) %reduce-scatter.4.cloned.1.call-update) | async-done | bytes 233488
  144.9 1.6 %slice.19 = f32[24,2304]{1,0:T(8,128)} slice(f32[24,2432]{1,0:T(8,128)} %bitcast.26), slice={[0:24], [0:2304]} | slice | bytes 442368 | tf_op jit(solution)/shard_map/slice | solution.py:95
  146.6 1.3 slice_reduce_fusion
  (4 shorter events, 0.1 us)
Async XLA Ops:
  7.2 64.3 %all-gather.4.cloned.1.call-start = ((), (), s32[]{:S(2)}) async-start(), calls=%async_computation.1 | async-start | bytes 10616832 | tf_op jit(solution)/shard_map/all_gather | solution.py:78
  7.9 137.0 %reduce-scatter.4.cloned.1.call-start = ((), (), s32[]{:S(2)}) async-start(), calls=%async_computation.2 | async-start | bytes 1167360
Sparse Core Ops, SparseCore 0:
  9.9 61.5 all-gather.3
  119.3 25.5 reduce-scatter.3

commit v3 on v2

--- a/solution.py
+++ b/solution.py
@@ -39,35 +39,43 @@
     out_ref[0, :, width:] = jnp.broadcast_to(class_mass, (classes_here, LANES))
 
 
-def turn_and_sum(by_turn, gathered, classes_here, rotations, chunks):
+def turn_and_sum(by_turn, gathered, angle, classes_here, rotations):
     local_refs, n = by_turn.shape
-    pixels = gathered.shape[1]
-    width = pixels // chunks
-    angle = (jnp.arange(width, dtype=jnp.int32) % ANG).reshape(1, width)
+    width = gathered.shape[1]
     return pl.pallas_call(
         functools.partial(turn_sum_kernel, classes_here, rotations),
-        grid=(chunks,),
+        grid=(1,),
         in_specs=[
             pl.BlockSpec((local_refs, n), lambda t: (0, 0)),
-            pl.BlockSpec((n, width), lambda t: (0, t)),
+            pl.BlockSpec((n, width), lambda t: (0, 0)),
             pl.BlockSpec((1, width), lambda t: (0, 0)),
         ],
-        out_specs=pl.BlockSpec((1, classes_here, width + LANES), lambda t: (t, 0, 0)),
-        out_shape=jax.ShapeDtypeStruct((chunks, classes_here, width + LANES), jnp.float32),
+        out_specs=pl.BlockSpec((1, classes_here, width + LANES), lambda t: (0, 0, 0)),
+        out_shape=jax.ShapeDtypeStruct((1, classes_here, width + LANES), jnp.float32),
         scratch_shapes=[pltpu.VMEM((local_refs, width), jnp.float32)],
         compiler_params=pltpu.CompilerParams(vmem_limit_bytes=60 * 1024 * 1024),
         cost_estimate=pl.CostEstimate(
-            flops=2 * local_refs * n * pixels,
-            bytes_accessed=2 * local_refs * n + 2 * n * pixels + 4 * classes_here * pixels,
+            flops=2 * local_refs * n * width,
+            bytes_accessed=2 * local_refs * n + 2 * n * width + 4 * classes_here * width,
             transcendentals=0,
         ),
     )(by_turn, gathered, angle)
 
 
-def per_device(chunks, images, references, class_prior):
+def gather_from_all(value, axis_name, size):
+    me = lax.axis_index(axis_name)
+    parts = [value]
+    for step in range(1, size):
+        perm = [(src, (src + step) % size) for src in range(size)]
+        parts.append(lax.ppermute(value, axis_name, perm))
+    return parts
+
+
+def per_device(n_img, n_ref, images, references, class_prior):
     local_refs, pixels = references.shape
     classes_here = class_prior.shape[0]
     rotations = local_refs // classes_here
+    width = pixels // n_img
 
     half_norm = 0.5 * jnp.einsum(
         "jp,jp->j", references, references, preferred_element_type=jnp.float32
@@ -75,30 +83,48 @@
     offsets = (jnp.log(class_prior)[:, None] - half_norm.reshape(classes_here, rotations)).reshape(
         local_refs
     )
-    gathered = lax.all_gather(images, "ref", axis=0, tiled=True)
-    products = lax.dot_general(
-        gathered, references, (((1,), (1,)), ((), ())), preferred_element_type=jnp.float32
-    )
+    pieces = []
+    products = None
+    for chunk in range(n_img):
+        cols = slice(chunk * width, (chunk + 1) * width)
+        piece = lax.all_gather(images[:, cols], "ref", axis=0, tiled=True)
+        pieces.append(piece)
+        part = lax.dot_general(
+            piece, references[:, cols], (((1,), (1,)), ((), ())), preferred_element_type=jnp.float32
+        )
+        products = part if products is None else products + part
     scores = products + offsets
     local_max = jnp.max(scores, axis=1)
     local_sum = jnp.sum(jnp.exp(scores - local_max[:, None]), axis=1)
-    stats = lax.all_gather(jnp.stack([local_max, local_sum]), "ref", axis=0)
-    top_score = jnp.max(stats[:, 0], axis=0)
-    denominator = jnp.sum(stats[:, 1] * jnp.exp(stats[:, 0] - top_score[None, :]), axis=0)
+    stats = gather_from_all(jnp.stack([local_max, local_sum]), "ref", n_ref)
+    top_score = stats[0][0]
+    for other in stats[1:]:
+        top_score = jnp.maximum(top_score, other[0])
+    denominator = None
+    for other in stats:
+        term = other[1] * jnp.exp(other[0] - top_score)
+        denominator = term if denominator is None else denominator + term
     weights = (jnp.exp(scores - top_score[:, None]) / denominator[:, None]).astype(jnp.bfloat16)
 
     n = weights.shape[0]
     by_turn = weights.reshape(n, classes_here, rotations).transpose(2, 1, 0).reshape(local_refs, n)
-    chunked = turn_and_sum(by_turn, gathered, classes_here, rotations, chunks)
-    reduced = lax.psum_scatter(chunked, "img", scatter_dimension=0, tiled=True)[0]
-    width = pixels // chunks
+    angle = (jnp.arange(width, dtype=jnp.int32) % ANG).reshape(1, width)
+    chunked = jnp.concatenate(
+        [turn_and_sum(by_turn, piece, angle, classes_here, rotations) for piece in pieces], axis=0
+    )
+    me = lax.axis_index("img")
+    reduced = chunked[me]
+    for step in range(1, n_img):
+        perm = [(src, (src + step) % n_img) for src in range(n_img)]
+        outgoing = lax.dynamic_index_in_dim(chunked, (me + step) % n_img, 0, keepdims=False)
+        reduced = reduced + lax.ppermute(outgoing, "img", perm)
     return (reduced[:, :width], reduced[:, width])
 
 
 def solution(mesh):
     placed = (P(("img", "ref"), None), P("ref", None), P("ref"))
     return jax.shard_map(
-        functools.partial(per_device, mesh.shape["img"]),
+        functools.partial(per_device, mesh.shape["img"], mesh.shape["ref"]),
         mesh=mesh,
         in_specs=placed,
         out_specs=(P("ref", "img"), P("ref")),

time: 155 us -> 216 us (1.39)
  waiting for transfers between devices: 81.4 us -> 121 us
  starting transfers between devices: 0.08 us -> 12.1 us
  matrix products: 14.1 us -> 24.1 us
  blocking collectives: 9.02 us -> 0 us
  Pallas kernels: 22.5 us -> 30.4 us
    all_gather x1 -> x4, waiting for transfers between devices: 55 us -> 97.7 us  [per_device(): piece = lax.all_gather(images[:, cols], 'ref', axis=0, tiled=True)]
    unnamed x3 -> x4, waiting for transfers between devices: 26.4 us -> 1.92 us
    ppermute x0 -> x10, waiting for transfers between devices: none -> 21.2 us  [the longest x3 17.4 us: per_device(): reduced = reduced + lax.ppermute(outgoing, 'img', perm)]
    ppermute x0 -> x10, starting transfers between devices: none -> 12 us  [the longest x7 7.47 us: gather_from_all(): parts.append(lax.ppermute(value, axis_name, perm))]
    dot_general x1 -> x4, matrix products: 14.1 us -> 24.1 us  [per_device(): lax.dot_general(piece, references[:, cols], (((1,), (1,)), ((), ())), pre...]
    all_gather x1 -> x0, blocking collectives: 9.02 us -> none  [per_device(): stats = lax.all_gather(jnp.stack([local_max, local_sum]), 'ref', axis=0)]
    pallas_call x1 -> x4, Pallas kernels: 22.5 us -> 30.4 us  [turn_and_sum(): pl.pallas_call(functools.partial(turn_sum_kernel, classes_here, rotations...]
    slice x0 -> x8, local copies, waits for them, and re-layouts: none -> 2.32 us  [the longest x1 2.28 us: per_device(): piece = lax.all_gather(images[:, cols], 'ref', axis=0, tiled=True)]
  transfers between devices with their start and end apart: 2 -> 14, of which waited for: 2 -> 9; matrix products, arithmetic and copies ran while one was open for 5% -> 12% of each run, Pallas kernels for 0% -> 0%
where the time goes in v3:
time: 216 us
  waiting for transfers between devices  121 us (56%)
  Pallas kernels  30.4 us (14%)
  matrix products  24.1 us (11%)
  between operations  13.9 us (6%)
  starting transfers between devices  12.1 us (6%)
  other arithmetic  9.37 us (4%)
  local copies, waits for them, and re-layouts  5.24 us (2%)
    all_gather x4, waiting for transfers between devices, per_device(): piece = lax.all_gather(images[:, cols], 'ref', axis=0, tiled=True)  97.7 us
    pallas_call x4, Pallas kernels, turn_and_sum(): pl.pallas_call(functools.partial(turn_sum_kernel, classes_here, rotations...  30.4 us
    dot_general x4, matrix products, per_device(): lax.dot_general(piece, references[:, cols], (((1,), (1,)), ((), ())), pre...  24.1 us
    ppermute x3, waiting for transfers between devices, per_device(): reduced = reduced + lax.ppermute(outgoing, 'img', perm)  17.4 us
    ppermute x7, starting transfers between devices, gather_from_all(): parts.append(lax.ppermute(value, axis_name, perm))  7.47 us
    dot_general x1, other arithmetic, per_device(): jnp.einsum('jp,jp->j', references, references, preferred_element_type=jnp...  7 us
    ppermute x3, starting transfers between devices, per_device(): reduced = reduced + lax.ppermute(outgoing, 'img', perm)  4.48 us
  transfers between devices with their start and end apart: 14, of which 9 were waited for; matrix products, arithmetic and copies ran while one was open for 12% of the time, Pallas kernels for 0%

profile of v3, /device:TPU:0, one launch (start us, length us, event | category | flops | bytes accessed | tf_op | source)
XLA Modules:
  0.0 216.0 jit_solution(14503758916577907128)
XLA Ops:
  7.2 2.3 %fusion.13 = (bf16[64,2304]{1,0:T(8,128)(2,1)}, bf16[64,2304]{1,0:T(8,128)(2,1)}, bf16[64,2304]{1,0:T(8,128)(2,1)}, bf16[64,2304]{1,0:T(8,128)(2,1)}) fusion(bf16[64,9216]{1,0:T(8,128)(2,1)} %param.3), kind=kLoop, calls=%fused_computation.26 | loop fusion | bytes 2359296 | tf_op jit(solution)/shard_map/slice | solution.py:90
  9.6 0.7 all-gather.11.cloned.1.call-update
  10.3 0.7 all-gather.7.cloned.1.call-update
  11.8 7.0 %fusion = f32[864]{0:T(1024)S(1)} fusion(bf16[864,9216]{1,0:T(8,128)(2,1)} %param.4), kind=kLoop, calls=%fused_computation.1 | loop fusion | flops 23887008 | bytes 15928704 | tf_op jit(solution)/shard_map/jp,jp->j/dot_general | solution.py:80
  18.8 22.9 %all-gather.9.cloned.1.call-done.images_ref = bf16[512,2304]{1,0:T(8,128)(2,1)} async-done(((bf16[64,2304]{1,0:T(8,128)(2,1)}), bf16[512,2304]{1,0:T(8,128)(2,1)}) %all-gather.9.cloned.1.call-update) | async-done | bytes 2359312 | tf_op jit(solution)/shard_map/all_gather | solution.py:90
  41.6 5.1 %fusion.3 = f32[512,864]{0,1:T(8,128)S(1)} fusion(bf16[512,2304]{1,0:T(8,128)(2,1)} %all-gather.9.cloned.1.call-done.images_ref, bf16[864,9216]{1,0:T(8,128)(2,1)} %param.4), kind=kOutput, calls=%fused_computation.4 | convolution fusion | flops 2038431744 | bytes 8110080 | tf_op jit(solution)/shard_map/dot_general | solution.py:92
  46.7 25.8 %all-gather.11.cloned.1.call-done.images_ref = bf16[512,2304]{1,0:T(8,128)(2,1)} async-done(((bf16[64,2304]{1,0:T(8,128)(2,1)}), bf16[512,2304]{1,0:T(8,128)(2,1)}) %all-gather.11.cloned.1.call-update) | async-done | bytes 2359312 | tf_op jit(solution)/shard_map/all_gather | solution.py:90
  72.6 6.3 %fusion.1 = f32[512,864]{0,1:T(8,128)} fusion(bf16[512,2304]{1,0:T(8,128)(2,1)} %all-gather.11.cloned.1.call-done.images_ref, bf16[864,9216]{1,0:T(8,128)(2,1)} %param.4), kind=kOutput, calls=%fused_computation.2 | convolution fusion | flops 2038431744 | bytes 8110080 | tf_op jit(solution)/shard_map/dot_general | solution.py:92
  78.9 24.7 %all-gather.7.cloned.1.call-done.images_ref = bf16[512,2304]{1,0:T(8,128)(2,1)} async-done(((bf16[64,2304]{1,0:T(8,128)(2,1)}), bf16[512,2304]{1,0:T(8,128)(2,1)}) %all-gather.7.cloned.1.call-update) | async-done | bytes 2359312 | tf_op jit(solution)/shard_map/all_gather | solution.py:90
  103.5 6.4 %fusion.5 = f32[512,864]{0,1:T(8,128)} fusion(bf16[512,2304]{1,0:T(8,128)(2,1)} %all-gather.7.cloned.1.call-done.images_ref, bf16[864,9216]{1,0:T(8,128)(2,1)} %param.4), kind=kOutput, calls=%fused_computation.6 | convolution fusion | flops 2038431744 | bytes 8110080 | tf_op jit(solution)/shard_map/dot_general | solution.py:92
  109.9 24.4 %all-gather.5.cloned.1.call-done.images_ref = bf16[512,2304]{1,0:T(8,128)(2,1)} async-done(((bf16[64,2304]{1,0:T(8,128)(2,1)}), bf16[512,2304]{1,0:T(8,128)(2,1)}) %all-gather.5.cloned.1.call-update) | async-done | bytes 2359312 | tf_op jit(solution)/shard_map/all_gather | solution.py:90
  134.3 6.3 %fusion.21 = (f32[512]{0:T(512)S(1)}, f32[512,864]{0,1:T(8,128)S(1)}) fusion(f32[864]{0:T(1024)S(1)} %multiply_subtract_fusion, f32[512,864]{0,1:T(8,128)} %fusion.1, f32[512,864]{0,1:T(8,128)S(1)} %fusion.3, f32[512,864]{0,1:T(8,128)} %fusion.5, bf16[512,2304]{1,0:T(8,128)(2,1)} %all-gather.5.cloned.1.call-done.images_ref, bf16[864,9216]{1,0:T(8,128)(2,1)} %param.4), kind=kOutput, calls=%fused_computation.34 | convolution fusion | flops 2040643072 | bytes 13424000 | tf_op jit(solution)/shard_map/dot_general | solution.py:92
  141.0 1.4 collective-permute-start.6
  142.3 0.6 and_select_fusion.angle_ref
  143.0 1.4 collective-permute-start.5
  145.0 1.5 collective-permute-start.2
  146.5 2.4 %collective-permute-start.1 = (f32[2,512]{1,0:T(2,128)S(1)}, f32[2,512]{1,0:T(2,128)S(1)}, u32[]{:S(2)}, u32[]{:S(2)}) collective-permute-start(f32[2,512]{1,0:T(2,128)S(1)} %pad_maximum_fusion.1), channel_id=1, source_target_pairs={{0,2},{1,3},{2,4},{3,5},{4,6},{5,7},{6,0},{7,1},{8,10},{9,11},{10,... | collective-permute-start | bytes 12296 | tf_op jit(solution)/shard_map/ppermute | solution.py:70
  149.2 1.8 collective-permute-done.1
  151.0 2.0 collective-permute-done
  153.5 1.2 copy.6
  154.7 7.6 %shard_map.53 = f32[1,24,2432]{2,1,0:T(8,128)} custom-call(bf16[864,512]{1,0:T(8,128)(2,1)} %bitcast.37, bf16[512,2304]{1,0:T(8,128)(2,1)} %all-gather.11.cloned.1.call-done.images_ref, s32[1,2304]{1,0:T(1,128)} %and_select_fusion.angle_ref), custom_call_target="tpu_custom_call" | custom-call | flops 2038431744 | bytes 3465216 | tf_op jit(solution)/shard_map/pallas_call | solution.py:45
  162.2 7.5 %shard_map.52 = f32[1,24,2432]{2,1,0:T(8,128)} custom-call(bf16[864,512]{1,0:T(8,128)(2,1)} %bitcast.38, bf16[512,2304]{1,0:T(8,128)(2,1)} %all-gather.9.cloned.1.call-done.images_ref, s32[1,2304]{1,0:T(1,128)} %and_select_fusion.angle_ref), custom_call_target="tpu_custom_call" | custom-call | flops 2038431744 | bytes 3465216 | tf_op jit(solution)/shard_map/pallas_call | solution.py:45
  169.8 7.7 %shard_map.51 = f32[1,24,2432]{2,1,0:T(8,128)} custom-call(bf16[864,512]{1,0:T(8,128)(2,1)} %bitcast.39, bf16[512,2304]{1,0:T(8,128)(2,1)} %all-gather.7.cloned.1.call-done.images_ref, s32[1,2304]{1,0:T(1,128)} %and_select_fusion.angle_ref), custom_call_target="tpu_custom_call" | custom-call | flops 2038431744 | bytes 3465216 | tf_op jit(solution)/shard_map/pallas_call | solution.py:45
  177.5 7.6 %shard_map.50 = f32[1,24,2432]{2,1,0:T(8,128)} custom-call(bf16[864,512]{1,0:T(8,128)(2,1)} %bitcast.40, bf16[512,2304]{1,0:T(8,128)(2,1)} %all-gather.5.cloned.1.call-done.images_ref, s32[1,2304]{1,0:T(1,128)} %and_select_fusion.angle_ref), custom_call_target="tpu_custom_call" | custom-call | flops 2038431744 | bytes 3465216 | tf_op jit(solution)/shard_map/pallas_call | solution.py:45
  185.1 1.0 pad_maximum_fusion
  186.2 1.5 collective-permute-start.7
  187.8 2.3 %collective-permute-start.9 = (f32[24,2432]{1,0:T(8,128)S(1)}, f32[24,2432]{1,0:T(8,128)S(1)}, u32[]{:S(2)}, u32[]{:S(2)}) collective-permute-start(f32[24,2432]{1,0:T(8,128)S(1)} %get-tuple-element.7), channel_id=1, source_target_pairs={{0,24},{8,0},{16,8},{24,16},{1,25},{9,1},{17,9},{25,17},{2,26},{10... | collective-permute-start | bytes 700424 | tf_op jit(solution)/shard_map/ppermute | solution.py:120
  190.7 6.1 %collective-permute-done.7 = f32[24,2432]{1,0:T(8,128)S(1)} collective-permute-done((f32[24,2432]{1,0:T(8,128)S(1)}, f32[24,2432]{1,0:T(8,128)S(1)}, u32[]{:S(2)}, u32[]{:S(2)}) %collective-permute-start.7) | collective-permute-done | bytes 233504 | tf_op jit(solution)/shard_map/ppermute | solution.py:120
  196.8 1.0 collective-permute-done.9
  197.8 10.3 %collective-permute-done.8 = f32[24,2432]{1,0:T(8,128)S(1)} collective-permute-done((f32[24,2432]{1,0:T(8,128)S(1)}, f32[24,2432]{1,0:T(8,128)S(1)}, u32[]{:S(2)}, u32[]{:S(2)}) %collective-permute-start.8) | collective-permute-done | bytes 233504 | tf_op jit(solution)/shard_map/ppermute | solution.py:120
  208.2 0.6 slice_reduce_fusion
  208.8 0.7 slice.117
  (41 shorter events, 3.4 us)
Async XLA Ops:
  7.2 4.4 %copy-start.3 = (f32[24]{0:T(128)S(1)}, f32[24]{0:T(128)}, u32[]{:S(2)}) copy-start(f32[24]{0:T(128)} %param.5) | copy-start | bytes 292
  7.2 34.5 %all-gather.9.cloned.1.call-start = ((), (), s32[]{:S(2)}) async-start(), calls=%async_computation.2 | async-start | bytes 2654208 | tf_op jit(solution)/shard_map/all_gather | solution.py:90
  9.5 63.0 %all-gather.11.cloned.1.call-start = ((), (), s32[]{:S(2)}) async-start(), calls=%async_computation.3 | async-start | bytes 2654208 | tf_op jit(solution)/shard_map/all_gather | solution.py:90
  10.3 93.2 %all-gather.7.cloned.1.call-start = ((), (), s32[]{:S(2)}) async-start(), calls=%async_computation.1 | async-start | bytes 2654208 | tf_op jit(solution)/shard_map/all_gather | solution.py:90
  11.0 123.3 %all-gather.5.cloned.1.call-start = ((), (), s32[]{:S(2)}) async-start(), calls=%async_computation | async-start | bytes 2654208 | tf_op jit(solution)/shard_map/all_gather | solution.py:90
  141.0 5.5 %collective-permute-start.6 = (f32[2,512]{1,0:T(2,128)S(1)}, f32[2,512]{1,0:T(2,128)S(1)}, u32[]{:S(2)}, u32[]{:S(2)}) collective-permute-start(f32[2,512]{1,0:T(2,128)S(1)} %pad_maximum_fusion.1), channel_id=1, source_target_pairs={{0,7},{1,0},{2,1},{3,2},{4,3},{5,4},{6,5},{7,6},{8,15},{9,8},{10,9... | collective-permute-start | bytes 12296 | tf_op jit(solution)/shard_map/ppermute | solution.py:70
  143.0 5.9 %collective-permute-start.5 = (f32[2,512]{1,0:T(2,128)S(1)}, f32[2,512]{1,0:T(2,128)S(1)}, u32[]{:S(2)}, u32[]{:S(2)}) collective-permute-start(f32[2,512]{1,0:T(2,128)S(1)} %pad_maximum_fusion.1), channel_id=1, source_target_pairs={{0,6},{1,7},{2,0},{3,1},{4,2},{5,3},{6,4},{7,5},{8,14},{9,15},{10,... | collective-permute-start | bytes 12296 | tf_op jit(solution)/shard_map/ppermute | solution.py:70
  144.3 4.8 %collective-permute-start.4 = (f32[2,512]{1,0:T(2,128)S(1)}, f32[2,512]{1,0:T(2,128)S(1)}, u32[]{:S(2)}, u32[]{:S(2)}) collective-permute-start(f32[2,512]{1,0:T(2,128)S(1)} %pad_maximum_fusion.1), channel_id=1, source_target_pairs={{0,5},{1,6},{2,7},{3,0},{4,1},{5,2},{6,3},{7,4},{8,13},{9,14},{10,... | collective-permute-start | bytes 12296 | tf_op jit(solution)/shard_map/ppermute | solution.py:70
  144.4 4.7 %collective-permute-start.3 = (f32[2,512]{1,0:T(2,128)S(1)}, f32[2,512]{1,0:T(2,128)S(1)}, u32[]{:S(2)}, u32[]{:S(2)}) collective-permute-start(f32[2,512]{1,0:T(2,128)S(1)} %pad_maximum_fusion.1), channel_id=1, source_target_pairs={{0,4},{1,5},{2,6},{3,7},{4,0},{5,1},{6,2},{7,3},{8,12},{9,13},{10,... | collective-permute-start | bytes 12296 | tf_op jit(solution)/shard_map/ppermute | solution.py:70
  145.0 4.2 %collective-permute-start.2 = (f32[2,512]{1,0:T(2,128)S(1)}, f32[2,512]{1,0:T(2,128)S(1)}, u32[]{:S(2)}, u32[]{:S(2)}) collective-permute-start(f32[2,512]{1,0:T(2,128)S(1)} %pad_maximum_fusion.1), channel_id=1, source_target_pairs={{0,3},{1,4},{2,5},{3,6},{4,7},{5,0},{6,1},{7,2},{8,11},{9,12},{10,... | collective-permute-start | bytes 12296 | tf_op jit(solution)/shard_map/ppermute | solution.py:70
  146.5 4.5 %collective-permute-start.1 = (f32[2,512]{1,0:T(2,128)S(1)}, f32[2,512]{1,0:T(2,128)S(1)}, u32[]{:S(2)}, u32[]{:S(2)}) collective-permute-start(f32[2,512]{1,0:T(2,128)S(1)} %pad_maximum_fusion.1), channel_id=1, source_target_pairs={{0,2},{1,3},{2,4},{3,5},{4,6},{5,7},{6,0},{7,1},{8,10},{9,11},{10,... | collective-permute-start | bytes 12296 | tf_op jit(solution)/shard_map/ppermute | solution.py:70
  148.8 4.2 %collective-permute-start = (f32[2,512]{1,0:T(2,128)S(1)}, f32[2,512]{1,0:T(2,128)S(1)}, u32[]{:S(2)}, u32[]{:S(2)}) collective-permute-start(f32[2,512]{1,0:T(2,128)S(1)} %pad_maximum_fusion.1), channel_id=1, source_target_pairs={{0,1},{1,2},{2,3},{3,4},{4,5},{5,6},{6,7},{7,0},{8,9},{9,10},{10,1... | collective-permute-start | bytes 12296 | tf_op jit(solution)/shard_map/ppermute | solution.py:70
  177.5 7.6 %copy-start = (f32[1,24,2432]{2,1,0:T(8,128)S(1)}, f32[1,24,2432]{2,1,0:T(8,128)}, u32[]{:S(2)}) copy-start(f32[1,24,2432]{2,1,0:T(8,128)} %shard_map.53) | copy-start | bytes 700420
  177.5 7.6 %copy-start.1 = (f32[1,24,2432]{2,1,0:T(8,128)S(1)}, f32[1,24,2432]{2,1,0:T(8,128)}, u32[]{:S(2)}) copy-start(f32[1,24,2432]{2,1,0:T(8,128)} %shard_map.52) | copy-start | bytes 700420
  177.5 7.6 %copy-start.2 = (f32[1,24,2432]{2,1,0:T(8,128)S(1)}, f32[1,24,2432]{2,1,0:T(8,128)}, u32[]{:S(2)}) copy-start(f32[1,24,2432]{2,1,0:T(8,128)} %shard_map.51) | copy-start | bytes 700420
  186.2 10.6 %collective-permute-start.7 = (f32[24,2432]{1,0:T(8,128)S(1)}, f32[24,2432]{1,0:T(8,128)S(1)}, u32[]{:S(2)}, u32[]{:S(2)}) collective-permute-start(f32[24,2432]{1,0:T(8,128)S(1)} %get-tuple-element.6), channel_id=1, source_target_pairs={{0,8},{8,16},{16,24},{24,0},{1,9},{9,17},{17,25},{25,1},{2,10},{10... | collective-permute-start | bytes 700424 | tf_op jit(solution)/shard_map/ppermute | solution.py:120
  187.8 10.1 %collective-permute-start.9 = (f32[24,2432]{1,0:T(8,128)S(1)}, f32[24,2432]{1,0:T(8,128)S(1)}, u32[]{:S(2)}, u32[]{:S(2)}) collective-permute-start(f32[24,2432]{1,0:T(8,128)S(1)} %get-tuple-element.7), channel_id=1, source_target_pairs={{0,24},{8,0},{16,8},{24,16},{1,25},{9,1},{17,9},{25,17},{2,26},{10... | collective-permute-start | bytes 700424 | tf_op jit(solution)/shard_map/ppermute | solution.py:120
  190.1 18.0 %collective-permute-start.8 = (f32[24,2432]{1,0:T(8,128)S(1)}, f32[24,2432]{1,0:T(8,128)S(1)}, u32[]{:S(2)}, u32[]{:S(2)}) collective-permute-start(f32[24,2432]{1,0:T(8,128)S(1)} %get-tuple-element.8), channel_id=1, source_target_pairs={{0,16},{8,24},{16,0},{24,8},{1,17},{9,25},{17,1},{25,9},{2,18},{10... | collective-permute-start | bytes 700424 | tf_op jit(solution)/shard_map/ppermute | solution.py:120
Sparse Core Ops, SparseCore 0:
  9.9 31.7 all-gather.8
  43.5 29.0 all-gather.10
  74.5 29.0 all-gather.6
  105.3 29.0 all-gather.4

commit v4 on v2

--- a/solution.py
+++ b/solution.py
@@ -23,15 +23,17 @@
     for row0 in range(0, classes_here, rows):
         for col0 in range(0, width, cols):
             angle = angle_ref[:, col0 : col0 + cols]
-            total = products_ref[row0 : row0 + rows, col0 : col0 + cols]
+            kept = products_ref[row0 : row0 + rows, col0 : col0 + cols]
+            every = None
             for turn_index in range(1, rotations):
                 start = turn_index * classes_here + row0
                 part = products_ref[start : start + rows, col0 : col0 + cols]
                 step = turn_index * shift
                 ahead = pltpu.roll(part, cols - step, 1)
-                behind = pltpu.roll(part, ANG - step, 1)
-                total = total + jnp.where(angle < ANG - step, ahead, behind)
-            out_ref[0, row0 : row0 + rows, col0 : col0 + cols] = total
+                kept = kept + jnp.where(angle < ANG - step, ahead, 0.0)
+                every = ahead if every is None else every + ahead
+            wrapped = every - (kept - products_ref[row0 : row0 + rows, col0 : col0 + cols])
+            out_ref[0, row0 : row0 + rows, col0 : col0 + cols] = kept + pltpu.roll(wrapped, ANG, 1)
     mass = jnp.sum(by_turn_ref[...].astype(jnp.float32), axis=1, keepdims=True)
     class_mass = mass[0:classes_here]
     for turn_index in range(1, rotations):

time: 155 us -> 147 us (0.948)
  Pallas kernels: 22.5 us -> 14.6 us
    pallas_call x1, Pallas kernels: 22.5 us -> 14.6 us  [turn_and_sum(): pl.pallas_call(functools.partial(turn_sum_kernel, classes_here, rotations...]
  transfers between devices with their start and end apart: 2 -> 2, of which waited for: 2 -> 2; matrix products, arithmetic and copies ran while one was open for 5% -> 6% of each run, Pallas kernels for 0% -> 0%
where the time goes in v4:
time: 147 us
  waiting for transfers between devices  81.4 us (55%)
  Pallas kernels  14.6 us (10%)
  matrix products  14.1 us (10%)
  between operations  14.1 us (10%)
  blocking collectives  9.02 us (6%)
  other arithmetic  8.32 us (6%)
  local copies, waits for them, and re-layouts  5.14 us (3%)
    all_gather x1, waiting for transfers between devices, per_device(): gathered = lax.all_gather(images, 'ref', axis=0, tiled=True)  55 us
    unnamed x3, waiting for transfers between devices  26.4 us
    pallas_call x1, Pallas kernels, turn_and_sum(): pl.pallas_call(functools.partial(turn_sum_kernel, classes_here, rotations...  14.6 us
    dot_general x1, matrix products, per_device(): lax.dot_general(gathered, references, (((1,), (1,)), ((), ())), preferred...  14.1 us
    all_gather x1, blocking collectives, per_device(): stats = lax.all_gather(jnp.stack([local_max, local_sum]), 'ref', axis=0)  9.02 us
    dot_general x1, other arithmetic, per_device(): jnp.einsum('jp,jp->j', references, references, preferred_element_type=jnp...  7 us
    slice x2, local copies, waits for them, and re-layouts, per_device(): return (reduced[:, :width], reduced[:, width])  2.97 us
  transfers between devices with their start and end apart: 2, of which 2 were waited for; matrix products, arithmetic and copies ran while one was open for 6% of the time, Pallas kernels for 0%

profile of v4, /device:TPU:0, one launch (start us, length us, event | category | flops | bytes accessed | tf_op | source)
XLA Modules:
  0.0 146.8 jit_solution(16435577076418717653)
XLA Ops:
  7.2 0.0 all-gather.4.cloned.1.call-start
  7.2 0.7 all-gather.4.cloned.1.call-update
  7.9 0.0 reduce-scatter.4.cloned.1.call-start
  7.9 0.7 log.3
  8.6 0.1 sub.36
  8.7 0.1 sub.37
  8.8 7.0 %fusion = f32[864]{0:T(1024)S(1)} fusion(bf16[864,9216]{1,0:T(8,128)(2,1)} %param.4), kind=kLoop, calls=%fused_computation.1 | loop fusion | flops 23887008 | bytes 15928704 | tf_op jit(solution)/shard_map/jp,jp->j/dot_general | solution.py:74
  15.8 0.6 and_select_fusion.angle_ref
  16.4 55.0 %all-gather.4.cloned.1.call-done.images_ref = bf16[512,9216]{1,0:T(8,128)(2,1)} async-done(((bf16[64,9216]{1,0:T(8,128)(2,1)}), bf16[512,9216]{1,0:T(8,128)(2,1)}) %all-gather.4.cloned.1.call-update) | async-done | bytes 9437200 | tf_op jit(solution)/shard_map/all_gather | solution.py:80
  71.4 14.1 %fusion.4 = (f32[512]{0:T(512)S(1)}, f32[512,864]{0,1:T(8,128)S(1)}) fusion(f32[864]{0:T(1024)S(1)} %multiply_subtract_fusion, bf16[512,9216]{1,0:T(8,128)(2,1)} %all-gather.4.cloned.1.call-done.images_ref, bf16[864,9216]{1,0:T(8,128)(2,1)} %param.4), kind=kOutput, calls=%fused_computation.15 | convolution fusion | flops 8154611200 | bytes 27137408 | tf_op jit(solution)/shard_map/dot_general | solution.py:81
  85.6 0.3 exponential_reduce_fusion
  85.9 9.0 %all-gather.1 = f32[8,2,512]{2,1,0:T(2,128)S(1)} all-gather(f32[1,2,512]{2,1,0:T(2,128)S(1)} %maximum_bitcast_fusion), channel_id=2, replica_groups=mesh['img'=4,'ref'=8] {'ref'}, dimensions={0}, use_global_device_ids=true | all-gather | bytes 36864 | tf_op jit(solution)/shard_map/all_gather | solution.py:87
  95.0 0.3 divide_convert_fusion
  95.3 0.2 reshape.46
  95.5 1.2 copy.10
  96.7 14.6 %shard_map.50 = f32[4,24,2432]{2,1,0:T(8,128)} custom-call(bf16[864,512]{1,0:T(8,128)(2,1)} %bitcast.25, bf16[512,9216]{1,0:T(8,128)(2,1)} %all-gather.4.cloned.1.call-done.images_ref, s32[1,2304]{1,0:T(1,128)} %and_select_fusion.angle_ref), custom_call_target="tpu_custom_call" | custom-call | flops 8153726976 | bytes 11206656 | tf_op jit(solution)/shard_map/pallas_call | solution.py:49
  111.3 0.0 reduce-scatter.4.cloned.1.call-update
  111.3 25.7 %reduce-scatter.4.cloned.1.call-done = f32[1,24,2432]{2,1,0:T(8,128)} async-done(((f32[4,24,2432]{2,1,0:T(8,128)}), f32[1,24,2432]{2,1,0:T(8,128)}) %reduce-scatter.4.cloned.1.call-update) | async-done | bytes 233488
  137.0 1.6 %slice.19 = f32[24,2304]{1,0:T(8,128)} slice(f32[24,2432]{1,0:T(8,128)} %bitcast.26), slice={[0:24], [0:2304]} | slice | bytes 442368 | tf_op jit(solution)/shard_map/slice | solution.py:97
  138.7 1.3 slice_reduce_fusion
  (4 shorter events, 0.1 us)
Async XLA Ops:
  7.2 64.3 %all-gather.4.cloned.1.call-start = ((), (), s32[]{:S(2)}) async-start(), calls=%async_computation.1 | async-start | bytes 10616832 | tf_op jit(solution)/shard_map/all_gather | solution.py:80
  7.9 129.1 %reduce-scatter.4.cloned.1.call-start = ((), (), s32[]{:S(2)}) async-start(), calls=%async_computation.2 | async-start | bytes 1167360
Sparse Core Ops, SparseCore 0:
  9.9 61.5 all-gather.3
  111.4 25.5 reduce-scatter.3

commit v5 on v4

--- a/solution.py
+++ b/solution.py
@@ -12,12 +12,15 @@
 GROUP_COLS = 1152
 
 
-def turn_sum_kernel(classes_here, rotations, by_turn_ref, images_ref, angle_ref, out_ref, products_ref):
+def turn_sum_kernel(
+    classes_here, rotations, by_turn_ref, own_ref, partner_ref, angle_ref, out_ref, products_ref
+):
     shift = ANG // rotations
-    width = images_ref.shape[1]
+    width = own_ref.shape[1]
+    half = own_ref.shape[0]
     products_ref[...] = jnp.dot(
-        by_turn_ref[...], images_ref[...], preferred_element_type=jnp.float32
-    )
+        by_turn_ref[:, 0:half], own_ref[...], preferred_element_type=jnp.float32
+    ) + jnp.dot(by_turn_ref[:, half:], partner_ref[...], preferred_element_type=jnp.float32)
     rows = 8 if classes_here % 8 == 0 else classes_here
     cols = GROUP_COLS if width % GROUP_COLS == 0 else width
     for row0 in range(0, classes_here, rows):
@@ -41,9 +44,9 @@
     out_ref[0, :, width:] = jnp.broadcast_to(class_mass, (classes_here, LANES))
 
 
-def turn_and_sum(by_turn, gathered, classes_here, rotations, chunks):
+def turn_and_sum(by_turn, own, partner, classes_here, rotations, chunks):
     local_refs, n = by_turn.shape
-    pixels = gathered.shape[1]
+    half, pixels = own.shape
     width = pixels // chunks
     angle = (jnp.arange(width, dtype=jnp.int32) % ANG).reshape(1, width)
     return pl.pallas_call(
@@ -51,7 +54,8 @@
         grid=(chunks,),
         in_specs=[
             pl.BlockSpec((local_refs, n), lambda t: (0, 0)),
-            pl.BlockSpec((n, width), lambda t: (0, t)),
+            pl.BlockSpec((half, width), lambda t: (0, t)),
+            pl.BlockSpec((half, width), lambda t: (0, t)),
             pl.BlockSpec((1, width), lambda t: (0, 0)),
         ],
         out_specs=pl.BlockSpec((1, classes_here, width + LANES), lambda t: (t, 0, 0)),
@@ -63,10 +67,10 @@
             bytes_accessed=2 * local_refs * n + 2 * n * pixels + 4 * classes_here * pixels,
             transcendentals=0,
         ),
-    )(by_turn, gathered, angle)
+    )(by_turn, own, partner, angle)
 
 
-def per_device(chunks, images, references, class_prior):
+def per_device(chunks, n_ref, images, references, class_prior):
     local_refs, pixels = references.shape
     classes_here = class_prior.shape[0]
     rotations = local_refs // classes_here
@@ -77,21 +81,43 @@
     offsets = (jnp.log(class_prior)[:, None] - half_norm.reshape(classes_here, rotations)).reshape(
         local_refs
     )
-    gathered = lax.all_gather(images, "ref", axis=0, tiled=True)
-    products = lax.dot_general(
-        gathered, references, (((1,), (1,)), ((), ())), preferred_element_type=jnp.float32
-    )
-    scores = products + offsets
-    local_max = jnp.max(scores, axis=1)
-    local_sum = jnp.sum(jnp.exp(scores - local_max[:, None]), axis=1)
-    stats = lax.all_gather(jnp.stack([local_max, local_sum]), "ref", axis=0)
+    core = lax.axis_index("ref") % 2
+    same_core = [[c + 2 * i for i in range(n_ref // 2)] for c in range(2)]
+    own = lax.all_gather(images, "ref", axis=0, tiled=True, axis_index_groups=same_core)
+    partner = lax.ppermute(own, "ref", [(d, d ^ 1) for d in range(n_ref)])
+
+    def scores_of(block):
+        products = lax.dot_general(
+            block, references, (((1,), (1,)), ((), ())), preferred_element_type=jnp.float32
+        )
+        return products + offsets
+
+    own_scores = scores_of(own)
+    partner_scores = scores_of(partner)
+
+    def local_stats(scores):
+        local_max = jnp.max(scores, axis=1)
+        return jnp.stack([local_max, jnp.sum(jnp.exp(scores - local_max[:, None]), axis=1)])
+
+    mine, theirs = local_stats(own_scores), local_stats(partner_scores)
+    common = jnp.where(core == 0, jnp.concatenate([mine, theirs], 1), jnp.concatenate([theirs, mine], 1))
+    stats = lax.all_gather(common, "ref", axis=0)
     top_score = jnp.max(stats[:, 0], axis=0)
     denominator = jnp.sum(stats[:, 1] * jnp.exp(stats[:, 0] - top_score[None, :]), axis=0)
-    weights = (jnp.exp(scores - top_score[:, None]) / denominator[:, None]).astype(jnp.bfloat16)
+    half = own.shape[0]
+    norm = jnp.stack([top_score, denominator])
+    norm = jnp.where(core == 0, norm, jnp.concatenate([norm[:, half:], norm[:, :half]], 1))
+
+    def weights_of(scores, part):
+        return (jnp.exp(scores - part[0][:, None]) / part[1][:, None]).astype(jnp.bfloat16)
+
+    weights = jnp.concatenate(
+        [weights_of(own_scores, norm[:, :half]), weights_of(partner_scores, norm[:, half:])], axis=0
+    )
 
     n = weights.shape[0]
     by_turn = weights.reshape(n, classes_here, rotations).transpose(2, 1, 0).reshape(local_refs, n)
-    chunked = turn_and_sum(by_turn, gathered, classes_here, rotations, chunks)
+    chunked = turn_and_sum(by_turn, own, partner, classes_here, rotations, chunks)
     reduced = lax.psum_scatter(chunked, "img", scatter_dimension=0, tiled=True)[0]
     width = pixels // chunks
     return (reduced[:, :width], reduced[:, width])
@@ -100,7 +126,7 @@
 def solution(mesh):
     placed = (P(("img", "ref"), None), P("ref", None), P("ref"))
     return jax.shard_map(
-        functools.partial(per_device, mesh.shape["img"]),
+        functools.partial(per_device, mesh.shape["img"], mesh.shape["ref"]),
         mesh=mesh,
         in_specs=placed,
         out_specs=(P("ref", "img"), P("ref")),

time: 147 us -> 158 us (1.075)
  waiting for transfers between devices: 81.4 us -> 88.1 us
  local copies, waits for them, and re-layouts: 5.14 us -> 7.51 us
  Pallas kernels: 14.6 us -> 16.9 us
    all_gather x1, waiting for transfers between devices: 55 us -> 61.7 us  [per_device(): lax.all_gather(images, 'ref', axis=0, tiled=True, axis_index_groups=same_...]
    unnamed x0 -> x2, local copies, waits for them, and re-layouts: none -> 2.37 us
    pallas_call x1, Pallas kernels: 14.6 us -> 16.9 us  [turn_and_sum(): pl.pallas_call(functools.partial(turn_sum_kernel, classes_here, rotations...]
    dot_general x1 -> x2, matrix products: 14.1 us -> 13.5 us  [scores_of(): lax.dot_general(block, references, (((1,), (1,)), ((), ())), preferred_el...]
  transfers between devices with their start and end apart: 2 -> 3, of which waited for: 2 -> 2; matrix products, arithmetic and copies ran while one was open for 6% -> 10% of each run, Pallas kernels for 0% -> 0%
where the time goes in v5:
time: 158 us
  waiting for transfers between devices  88.1 us (56%)
  Pallas kernels  16.9 us (11%)
  between operations  14.1 us (9%)
  matrix products  13.5 us (9%)
  blocking collectives  9.21 us (6%)
  other arithmetic  8.71 us (6%)
  local copies, waits for them, and re-layouts  7.51 us (5%)
    all_gather x1, waiting for transfers between devices, per_device(): lax.all_gather(images, 'ref', axis=0, tiled=True, axis_index_groups=same_...  61.7 us
    unnamed x3, waiting for transfers between devices  26.4 us
    pallas_call x1, Pallas kernels, turn_and_sum(): pl.pallas_call(functools.partial(turn_sum_kernel, classes_here, rotations...  16.9 us
    dot_general x2, matrix products, scores_of(): lax.dot_general(block, references, (((1,), (1,)), ((), ())), preferred_el...  13.5 us
    all_gather x1, blocking collectives, per_device(): stats = lax.all_gather(common, 'ref', axis=0)  9.21 us
    dot_general x1, other arithmetic, per_device(): jnp.einsum('jp,jp->j', references, references, preferred_element_type=jnp...  7.24 us
  transfers between devices with their start and end apart: 3, of which 2 were waited for; matrix products, arithmetic and copies ran while one was open for 10% of the time, Pallas kernels for 0%

profile of v5, /device:TPU:0, one launch (start us, length us, event | category | flops | bytes accessed | tf_op | source)
XLA Modules:
  0.0 158.1 jit_solution(8994937952170005949)
XLA Ops:
  7.2 0.0 all-gather.2.cloned.1.call-start
  7.2 0.7 all-gather.2.cloned.1.call-update
  7.9 0.0 reduce-scatter.4.cloned.1.call-start
  7.9 61.7 %all-gather.2.cloned.1.call-done.own_ref = bf16[256,9216]{1,0:T(8,128)(2,1)} async-done(((bf16[64,9216]{1,0:T(8,128)(2,1)}), bf16[256,9216]{1,0:T(8,128)(2,1)}) %all-gather.2.cloned.1.call-update) | async-done | bytes 4718608 | tf_op jit(solution)/shard_map/all_gather | solution.py:86
  69.6 0.0 collective-permute-start
  69.6 0.7 log.3
  70.3 0.1 sub.56
  70.4 0.1 sub.57
  70.5 0.0 copy-start
  70.5 7.2 %fusion = f32[864]{0:T(1024)S(1)} fusion(bf16[864,9216]{1,0:T(8,128)(2,1)} %param.4), kind=kLoop, calls=%fused_computation.1 | loop fusion | flops 23887008 | bytes 15928704 | tf_op jit(solution)/shard_map/jp,jp->j/dot_general | solution.py:78
  77.7 0.6 and_select_fusion.angle_ref
  78.4 2.4 %copy-done = bf16[864,9216]{1,0:T(8,128)(2,1)S(1)} copy-done((bf16[864,9216]{1,0:T(8,128)(2,1)S(1)}, bf16[864,9216]{1,0:T(8,128)(2,1)}, u32[]{:S(2)}) %copy-start) | copy-done | bytes 15925272
  80.7 6.8 %fusion.10 = (f32[256]{0:T(256)S(1)}, f32[256,864]{0,1:T(8,128)S(1)}) fusion(f32[864]{0:T(1024)S(1)} %multiply_subtract_fusion, bf16[256,9216]{1,0:T(8,128)(2,1)} %all-gather.2.cloned.1.call-done.own_ref, bf16[864,9216]{1,0:T(8,128)(2,1)S(1)} %copy-done), kind=kOutput, calls=%fused_computation.31 | convolution fusion | flops 4077305600 | bytes 21533056 | tf_op jit(solution)/shard_map/dot_general | solution.py:90
  87.5 0.2 exponential_reduce_fusion.1
  87.7 0.0 collective-permute-done.partner_ref
  87.7 6.8 %fusion.9 = (f32[256]{0:T(256)S(1)}, f32[256,864]{0,1:T(8,128)S(1)}) fusion(f32[864]{0:T(1024)S(1)} %multiply_subtract_fusion, bf16[256,9216]{1,0:T(8,128)(2,1)} %collective-permute-done.partner_ref, bf16[864,9216]{1,0:T(8,128)(2,1)S(1)} %copy-done), kind=kOutput, calls=%fused_computation.30 | convolution fusion | flops 4077305600 | bytes 21533056 | tf_op jit(solution)/shard_map/dot_general | solution.py:90
  94.5 0.2 exponential_reduce_fusion
  94.7 9.2 %all_gather.8 = f32[8,2,512]{2,1,0:T(2,128)S(1)} all-gather(f32[1,2,512]{2,1,0:T(2,128)S(1)} %maximum_select_fusion), channel_id=1, replica_groups=mesh['img'=4,'ref'=8] {'ref'}, dimensions={0}, use_global_device_ids=true | all-gather | bytes 36864 | tf_op jit(solution)/shard_map/all_gather | solution.py:104
  104.0 0.1 divide_convert_fusion.1
  104.2 0.1 divide_convert_fusion
  104.3 0.1 pad_maximum_fusion
  104.4 0.2 reshape.104
  104.6 1.2 copy.10
  105.8 16.9 %shard_map.50 = f32[4,24,2432]{2,1,0:T(8,128)} custom-call(bf16[864,512]{1,0:T(8,128)(2,1)} %bitcast.37, bf16[256,9216]{1,0:T(8,128)(2,1)} %all-gather.2.cloned.1.call-done.own_ref, bf16[256,9216]{1,0:T(8,128)(2,1)} %collective-permute-done.partner_ref, s32[1,2304]{1,0:T(1,128)} %and_select_fusion.angle_ref), custom_call_target="tpu_custom_call" | custom-call | flops 8153726976 | bytes 11206656 | tf_op jit(solution)/shard_map/pallas_call | solution.py:52
  122.6 0.0 reduce-scatter.4.cloned.1.call-update
  122.6 25.7 %reduce-scatter.4.cloned.1.call-done = f32[1,24,2432]{2,1,0:T(8,128)} async-done(((f32[4,24,2432]{2,1,0:T(8,128)}), f32[1,24,2432]{2,1,0:T(8,128)}) %reduce-scatter.4.cloned.1.call-update) | async-done | bytes 233488
  148.3 1.6 %slice.57 = f32[24,2304]{1,0:T(8,128)} slice(f32[24,2432]{1,0:T(8,128)} %bitcast.38), slice={[0:24], [0:2304]} | slice | bytes 442368 | tf_op jit(solution)/shard_map/slice | solution.py:123
  150.0 1.3 slice_reduce_fusion
  (8 shorter events, 0.1 us)
Async XLA Ops:
  7.2 62.5 %all-gather.2.cloned.1.call-start = ((), (), s32[]{:S(2)}) async-start(), calls=%async_computation.1 | async-start | bytes 5898240 | tf_op jit(solution)/shard_map/all_gather | solution.py:86
  7.9 140.4 %reduce-scatter.4.cloned.1.call-start = ((), (), s32[]{:S(2)}) async-start(), calls=%async_computation.2 | async-start | bytes 1167360
  69.6 18.1 %collective-permute-start = (bf16[256,9216]{1,0:T(8,128)(2,1)}, bf16[256,9216]{1,0:T(8,128)(2,1)}, u32[]{:S(2)}, u32[]{:S(2)}) collective-permute-start(bf16[256,9216]{1,0:T(8,128)(2,1)} %all-gather.2.cloned.1.call-done.own_ref), channel_id=1, source_target_pairs={{0,1},{1,0},{2,3},{3,2},{4,5},{5,4},{6,7},{7,6},{8,9},{9,8},{10,11... | collective-permute-start | bytes 14155784 | tf_op jit(solution)/shard_map/ppermute | solution.py:87
  70.5 10.3 %copy-start = (bf16[864,9216]{1,0:T(8,128)(2,1)S(1)}, bf16[864,9216]{1,0:T(8,128)(2,1)}, u32[]{:S(2)}) copy-start(bf16[864,9216]{1,0:T(8,128)(2,1)} %param.4) | copy-start | bytes 47775748
Sparse Core Ops, SparseCore 0:
  9.8 59.7 all-gather.1
  122.8 25.5 reduce-scatter.3

commit v6 on v4

--- a/solution.py
+++ b/solution.py
@@ -34,11 +34,6 @@
                 every = ahead if every is None else every + ahead
             wrapped = every - (kept - products_ref[row0 : row0 + rows, col0 : col0 + cols])
             out_ref[0, row0 : row0 + rows, col0 : col0 + cols] = kept + pltpu.roll(wrapped, ANG, 1)
-    mass = jnp.sum(by_turn_ref[...].astype(jnp.float32), axis=1, keepdims=True)
-    class_mass = mass[0:classes_here]
-    for turn_index in range(1, rotations):
-        class_mass = class_mass + mass[turn_index * classes_here : (turn_index + 1) * classes_here]
-    out_ref[0, :, width:] = jnp.broadcast_to(class_mass, (classes_here, LANES))
 
 
 def turn_and_sum(by_turn, gathered, classes_here, rotations, chunks):
@@ -54,8 +49,8 @@
             pl.BlockSpec((n, width), lambda t: (0, t)),
             pl.BlockSpec((1, width), lambda t: (0, 0)),
         ],
-        out_specs=pl.BlockSpec((1, classes_here, width + LANES), lambda t: (t, 0, 0)),
-        out_shape=jax.ShapeDtypeStruct((chunks, classes_here, width + LANES), jnp.float32),
+        out_specs=pl.BlockSpec((1, classes_here, width), lambda t: (t, 0, 0)),
+        out_shape=jax.ShapeDtypeStruct((chunks, classes_here, width), jnp.float32),
         scratch_shapes=[pltpu.VMEM((local_refs, width), jnp.float32)],
         compiler_params=pltpu.CompilerParams(vmem_limit_bytes=60 * 1024 * 1024),
         cost_estimate=pl.CostEstimate(
@@ -91,11 +86,16 @@
 
     n = weights.shape[0]
     by_turn = weights.reshape(n, classes_here, rotations).transpose(2, 1, 0).reshape(local_refs, n)
+    local_mass = (
+        jnp.sum(weights.astype(jnp.float32), axis=0).reshape(classes_here, rotations).sum(axis=1)
+    )
+    class_weights = local_mass
+    for step in range(1, chunks):
+        perm = [(src, (src + step) % chunks) for src in range(chunks)]
+        class_weights = class_weights + lax.ppermute(local_mass, "img", perm)
     chunked = turn_and_sum(by_turn, gathered, classes_here, rotations, chunks)
-    reduced = lax.psum_scatter(chunked, "img", scatter_dimension=0, tiled=True)[0]
-    width = pixels // chunks
-    return (reduced[:, :width], reduced[:, width])
-
+    class_sums = lax.psum_scatter(chunked, "img", scatter_dimension=0, tiled=True)
+    return (class_sums[0], class_weights)
 
 def solution(mesh):
     placed = (P(("img", "ref"), None), P("ref", None), P("ref"))

time: 147 us -> 143 us (0.973)
  waiting for transfers between devices: 81.4 us -> 74.4 us
  starting transfers between devices: 0.08 us -> 5.45 us
  local copies, waits for them, and re-layouts: 5.14 us -> 2.24 us
    unnamed x3 -> x2, waiting for transfers between devices: 26.4 us -> 0.7 us
    reduce_scatter x0 -> x1, waiting for transfers between devices: none -> 16.6 us  [per_device(): lax.psum_scatter(chunked, 'img', scatter_dimension=0, tiled=True)]
    ppermute x0 -> x3, starting transfers between devices: none -> 5.38 us  [per_device(): class_weights = class_weights + lax.ppermute(local_mass, 'img', perm)]
    slice x2 -> x0, local copies, waits for them, and re-layouts: 2.97 us -> none  [per_device(): return (reduced[:, :width], reduced[:, width])]
    ppermute x0 -> x3, waiting for transfers between devices: none -> 2.1 us  [per_device(): class_weights = class_weights + lax.ppermute(local_mass, 'img', perm)]
  transfers between devices with their start and end apart: 2 -> 5, of which waited for: 2 -> 4; matrix products, arithmetic and copies ran while one was open for 6% -> 6% of each run, Pallas kernels for 0% -> 0%
where the time goes in v6:
time: 143 us
  waiting for transfers between devices  74.4 us (52%)
  Pallas kernels  14.5 us (10%)
  matrix products  14.1 us (10%)
  between operations  14.1 us (10%)
  other arithmetic  9.05 us (6%)
  blocking collectives  9.02 us (6%)
  starting transfers between devices  5.45 us (4%)
  local copies, waits for them, and re-layouts  2.24 us (2%)
    all_gather x1, waiting for transfers between devices, per_device(): gathered = lax.all_gather(images, 'ref', axis=0, tiled=True)  55 us
    reduce_scatter x1, waiting for transfers between devices, per_device(): lax.psum_scatter(chunked, 'img', scatter_dimension=0, tiled=True)  16.6 us
    pallas_call x1, Pallas kernels, turn_and_sum(): pl.pallas_call(functools.partial(turn_sum_kernel, classes_here, rotations...  14.5 us
    dot_general x1, matrix products, per_device(): lax.dot_general(gathered, references, (((1,), (1,)), ((), ())), preferred...  14.1 us
    all_gather x1, blocking collectives, per_device(): stats = lax.all_gather(jnp.stack([local_max, local_sum]), 'ref', axis=0)  9.02 us
    dot_general x1, other arithmetic, per_device(): jnp.einsum('jp,jp->j', references, references, preferred_element_type=jnp...  7 us
    ppermute x3, starting transfers between devices, per_device(): class_weights = class_weights + lax.ppermute(local_mass, 'img', perm)  5.38 us
  transfers between devices with their start and end apart: 5, of which 4 were waited for; matrix products, arithmetic and copies ran while one was open for 6% of the time, Pallas kernels for 0%

profile of v6, /device:TPU:0, one launch (start us, length us, event | category | flops | bytes accessed | tf_op | source)
XLA Modules:
  0.0 142.9 jit_solution(14532213579058792866)
XLA Ops:
  7.2 0.0 all-gather.4.cloned.1.call-start
  7.2 0.7 all-gather.4.cloned.1.call-update
  7.9 0.0 reduce-scatter.2.cloned.1.call-start
  7.9 0.7 log.3
  8.6 0.1 sub.36
  8.7 0.1 sub.37
  8.8 7.0 %fusion = f32[864]{0:T(1024)S(1)} fusion(bf16[864,9216]{1,0:T(8,128)(2,1)} %param.4), kind=kLoop, calls=%fused_computation.1 | loop fusion | flops 23887008 | bytes 15928704 | tf_op jit(solution)/shard_map/jp,jp->j/dot_general | solution.py:69
  15.8 0.6 and_select_fusion.angle_ref
  16.4 55.0 %all-gather.4.cloned.1.call-done.images_ref = bf16[512,9216]{1,0:T(8,128)(2,1)} async-done(((bf16[64,9216]{1,0:T(8,128)(2,1)}), bf16[512,9216]{1,0:T(8,128)(2,1)}) %all-gather.4.cloned.1.call-update) | async-done | bytes 9437200 | tf_op jit(solution)/shard_map/all_gather | solution.py:75
  71.4 14.1 %fusion.4 = (f32[512]{0:T(512)S(1)}, f32[512,864]{0,1:T(8,128)S(1)}) fusion(f32[864]{0:T(1024)S(1)} %multiply_subtract_fusion, bf16[512,9216]{1,0:T(8,128)(2,1)} %all-gather.4.cloned.1.call-done.images_ref, bf16[864,9216]{1,0:T(8,128)(2,1)} %param.4), kind=kOutput, calls=%fused_computation.16 | convolution fusion | flops 8154611200 | bytes 27137408 | tf_op jit(solution)/shard_map/dot_general | solution.py:76
  85.6 0.3 exponential_reduce_fusion
  85.9 9.0 %all-gather.1 = f32[8,2,512]{2,1,0:T(2,128)S(1)} all-gather(f32[1,2,512]{2,1,0:T(2,128)S(1)} %maximum_bitcast_fusion), channel_id=2, replica_groups=mesh['img'=4,'ref'=8] {'ref'}, dimensions={0}, use_global_device_ids=true | all-gather | bytes 36864 | tf_op jit(solution)/shard_map/all_gather | solution.py:82
  95.0 0.4 convert_reduce_fusion
  95.4 0.2 reshape.49
  95.6 1.2 copy.12
  96.7 14.5 %shard_map.50 = f32[4,24,2304]{2,1,0:T(8,128)} custom-call(bf16[864,512]{1,0:T(8,128)(2,1)} %bitcast.24, bf16[512,9216]{1,0:T(8,128)(2,1)} %all-gather.4.cloned.1.call-done.images_ref, s32[1,2304]{1,0:T(1,128)} %and_select_fusion.angle_ref), custom_call_target="tpu_custom_call" | custom-call | flops 8153726976 | bytes 11206656 | tf_op jit(solution)/shard_map/pallas_call | solution.py:44
  111.2 0.0 reduce-scatter.2.cloned.1.call-update
  111.3 0.1 reshape.51
  111.4 0.1 reduce_sum.39
  111.5 1.5 %collective-permute-start = (f32[24]{0:T(128)S(1)}, f32[24]{0:T(128)S(1)}, u32[]{:S(2)}, u32[]{:S(2)}) collective-permute-start(f32[24]{0:T(128)S(1)} %reduce_sum.39), channel_id=1, source_target_pairs={{0,8},{8,16},{16,24},{24,0},{1,9},{9,17},{17,25},{25,1},{2,10},{10... | collective-permute-start | bytes 296 | tf_op jit(solution)/shard_map/ppermute | solution.py:95
  113.0 2.4 %collective-permute-start.1 = (f32[24]{0:T(128)S(1)}, f32[24]{0:T(128)S(1)}, u32[]{:S(2)}, u32[]{:S(2)}) collective-permute-start(f32[24]{0:T(128)S(1)} %reduce_sum.39), channel_id=1, source_target_pairs={{0,16},{8,24},{16,0},{24,8},{1,17},{9,25},{17,1},{25,9},{2,18},{10... | collective-permute-start | bytes 296 | tf_op jit(solution)/shard_map/ppermute | solution.py:95
  115.4 1.4 %collective-permute-start.2 = (f32[24]{0:T(128)S(1)}, f32[24]{0:T(128)S(1)}, u32[]{:S(2)}, u32[]{:S(2)}) collective-permute-start(f32[24]{0:T(128)S(1)} %reduce_sum.39), channel_id=1, source_target_pairs={{0,24},{8,0},{16,8},{24,16},{1,25},{9,1},{17,9},{25,17},{2,26},{10... | collective-permute-start | bytes 296 | tf_op jit(solution)/shard_map/ppermute | solution.py:95
  116.8 0.0 collective-permute-done
  116.9 0.6 collective-permute-done.1
  117.4 1.5 %collective-permute-done.2 = f32[24]{0:T(128)S(1)} collective-permute-done((f32[24]{0:T(128)S(1)}, f32[24]{0:T(128)S(1)}, u32[]{:S(2)}, u32[]{:S(2)}) %collective-permute-start.2) | collective-permute-done | bytes 128 | tf_op jit(solution)/shard_map/ppermute | solution.py:95
  118.9 0.5 add_add_fusion
  119.5 16.6 %reduce-scatter.2.cloned.1.call-done = f32[1,24,2304]{2,1,0:T(8,128)} async-done(((f32[4,24,2304]{2,1,0:T(8,128)}), f32[1,24,2304]{2,1,0:T(8,128)}) %reduce-scatter.2.cloned.1.call-update) | async-done | bytes 221200 | tf_op jit(solution)/shard_map/reduce_scatter | solution.py:97
  (4 shorter events, 0.1 us)
Async XLA Ops:
  7.2 64.3 %all-gather.4.cloned.1.call-start = ((), (), s32[]{:S(2)}) async-start(), calls=%async_computation.1 | async-start | bytes 10616832 | tf_op jit(solution)/shard_map/all_gather | solution.py:75
  7.9 128.1 %reduce-scatter.2.cloned.1.call-start = ((), (), s32[]{:S(2)}) async-start(), calls=%async_computation.2 | async-start | bytes 1105920 | tf_op jit(solution)/shard_map/reduce_scatter | solution.py:97
  111.5 5.4 %collective-permute-start = (f32[24]{0:T(128)S(1)}, f32[24]{0:T(128)S(1)}, u32[]{:S(2)}, u32[]{:S(2)}) collective-permute-start(f32[24]{0:T(128)S(1)} %reduce_sum.39), channel_id=1, source_target_pairs={{0,8},{8,16},{16,24},{24,0},{1,9},{9,17},{17,25},{25,1},{2,10},{10... | collective-permute-start | bytes 296 | tf_op jit(solution)/shard_map/ppermute | solution.py:95
  113.0 4.4 %collective-permute-start.1 = (f32[24]{0:T(128)S(1)}, f32[24]{0:T(128)S(1)}, u32[]{:S(2)}, u32[]{:S(2)}) collective-permute-start(f32[24]{0:T(128)S(1)} %reduce_sum.39), channel_id=1, source_target_pairs={{0,16},{8,24},{16,0},{24,8},{1,17},{9,25},{17,1},{25,9},{2,18},{10... | collective-permute-start | bytes 296 | tf_op jit(solution)/shard_map/ppermute | solution.py:95
  115.4 3.5 %collective-permute-start.2 = (f32[24]{0:T(128)S(1)}, f32[24]{0:T(128)S(1)}, u32[]{:S(2)}, u32[]{:S(2)}) collective-permute-start(f32[24]{0:T(128)S(1)} %reduce_sum.39), channel_id=1, source_target_pairs={{0,24},{8,0},{16,8},{24,16},{1,25},{9,1},{17,9},{25,17},{2,26},{10... | collective-permute-start | bytes 296 | tf_op jit(solution)/shard_map/ppermute | solution.py:95
Sparse Core Ops, SparseCore 0:
  9.9 61.5 all-gather.3
  111.4 24.5 reduce-scatter.1

commit v7 on v6

--- a/solution.py
+++ b/solution.py
@@ -61,6 +61,47 @@
     )(by_turn, gathered, angle)
 
 
+def score_kernel(images_ref, references_ref, offsets_ref, out_ref, acc_ref):
+    step = pl.program_id(0)
+
+    @pl.when(step == 0)
+    def _():
+        acc_ref[...] = jnp.zeros_like(acc_ref)
+
+    acc_ref[...] += lax.dot_general(
+        images_ref[...], references_ref[...], (((1,), (1,)), ((), ())),
+        preferred_element_type=jnp.float32,
+    )
+
+    @pl.when(step == pl.num_programs(0) - 1)
+    def _():
+        out_ref[...] = acc_ref[...] + offsets_ref[...]
+
+
+def scores_of(gathered, references, offsets):
+    n, pixels = gathered.shape
+    local_refs = references.shape[0]
+    depth = GROUP_COLS if pixels % GROUP_COLS == 0 else pixels
+    return pl.pallas_call(
+        score_kernel,
+        grid=(pixels // depth,),
+        in_specs=[
+            pl.BlockSpec((n, depth), lambda k: (0, k)),
+            pl.BlockSpec((local_refs, depth), lambda k: (0, k)),
+            pl.BlockSpec((1, local_refs), lambda k: (0, 0)),
+        ],
+        out_specs=pl.BlockSpec((n, local_refs), lambda k: (0, 0)),
+        out_shape=jax.ShapeDtypeStruct((n, local_refs), jnp.float32),
+        scratch_shapes=[pltpu.VMEM((n, local_refs), jnp.float32)],
+        compiler_params=pltpu.CompilerParams(vmem_limit_bytes=60 * 1024 * 1024),
+        cost_estimate=pl.CostEstimate(
+            flops=2 * n * local_refs * pixels,
+            bytes_accessed=2 * n * pixels + 2 * local_refs * pixels + 4 * n * local_refs,
+            transcendentals=0,
+        ),
+    )(gathered, references, offsets.reshape(1, local_refs))
+
+
 def per_device(chunks, images, references, class_prior):
     local_refs, pixels = references.shape
     classes_here = class_prior.shape[0]
@@ -73,10 +114,7 @@
         local_refs
     )
     gathered = lax.all_gather(images, "ref", axis=0, tiled=True)
-    products = lax.dot_general(
-        gathered, references, (((1,), (1,)), ((), ())), preferred_element_type=jnp.float32
-    )
-    scores = products + offsets
+    scores = scores_of(gathered, references, offsets)
     local_max = jnp.max(scores, axis=1)
     local_sum = jnp.sum(jnp.exp(scores - local_max[:, None]), axis=1)
     stats = lax.all_gather(jnp.stack([local_max, local_sum]), "ref", axis=0)

time: 143 us -> 151 us (1.056)
  Pallas kernels: 14.5 us -> 31.4 us
  matrix products: 14.1 us -> 0 us
  local copies, waits for them, and re-layouts: 2.24 us -> 5.46 us
  other arithmetic: 9.05 us -> 11.1 us
    pallas_call x0 -> x1, Pallas kernels: none -> 16.9 us  [scores_of(): pl.pallas_call(score_kernel, grid=(pixels // depth,), in_specs=[pl.BlockS...]
    dot_general x1 -> x0, matrix products: 14.1 us -> none  [per_device(): lax.dot_general(gathered, references, (((1,), (1,)), ((), ())), preferred...]
    reduce_max x0 -> x1, other arithmetic: none -> 1.8 us  [per_device(): local_max = jnp.max(scores, axis=1)]
  transfers between devices with their start and end apart: 5 -> 5, of which waited for: 4 -> 4; matrix products, arithmetic and copies ran while one was open for 6% -> 7% of each run, Pallas kernels for 0% -> 0%
where the time goes in v7:
time: 151 us; the launch traced here: 150 us
  waiting for transfers between devices  73.8 us (49%)
  Pallas kernels  31.4 us (21%)
  between operations  14.1 us (9%)
  other arithmetic  11.1 us (7%)
  blocking collectives  9.02 us (6%)
  local copies, waits for them, and re-layouts  5.46 us (4%)
  starting transfers between devices  5.45 us (4%)
    all_gather x1, waiting for transfers between devices, per_device(): gathered = lax.all_gather(images, 'ref', axis=0, tiled=True)  54.4 us
    pallas_call x1, Pallas kernels, scores_of(): pl.pallas_call(score_kernel, grid=(pixels // depth,), in_specs=[pl.BlockS...  16.9 us
    reduce_scatter x1, waiting for transfers between devices, per_device(): lax.psum_scatter(chunked, 'img', scatter_dimension=0, tiled=True)  16.6 us
    pallas_call x1, Pallas kernels, turn_and_sum(): pl.pallas_call(functools.partial(turn_sum_kernel, classes_here, rotations...  14.5 us
    all_gather x1, blocking collectives, per_device(): stats = lax.all_gather(jnp.stack([local_max, local_sum]), 'ref', axis=0)  9.02 us
    dot_general x1, other arithmetic, per_device(): jnp.einsum('jp,jp->j', references, references, preferred_element_type=jnp...  7 us
    ppermute x3, starting transfers between devices, per_device(): class_weights = class_weights + lax.ppermute(local_mass, 'img', perm)  5.38 us
  transfers between devices with their start and end apart: 5, of which 4 were waited for; matrix products, arithmetic and copies ran while one was open for 7% of the time, Pallas kernels for 0%

profile of v7, /device:TPU:0, one launch (start us, length us, event | category | flops | bytes accessed | tf_op | source)
XLA Modules:
  0.0 150.3 jit_solution(15956827098489971659)
XLA Ops:
  7.2 0.0 all-gather.4.cloned.1.call-start
  7.2 0.7 all-gather.4.cloned.1.call-update
  7.9 0.0 reduce-scatter.2.cloned.1.call-start
  7.9 0.7 log.3
  8.6 0.1 sub.38
  8.7 0.1 sub.39
  8.8 7.0 %fusion = f32[864]{0:T(1024)S(1)} fusion(bf16[864,9216]{1,0:T(8,128)(2,1)} %references_ref.1), kind=kLoop, calls=%fused_computation.1 | loop fusion | flops 23887008 | bytes 15928704 | tf_op jit(solution)/shard_map/jp,jp->j/dot_general | solution.py:110
  15.8 0.6 sub.41.offsets_ref
  16.4 0.6 and_select_fusion.angle_ref
  17.0 54.4 %all-gather.4.cloned.1.call-done.images_ref = bf16[512,9216]{1,0:T(8,128)(2,1)} async-done(((bf16[64,9216]{1,0:T(8,128)(2,1)}), bf16[512,9216]{1,0:T(8,128)(2,1)}) %all-gather.4.cloned.1.call-update) | async-done | bytes 9437200 | tf_op jit(solution)/shard_map/all_gather | solution.py:116
  71.4 16.9 %shard_map.50 = f32[512,864]{1,0:T(8,128)} custom-call(bf16[512,9216]{1,0:T(8,128)(2,1)} %all-gather.4.cloned.1.call-done.images_ref, bf16[864,9216]{1,0:T(8,128)(2,1)} %references_ref.1, f32[1,864]{1,0:T(1,128)} %sub.41.offsets_ref), custom_call_target="tpu_custom_call" | custom-call | flops 8153726976 | bytes 27131904 | tf_op jit(solution)/shard_map/pallas_call | solution.py:85
  88.3 0.0 copy-start
  88.3 1.8 %reduce_max.18 = f32[512]{0:T(512)S(1)} reduce(f32[512,864]{1,0:T(8,128)} %shard_map.50, f32[]{:T(128)} %constant.14.clone.1), dimensions={1}, to_apply=%region_0.0 | reduce | flops 441856 | bytes 1771524 | tf_op jit(solution)/shard_map/reduce_max | solution.py:118
  90.1 0.2 copy-done
  90.4 0.5 exponential_reduce_fusion
  90.9 9.0 %all-gather.1 = f32[8,2,512]{2,1,0:T(2,128)S(1)} all-gather(f32[1,2,512]{2,1,0:T(2,128)S(1)} %maximum_bitcast_fusion), channel_id=2, replica_groups=mesh['img'=4,'ref'=8] {'ref'}, dimensions={0}, use_global_device_ids=true | all-gather | bytes 36864 | tf_op jit(solution)/shard_map/all_gather | solution.py:120
  100.0 0.5 convert_reduce_fusion
  100.5 1.3 copy.14
  101.8 1.2 reshape.48
  103.0 1.2 copy.15
  104.2 14.5 %shard_map.51 = f32[4,24,2304]{2,1,0:T(8,128)} custom-call(bf16[864,512]{1,0:T(8,128)(2,1)} %bitcast.22, bf16[512,9216]{1,0:T(8,128)(2,1)} %all-gather.4.cloned.1.call-done.images_ref, s32[1,2304]{1,0:T(1,128)} %and_select_fusion.angle_ref), custom_call_target="tpu_custom_call" | custom-call | flops 8153726976 | bytes 11206656 | tf_op jit(solution)/shard_map/pallas_call | solution.py:44
  118.7 0.0 reduce-scatter.2.cloned.1.call-update
  118.7 0.1 reshape.50
  118.8 0.1 reduce_sum.39
  118.9 1.5 %collective-permute-start = (f32[24]{0:T(128)S(1)}, f32[24]{0:T(128)S(1)}, u32[]{:S(2)}, u32[]{:S(2)}) collective-permute-start(f32[24]{0:T(128)S(1)} %reduce_sum.39), channel_id=1, source_target_pairs={{0,8},{8,16},{16,24},{24,0},{1,9},{9,17},{17,25},{25,1},{2,10},{10... | collective-permute-start | bytes 296 | tf_op jit(solution)/shard_map/ppermute | solution.py:133
  120.5 2.4 %collective-permute-start.1 = (f32[24]{0:T(128)S(1)}, f32[24]{0:T(128)S(1)}, u32[]{:S(2)}, u32[]{:S(2)}) collective-permute-start(f32[24]{0:T(128)S(1)} %reduce_sum.39), channel_id=1, source_target_pairs={{0,16},{8,24},{16,0},{24,8},{1,17},{9,25},{17,1},{25,9},{2,18},{10... | collective-permute-start | bytes 296 | tf_op jit(solution)/shard_map/ppermute | solution.py:133
  122.9 1.4 collective-permute-start.2
  124.3 0.0 collective-permute-done
  124.3 0.6 collective-permute-done.1
  124.9 1.5 %collective-permute-done.2 = f32[24]{0:T(128)S(1)} collective-permute-done((f32[24]{0:T(128)S(1)}, f32[24]{0:T(128)S(1)}, u32[]{:S(2)}, u32[]{:S(2)}) %collective-permute-start.2) | collective-permute-done | bytes 128 | tf_op jit(solution)/shard_map/ppermute | solution.py:133
  126.4 0.5 add_add_fusion
  126.9 16.6 %reduce-scatter.2.cloned.1.call-done = f32[1,24,2304]{2,1,0:T(8,128)} async-done(((f32[4,24,2304]{2,1,0:T(8,128)}), f32[1,24,2304]{2,1,0:T(8,128)}) %reduce-scatter.2.cloned.1.call-update) | async-done | bytes 221200 | tf_op jit(solution)/shard_map/reduce_scatter | solution.py:135
  (4 shorter events, 0.1 us)
Async XLA Ops:
  7.2 64.3 %all-gather.4.cloned.1.call-start = ((), (), s32[]{:S(2)}) async-start(), calls=%async_computation.1 | async-start | bytes 10616832 | tf_op jit(solution)/shard_map/all_gather | solution.py:116
  7.9 135.6 %reduce-scatter.2.cloned.1.call-start = ((), (), s32[]{:S(2)}) async-start(), calls=%async_computation.2 | async-start | bytes 1105920 | tf_op jit(solution)/shard_map/reduce_scatter | solution.py:135
  88.3 2.1 %copy-start = (f32[512,864]{1,0:T(8,128)S(1)}, f32[512,864]{1,0:T(8,128)}, u32[]{:S(2)}) copy-start(f32[512,864]{1,0:T(8,128)} %shard_map.50) | copy-start | bytes 5308420
  118.9 5.4 %collective-permute-start = (f32[24]{0:T(128)S(1)}, f32[24]{0:T(128)S(1)}, u32[]{:S(2)}, u32[]{:S(2)}) collective-permute-start(f32[24]{0:T(128)S(1)} %reduce_sum.39), channel_id=1, source_target_pairs={{0,8},{8,16},{16,24},{24,0},{1,9},{9,17},{17,25},{25,1},{2,10},{10... | collective-permute-start | bytes 296 | tf_op jit(solution)/shard_map/ppermute | solution.py:133
  120.5 4.4 %collective-permute-start.1 = (f32[24]{0:T(128)S(1)}, f32[24]{0:T(128)S(1)}, u32[]{:S(2)}, u32[]{:S(2)}) collective-permute-start(f32[24]{0:T(128)S(1)} %reduce_sum.39), channel_id=1, source_target_pairs={{0,16},{8,24},{16,0},{24,8},{1,17},{9,25},{17,1},{25,9},{2,18},{10... | collective-permute-start | bytes 296 | tf_op jit(solution)/shard_map/ppermute | solution.py:133
  122.9 3.5 %collective-permute-start.2 = (f32[24]{0:T(128)S(1)}, f32[24]{0:T(128)S(1)}, u32[]{:S(2)}, u32[]{:S(2)}) collective-permute-start(f32[24]{0:T(128)S(1)} %reduce_sum.39), channel_id=1, source_target_pairs={{0,24},{8,0},{16,8},{24,16},{1,25},{9,1},{17,9},{25,17},{2,26},{10... | collective-permute-start | bytes 296 | tf_op jit(solution)/shard_map/ppermute | solution.py:133
Sparse Core Ops, SparseCore 0:
  9.9 61.5 all-gather.3
  118.8 24.5 reduce-scatter.1

commit v8 on v6

--- a/solution.py
+++ b/solution.py
@@ -1,6 +1,7 @@
 import functools
 
 import jax
+import numpy as np
 import jax.numpy as jnp
 from jax import lax
 from jax.experimental import pallas as pl
@@ -61,7 +62,54 @@
     )(by_turn, gathered, angle)
 
 
-def per_device(chunks, images, references, class_prior):
+def ring_order(chips):
+    if chips == 4:
+        return [0, 1, 3, 2]
+    order = []
+    for row in range(chips // 2):
+        order += [2 * row, 2 * row + 1] if row % 2 == 0 else [2 * row + 1, 2 * row]
+    return order
+
+
+def ring_gather(images, n_ref):
+    chips = n_ref // 2
+    block = images.shape[0]
+    ring = ring_order(chips)
+    place = {chip: i for i, chip in enumerate(ring)}
+
+    def ahead(chip, hops):
+        return ring[(place[chip] + hops) % chips]
+
+    to_next = [(2 * c + k, 2 * ahead(c, 1) + k) for c in range(chips) for k in range(2)]
+    to_prev = [(2 * c + k, 2 * ahead(c, -1) + k) for c in range(chips) for k in range(2)]
+    to_partner = [(d, d ^ 1) for d in range(n_ref)]
+    pieces = [(images, 0, 0, block)]
+    from_prev = images
+    from_next = images
+    for hops in range(1, (chips + 1) // 2):
+        from_prev = lax.ppermute(from_prev, "ref", to_next)
+        from_next = lax.ppermute(from_next, "ref", to_prev)
+        pieces += [(from_prev, -hops, 0, block), (from_next, hops, 0, block)]
+    if chips % 2 == 0:
+        half = block // 2
+        top = lax.ppermute(from_prev[:half], "ref", to_next)
+        bottom = lax.ppermute(from_next[half:], "ref", to_prev)
+        pieces += [(top, chips // 2, 0, half), (bottom, chips // 2, half, block - half)]
+    arrays = [piece[0] for piece in pieces]
+    arrays += [lax.ppermute(piece[0], "ref", to_partner) for piece in pieces]
+    table = []
+    for device in range(n_ref):
+        chip, core = device // 2, device % 2
+        rows = []
+        for side in (core, 1 - core):
+            for _, hops, first, count in pieces:
+                origin = 2 * ahead(chip, hops) + side
+                rows += list(range(origin * block + first, origin * block + first + count))
+        table.append(rows)
+    return jnp.concatenate(arrays, axis=0), np.array(table, np.int32)
+
+
+def per_device(chunks, n_ref, images, references, class_prior):
     local_refs, pixels = references.shape
     classes_here = class_prior.shape[0]
     rotations = local_refs // classes_here
@@ -72,16 +120,21 @@
     offsets = (jnp.log(class_prior)[:, None] - half_norm.reshape(classes_here, rotations)).reshape(
         local_refs
     )
-    gathered = lax.all_gather(images, "ref", axis=0, tiled=True)
+    gathered, table = ring_gather(images, n_ref)
+    to_group = jnp.asarray(table)[lax.axis_index("ref")]
+    from_group = jnp.asarray(np.argsort(table, axis=1).astype(np.int32))[lax.axis_index("ref")]
     products = lax.dot_general(
         gathered, references, (((1,), (1,)), ((), ())), preferred_element_type=jnp.float32
     )
     scores = products + offsets
     local_max = jnp.max(scores, axis=1)
     local_sum = jnp.sum(jnp.exp(scores - local_max[:, None]), axis=1)
-    stats = lax.all_gather(jnp.stack([local_max, local_sum]), "ref", axis=0)
+    in_group_order = jnp.take(jnp.stack([local_max, local_sum]), from_group, axis=1)
+    stats = lax.all_gather(in_group_order, "ref", axis=0)
     top_score = jnp.max(stats[:, 0], axis=0)
     denominator = jnp.sum(stats[:, 1] * jnp.exp(stats[:, 0] - top_score[None, :]), axis=0)
+    norm = jnp.take(jnp.stack([top_score, denominator]), to_group, axis=1)
+    top_score, denominator = norm[0], norm[1]
     weights = (jnp.exp(scores - top_score[:, None]) / denominator[:, None]).astype(jnp.bfloat16)
 
     n = weights.shape[0]
@@ -100,7 +153,7 @@
 def solution(mesh):
     placed = (P(("img", "ref"), None), P("ref", None), P("ref"))
     return jax.shard_map(
-        functools.partial(per_device, mesh.shape["img"]),
+        functools.partial(per_device, mesh.shape["img"], mesh.shape["ref"]),
         mesh=mesh,
         in_specs=placed,
         out_specs=(P("ref", "img"), P("ref")),

time: 143 us -> 132 us (0.923)
  waiting for transfers between devices: 74.4 us -> 41.6 us
  local copies, waits for them, and re-layouts: 2.24 us -> 17.5 us
  starting transfers between devices: 5.45 us -> 10.6 us
  other arithmetic: 9.05 us -> 13.1 us
  matrix products: 14.1 us -> 11.6 us
    all_gather x1 -> x0, waiting for transfers between devices: 55 us -> none  [per_device(): gathered = lax.all_gather(images, 'ref', axis=0, tiled=True)]
    ppermute x0 -> x9, waiting for transfers between devices: none -> 21.9 us  [the longest x1 11.9 us: ring_gather(): from_prev = lax.ppermute(from_prev, 'ref', to_next)]
    unnamed x0 -> x28, local copies, waits for them, and re-layouts: none -> 10.9 us
    ppermute x0 -> x9, starting transfers between devices: none -> 5.9 us  [the longest x1 2.99 us: ring_gather(): from_prev = lax.ppermute(from_prev, 'ref', to_next)]
    ppermute x3, waiting for transfers between devices: 2.1 us -> 4.66 us  [per_device(): class_weights = class_weights + lax.ppermute(local_mass, 'img', perm)]
    dot_general x1, matrix products: 14.1 us -> 11.6 us  [per_device(): lax.dot_general(gathered, references, (((1,), (1,)), ((), ())), preferred...]
    gather x0 -> x2, local copies, waits for them, and re-layouts: none -> 2.07 us  [the longest x1 1.04 us: per_device(): jnp.take(jnp.stack([local_max, local_sum]), from_group, axis=1)]
    dot_general x1, other arithmetic: 7 us -> 8.61 us  [per_device(): jnp.einsum('jp,jp->j', references, references, preferred_element_type=jnp...]
  transfers between devices with their start and end apart: 5 -> 13, of which waited for: 4 -> 6; matrix products, arithmetic and copies ran while one was open for 6% -> 19% of each run, Pallas kernels for 0% -> 0%
where the time goes in v8:
time: 132 us
  waiting for transfers between devices  41.6 us (32%)
  local copies, waits for them, and re-layouts  17.5 us (13%)
  Pallas kernels  14.5 us (11%)
  between operations  14.3 us (11%)
  other arithmetic  13.1 us (10%)
  matrix products  11.6 us (9%)
  starting transfers between devices  10.6 us (8%)
  blocking collectives  8.98 us (7%)
    reduce_scatter x1, waiting for transfers between devices, per_device(): lax.psum_scatter(chunked, 'img', scatter_dimension=0, tiled=True)  15 us
    pallas_call x1, Pallas kernels, turn_and_sum(): pl.pallas_call(functools.partial(turn_sum_kernel, classes_here, rotations...  14.5 us
    ppermute x1, waiting for transfers between devices, ring_gather(): from_prev = lax.ppermute(from_prev, 'ref', to_next)  11.9 us
    dot_general x1, matrix products, per_device(): lax.dot_general(gathered, references, (((1,), (1,)), ((), ())), preferred...  11.6 us
    unnamed x28, local copies, waits for them, and re-layouts  10.9 us
    ppermute x1, waiting for transfers between devices, ring_gather(): top = lax.ppermute(from_prev[:half], 'ref', to_next)  9.65 us
    all_gather x1, blocking collectives, per_device(): stats = lax.all_gather(in_group_order, 'ref', axis=0)  8.98 us
    dot_general x1, other arithmetic, per_device(): jnp.einsum('jp,jp->j', references, references, preferred_element_type=jnp...  8.61 us
  transfers between devices with their start and end apart: 13, of which 6 were waited for; matrix products, arithmetic and copies ran while one was open for 19% of the time, Pallas kernels for 0%

profile of v8, /device:TPU:0, one launch (start us, length us, event | category | flops | bytes accessed | tf_op | source)
XLA Modules:
  0.0 132.2 jit_solution(11764308394468254812)
XLA Ops:
  7.2 3.0 %collective-permute-start = (bf16[64,9216]{1,0:T(8,128)(2,1)}, bf16[64,9216]{1,0:T(8,128)(2,1)S(1)}, u32[]{:S(2)}, u32[]{:S(2)}) collective-permute-start(bf16[64,9216]{1,0:T(8,128)(2,1)} %param.7), channel_id=1, source_target_pairs={{0,2},{1,3},{2,6},{3,7},{4,0},{5,1},{6,4},{7,5},{8,10},{9,11},{10,... | collective-permute-start | bytes 3538952 | tf_op jit(solution)/shard_map/ppermute | solution.py:90
  10.3 0.7 constant_dynamic-slice_fusion
  11.0 0.6 compare_select_fusion.1
  12.1 0.6 compare_select_fusion
  13.2 0.6 and_select_fusion.angle_ref
  13.8 0.7 log.3
  14.7 8.6 %fusion = f32[864]{0:T(1024)S(1)} fusion(bf16[864,9216]{1,0:T(8,128)(2,1)} %param.8), kind=kLoop, calls=%fused_computation.3 | loop fusion | flops 23887008 | bytes 15928704 | tf_op jit(solution)/shard_map/jp,jp->j/dot_general | solution.py:117
  23.4 1.1 constant_dynamic-update-slice_fusion.9
  24.5 11.9 %collective-permute-done = bf16[64,9216]{1,0:T(8,128)(2,1)S(1)} collective-permute-done((bf16[64,9216]{1,0:T(8,128)(2,1)}, bf16[64,9216]{1,0:T(8,128)(2,1)S(1)}, u32[]{:S(2)}, u32[]{:S(2)}) %collective-permute-start) | collective-permute-done | bytes 1179680 | tf_op jit(solution)/shard_map/ppermute | solution.py:90
  36.5 1.8 %collective-permute-start.2 = (bf16[32,9216]{1,0:T(8,128)(2,1)S(1)}, bf16[32,9216]{1,0:T(8,128)(2,1)S(1)}, u32[]{:S(2)}, u32[]{:S(2)}) collective-permute-start(bf16[32,9216]{1,0:T(8,128)(2,1)S(1)} %slice.29), channel_id=1, source_target_pairs={{0,2},{1,3},{2,6},{3,7},{4,0},{5,1},{6,4},{7,5},{8,10},{9,11},{10,... | collective-permute-start | bytes 1769480 | tf_op jit(solution)/shard_map/ppermute | solution.py:95
  39.1 1.1 constant_dynamic-update-slice_fusion.8
  40.3 1.1 constant_dynamic-update-slice_fusion.7
  41.4 9.7 %collective-permute-done.2 = bf16[32,9216]{1,0:T(8,128)(2,1)S(1)} collective-permute-done((bf16[32,9216]{1,0:T(8,128)(2,1)S(1)}, bf16[32,9216]{1,0:T(8,128)(2,1)S(1)}, u32[]{:S(2)}, u32[]{:S(2)}) %collective-permute-start.2) | collective-permute-done | bytes 589856 | tf_op jit(solution)/shard_map/ppermute | solution.py:95
  51.0 0.9 constant_dynamic-update-slice_fusion.6
  52.4 0.9 constant_dynamic-update-slice_fusion.5
  53.3 2.5 %constant_dynamic-update-slice_fusion.4 = bf16[512,9216]{1,0:T(8,128)(2,1)} fusion(bf16[512,9216]{1,0:T(8,128)(2,1)} %constant_dynamic-update-slice_fusion.5, bf16[64,9216]{1,0:T(8,128)(2,1)} %collective-permute-done.4), kind=kLoop, calls=%fused_computation.17 | loop fusion | bytes 2359296
  55.8 1.1 constant_dynamic-update-slice_fusion.3
  56.9 1.1 constant_dynamic-update-slice_fusion.2
  58.0 0.9 constant_dynamic-update-slice_fusion.1
  59.0 0.9 constant_dynamic-update-slice_fusion.images_ref
  59.9 11.6 %fusion.5 = (f32[512]{0:T(512)S(1)}, f32[512,864]{0,1:T(8,128)S(1)}) fusion(f32[864]{0:T(1024)S(1)} %multiply_subtract_fusion, bf16[512,9216]{1,0:T(8,128)(2,1)} %constant_dynamic-update-slice_fusion.images_ref, bf16[864,9216]{1,0:T(8,128)(2,1)S(1)} %bitcast.34), kind=kOutput, calls=%fused_computation.42 | convolution fusion | flops 8154611200 | bytes 27137408 | tf_op jit(solution)/shard_map/dot_general | solution.py:126
  72.0 1.0 gather_fusion
  73.3 9.0 %all-gather.1 = f32[8,2,512]{2,1,0:T(2,128)S(1)} all-gather(f32[1,2,512]{2,1,0:T(2,128)S(1)} %copy.26), channel_id=2, replica_groups=mesh['img'=4,'ref'=8] {'ref'}, dimensions={0}, use_global_device_ids=true | all-gather | bytes 36864 | tf_op jit(solution)/shard_map/all_gather | solution.py:133
  82.5 1.0 gather_fusion.1
  84.6 1.2 copy.30
  85.8 14.5 %shard_map.68 = f32[4,24,2304]{2,1,0:T(8,128)} custom-call(bf16[864,512]{1,0:T(8,128)(2,1)} %bitcast.36, bf16[512,9216]{1,0:T(8,128)(2,1)} %constant_dynamic-update-slice_fusion.images_ref, s32[1,2304]{1,0:T(1,128)} %and_select_fusion.angle_ref), custom_call_target="tpu_custom_call" | custom-call | flops 8153726976 | bytes 11206656 | tf_op jit(solution)/shard_map/pallas_call | solution.py:45
  100.5 2.6 %collective-permute-start.10 = (f32[24]{0:T(128)S(1)}, f32[24]{0:T(128)S(1)}, u32[]{:S(2)}, u32[]{:S(2)}) collective-permute-start(f32[24]{0:T(128)S(1)} %reduce_sum.39), channel_id=1, source_target_pairs={{0,16},{8,24},{16,0},{24,8},{1,17},{9,25},{17,1},{25,9},{2,18},{10... | collective-permute-start | bytes 296 | tf_op jit(solution)/shard_map/ppermute | solution.py:148
  103.2 1.3 %collective-permute-start.11 = (f32[24]{0:T(128)S(1)}, f32[24]{0:T(128)S(1)}, u32[]{:S(2)}, u32[]{:S(2)}) collective-permute-start(f32[24]{0:T(128)S(1)} %reduce_sum.39), channel_id=1, source_target_pairs={{0,24},{8,0},{16,8},{24,16},{1,25},{9,1},{17,9},{25,17},{2,26},{10... | collective-permute-start | bytes 296 | tf_op jit(solution)/shard_map/ppermute | solution.py:148
  104.5 0.7 collective-permute-start.9
  105.2 1.5 %collective-permute-done.11 = f32[24]{0:T(128)S(1)} collective-permute-done((f32[24]{0:T(128)S(1)}, f32[24]{0:T(128)S(1)}, u32[]{:S(2)}, u32[]{:S(2)}) %collective-permute-start.11) | collective-permute-done | bytes 128 | tf_op jit(solution)/shard_map/ppermute | solution.py:148
  106.7 3.1 %collective-permute-done.9 = f32[24]{0:T(128)S(1)} collective-permute-done((f32[24]{0:T(128)S(1)}, f32[24]{0:T(128)S(1)}, u32[]{:S(2)}, u32[]{:S(2)}) %collective-permute-start.9) | collective-permute-done | bytes 128 | tf_op jit(solution)/shard_map/ppermute | solution.py:148
  110.4 15.0 %reduce-scatter.2.cloned.1.call-done = f32[1,24,2304]{2,1,0:T(8,128)} async-done(((f32[4,24,2304]{2,1,0:T(8,128)}), f32[1,24,2304]{2,1,0:T(8,128)}) %reduce-scatter.2.cloned.1.call-update) | async-done | bytes 221200 | tf_op jit(solution)/shard_map/reduce_scatter | solution.py:150
  (61 shorter events, 5.5 us)
Async XLA Ops:
  7.2 16.2 %copy-start = (bf16[64,9216]{1,0:T(8,128)(2,1)S(1)}, bf16[64,9216]{1,0:T(8,128)(2,1)}, u32[]{:S(2)}) copy-start(bf16[64,9216]{1,0:T(8,128)(2,1)} %param.7) | copy-start | bytes 3538948
  7.2 118.2 %reduce-scatter.2.cloned.1.call-start = ((), (), s32[]{:S(2)}) async-start(), calls=%async_computation.1 | async-start | bytes 1105920 | tf_op jit(solution)/shard_map/reduce_scatter | solution.py:150
  7.2 29.2 %collective-permute-start = (bf16[64,9216]{1,0:T(8,128)(2,1)}, bf16[64,9216]{1,0:T(8,128)(2,1)S(1)}, u32[]{:S(2)}, u32[]{:S(2)}) collective-permute-start(bf16[64,9216]{1,0:T(8,128)(2,1)} %param.7), channel_id=1, source_target_pairs={{0,2},{1,3},{2,6},{3,7},{4,0},{5,1},{6,4},{7,5},{8,10},{9,11},{10,... | collective-permute-start | bytes 3538952 | tf_op jit(solution)/shard_map/ppermute | solution.py:90
  10.2 28.0 %collective-permute-start.1 = (bf16[64,9216]{1,0:T(8,128)(2,1)}, bf16[64,9216]{1,0:T(8,128)(2,1)S(1)}, u32[]{:S(2)}, u32[]{:S(2)}) collective-permute-start(bf16[64,9216]{1,0:T(8,128)(2,1)} %param.7), channel_id=1, source_target_pairs={{0,4},{1,5},{2,0},{3,1},{4,6},{5,7},{6,2},{7,3},{8,12},{9,13},{10,... | collective-permute-start | bytes 3538952 | tf_op jit(solution)/shard_map/ppermute | solution.py:91
  10.3 43.0 %collective-permute-start.4 = (bf16[64,9216]{1,0:T(8,128)(2,1)}, bf16[64,9216]{1,0:T(8,128)(2,1)}, u32[]{:S(2)}, u32[]{:S(2)}) collective-permute-start(bf16[64,9216]{1,0:T(8,128)(2,1)} %param.7), channel_id=1, source_target_pairs={{0,1},{1,0},{2,3},{3,2},{4,5},{5,4},{6,7},{7,6},{8,9},{9,8},{10,11... | collective-permute-start | bytes 3538952 | tf_op jit(solution)/shard_map/ppermute | solution.py:99
  14.7 8.7 %copy-start.1 = (s32[512]{0:T(512)S(1)}, s32[512]{0:T(512)}, u32[]{:S(2)}) copy-start(s32[512]{0:T(512)} %compare_select_fusion.1) | copy-start | bytes 6148
  14.7 8.7 %copy-start.2 = (s32[512]{0:T(512)S(1)}, s32[512]{0:T(512)}, u32[]{:S(2)}) copy-start(s32[512]{0:T(512)} %compare_select_fusion) | copy-start | bytes 6148
  14.7 45.2 %slice-start = ((s8[15925248]{0:T(1024)(128)(4,1)}), s8[4194304]{0:T(1024)(128)(4,1)S(1)}, s32[]{:S(2)}) async-start(s8[15925248]{0:T(1024)(128)(4,1)} %bitcast.33), calls=%async_computation.2 | async-start | bytes 8388608
  14.7 45.2 %slice-start.1 = ((s8[15925248]{0:T(1024)(128)(4,1)}), s8[4194304]{0:T(1024)(128)(4,1)S(1)}, s32[]{:S(2)}) async-start(s8[15925248]{0:T(1024)(128)(4,1)} %bitcast.33), calls=%async_computation.3 | async-start | bytes 8388608
  24.5 35.4 %slice-start.2 = ((s8[15925248]{0:T(1024)(128)(4,1)}), s8[4194304]{0:T(1024)(128)(4,1)S(1)}, s32[]{:S(2)}) async-start(s8[15925248]{0:T(1024)(128)(4,1)} %bitcast.33), calls=%async_computation.4 | async-start | bytes 8388608
  36.5 14.6 %collective-permute-start.2 = (bf16[32,9216]{1,0:T(8,128)(2,1)S(1)}, bf16[32,9216]{1,0:T(8,128)(2,1)S(1)}, u32[]{:S(2)}, u32[]{:S(2)}) collective-permute-start(bf16[32,9216]{1,0:T(8,128)(2,1)S(1)} %slice.29), channel_id=1, source_target_pairs={{0,2},{1,3},{2,6},{3,7},{4,0},{5,1},{6,4},{7,5},{8,10},{9,11},{10,... | collective-permute-start | bytes 1769480 | tf_op jit(solution)/shard_map/ppermute | solution.py:95
  38.3 14.0 %collective-permute-start.3 = (bf16[32,9216]{1,0:T(8,128)(2,1)S(1)}, bf16[32,9216]{1,0:T(8,128)(2,1)S(1)}, u32[]{:S(2)}, u32[]{:S(2)}) collective-permute-start(bf16[32,9216]{1,0:T(8,128)(2,1)S(1)} %slice.30), channel_id=1, source_target_pairs={{0,4},{1,5},{2,0},{3,1},{4,6},{5,7},{6,2},{7,3},{8,12},{9,13},{10,... | collective-permute-start | bytes 1769480 | tf_op jit(solution)/shard_map/ppermute | solution.py:96
  38.6 17.2 %collective-permute-start.5 = (bf16[64,9216]{1,0:T(8,128)(2,1)S(1)}, bf16[64,9216]{1,0:T(8,128)(2,1)S(1)}, u32[]{:S(2)}, u32[]{:S(2)}) collective-permute-start(bf16[64,9216]{1,0:T(8,128)(2,1)S(1)} %collective-permute-done), channel_id=1, source_target_pairs={{0,1},{1,0},{2,3},{3,2},{4,5},{5,4},{6,7},{7,6},{8,9},{9,8},{10,11... | collective-permute-start | bytes 3538952 | tf_op jit(solution)/shard_map/ppermute | solution.py:99
  38.6 18.3 %collective-permute-start.6 = (bf16[64,9216]{1,0:T(8,128)(2,1)S(1)}, bf16[64,9216]{1,0:T(8,128)(2,1)S(1)}, u32[]{:S(2)}, u32[]{:S(2)}) collective-permute-start(bf16[64,9216]{1,0:T(8,128)(2,1)S(1)} %collective-permute-done.1), channel_id=1, source_target_pairs={{0,1},{1,0},{2,3},{3,2},{4,5},{5,4},{6,7},{7,6},{8,9},{9,8},{10,11... | collective-permute-start | bytes 3538952 | tf_op jit(solution)/shard_map/ppermute | solution.py:99
  51.0 7.0 %collective-permute-start.7 = (bf16[32,9216]{1,0:T(8,128)(2,1)S(1)}, bf16[32,9216]{1,0:T(8,128)(2,1)S(1)}, u32[]{:S(2)}, u32[]{:S(2)}) collective-permute-start(bf16[32,9216]{1,0:T(8,128)(2,1)S(1)} %collective-permute-done.2), channel_id=1, source_target_pairs={{0,1},{1,0},{2,3},{3,2},{4,5},{5,4},{6,7},{7,6},{8,9},{9,8},{10,11... | collective-permute-start | bytes 1769480 | tf_op jit(solution)/shard_map/ppermute | solution.py:99
  52.2 6.7 %collective-permute-start.8 = (bf16[32,9216]{1,0:T(8,128)(2,1)S(1)}, bf16[32,9216]{1,0:T(8,128)(2,1)S(1)}, u32[]{:S(2)}, u32[]{:S(2)}) collective-permute-start(bf16[32,9216]{1,0:T(8,128)(2,1)S(1)} %collective-permute-done.3), channel_id=1, source_target_pairs={{0,1},{1,0},{2,3},{3,2},{4,5},{5,4},{6,7},{7,6},{8,9},{9,8},{10,11... | collective-permute-start | bytes 1769480 | tf_op jit(solution)/shard_map/ppermute | solution.py:99
  53.3 6.6 %slice-start.3 = ((s8[15925248]{0:T(1024)(128)(4,1)}), s8[3342336]{0:T(1024)(128)(4,1)S(1)}, s32[]{:S(2)}) async-start(s8[15925248]{0:T(1024)(128)(4,1)} %bitcast.33), calls=%async_computation.5 | async-start | bytes 6684672
  59.9 13.2 %copy-start.4 = (pred[512]{0:T(512)(128)(4,1)S(1)}, pred[512]{0:T(512)(128)(4,1)}, u32[]{:S(2)}) copy-start(pred[512]{0:T(512)(128)(4,1)} %compare_and_fusion.1) | copy-start | bytes 1540
  59.9 23.7 %copy-start.3 = (pred[512]{0:T(512)(128)(4,1)S(1)}, pred[512]{0:T(512)(128)(4,1)}, u32[]{:S(2)}) copy-start(pred[512]{0:T(512)(128)(4,1)} %compare_and_fusion) | copy-start | bytes 1540
  100.5 4.7 %collective-permute-start.10 = (f32[24]{0:T(128)S(1)}, f32[24]{0:T(128)S(1)}, u32[]{:S(2)}, u32[]{:S(2)}) collective-permute-start(f32[24]{0:T(128)S(1)} %reduce_sum.39), channel_id=1, source_target_pairs={{0,16},{8,24},{16,0},{24,8},{1,17},{9,25},{17,1},{25,9},{2,18},{10... | collective-permute-start | bytes 296 | tf_op jit(solution)/shard_map/ppermute | solution.py:148
  103.2 3.5 %collective-permute-start.11 = (f32[24]{0:T(128)S(1)}, f32[24]{0:T(128)S(1)}, u32[]{:S(2)}, u32[]{:S(2)}) collective-permute-start(f32[24]{0:T(128)S(1)} %reduce_sum.39), channel_id=1, source_target_pairs={{0,24},{8,0},{16,8},{24,16},{1,25},{9,1},{17,9},{25,17},{2,26},{10... | collective-permute-start | bytes 296 | tf_op jit(solution)/shard_map/ppermute | solution.py:148
  104.5 5.3 %collective-permute-start.9 = (f32[24]{0:T(128)S(1)}, f32[24]{0:T(128)S(1)}, u32[]{:S(2)}, u32[]{:S(2)}) collective-permute-start(f32[24]{0:T(128)S(1)} %reduce_sum.39), channel_id=1, source_target_pairs={{0,8},{8,16},{16,24},{24,0},{1,9},{9,17},{17,25},{25,1},{2,10},{10... | collective-permute-start | bytes 296 | tf_op jit(solution)/shard_map/ppermute | solution.py:148
Sparse Core Ops, SparseCore 0:
  100.4 24.9 reduce-scatter.1

commit v9 on v8

--- a/solution.py
+++ b/solution.py
@@ -147,8 +147,13 @@
         perm = [(src, (src + step) % chunks) for src in range(chunks)]
         class_weights = class_weights + lax.ppermute(local_mass, "img", perm)
     chunked = turn_and_sum(by_turn, gathered, classes_here, rotations, chunks)
-    class_sums = lax.psum_scatter(chunked, "img", scatter_dimension=0, tiled=True)
-    return (class_sums[0], class_weights)
+    me = lax.axis_index("img")
+    class_sums = lax.dynamic_index_in_dim(chunked, me, 0, keepdims=False)
+    for step in range(1, chunks):
+        perm = [(src, (src + step) % chunks) for src in range(chunks)]
+        outgoing = lax.dynamic_index_in_dim(chunked, (me + step) % chunks, 0, keepdims=False)
+        class_sums = class_sums + lax.ppermute(outgoing, "img", perm)
+    return (class_sums, class_weights)
 
 def solution(mesh):
     placed = (P(("img", "ref"), None), P("ref", None), P("ref"))

time: 132 us -> 122 us (0.924); the launches traced: 132 us -> 120 us
  between operations: 14.3 us -> 0.88 us
  waiting for transfers between devices: 41.6 us -> 37.2 us
  starting transfers between devices: 10.6 us -> 14.6 us
  local copies, waits for them, and re-layouts: 17.5 us -> 19.3 us
    reduce_scatter x1 -> x0, waiting for transfers between devices: 15 us -> none  [per_device(): lax.psum_scatter(chunked, 'img', scatter_dimension=0, tiled=True)]
    ppermute x0 -> x3, waiting for transfers between devices: none -> 13.9 us  [per_device(): class_sums = class_sums + lax.ppermute(outgoing, 'img', perm)]
    ppermute x3, waiting for transfers between devices: 4.66 us -> 0.01 us  [per_device(): class_weights = class_weights + lax.ppermute(local_mass, 'img', perm)]
    ppermute x0 -> x3, starting transfers between devices: none -> 3.1 us  [per_device(): class_sums = class_sums + lax.ppermute(outgoing, 'img', perm)]
    add x0 -> x1, other arithmetic: none -> 1.68 us  [per_device(): class_sums = class_sums + lax.ppermute(outgoing, 'img', perm)]
    dot_general x1, other arithmetic: 8.61 us -> 7 us  [per_device(): jnp.einsum('jp,jp->j', references, references, preferred_element_type=jnp...]
    ppermute x1, waiting for transfers between devices: 11.9 us -> 13.3 us  [ring_gather(): from_prev = lax.ppermute(from_prev, 'ref', to_next)]
    unnamed x28 -> x24, local copies, waits for them, and re-layouts: 10.9 us -> 10.7 us
  transfers between devices with their start and end apart: 13 -> 15, of which waited for: 6 -> 5; matrix products, arithmetic and copies ran while one was open for 19% -> 21% of each run, Pallas kernels for 0% -> 12%
where the time goes in v9:
time: 122 us; the launch traced here: 120 us
  waiting for transfers between devices  37.2 us (30%)
  local copies, waits for them, and re-layouts  19.3 us (16%)
  starting transfers between devices  14.6 us (12%)
  Pallas kernels  14.5 us (12%)
  other arithmetic  12.7 us (10%)
  matrix products  11.6 us (10%)
  blocking collectives  8.97 us (7%)
    pallas_call x1, Pallas kernels, turn_and_sum(): pl.pallas_call(functools.partial(turn_sum_kernel, classes_here, rotations...  14.5 us
    ppermute x3, waiting for transfers between devices, per_device(): class_sums = class_sums + lax.ppermute(outgoing, 'img', perm)  13.9 us
    ppermute x1, waiting for transfers between devices, ring_gather(): from_prev = lax.ppermute(from_prev, 'ref', to_next)  13.3 us
    dot_general x1, matrix products, per_device(): lax.dot_general(gathered, references, (((1,), (1,)), ((), ())), preferred...  11.6 us
    unnamed x24, local copies, waits for them, and re-layouts  10.7 us
    ppermute x1, waiting for transfers between devices, ring_gather(): top = lax.ppermute(from_prev[:half], 'ref', to_next)  9.65 us
    all_gather x1, blocking collectives, per_device(): stats = lax.all_gather(in_group_order, 'ref', axis=0)  8.97 us
    dot_general x1, other arithmetic, per_device(): jnp.einsum('jp,jp->j', references, references, preferred_element_type=jnp...  7 us
  transfers between devices with their start and end apart: 15, of which 5 were waited for; matrix products, arithmetic and copies ran while one was open for 21% of the time, Pallas kernels for 12%

profile of v9, /device:TPU:0, one launch (start us, length us, event | category | flops | bytes accessed | tf_op | source)
XLA Modules:
  0.0 119.8 jit_solution(7141791748335416810)
XLA Ops:
  0.6 3.0 %collective-permute-start = (bf16[64,9216]{1,0:T(8,128)(2,1)}, bf16[64,9216]{1,0:T(8,128)(2,1)S(1)}, u32[]{:S(2)}, u32[]{:S(2)}) collective-permute-start(bf16[64,9216]{1,0:T(8,128)(2,1)} %param.7), channel_id=1, source_target_pairs={{0,2},{1,3},{2,6},{3,7},{4,0},{5,1},{6,4},{7,5},{8,10},{9,11},{10,... | collective-permute-start | bytes 3538952 | tf_op jit(solution)/shard_map/ppermute | solution.py:90
  3.7 0.7 constant_dynamic-slice_fusion
  4.4 0.7 constant_dynamic-slice_fusion.1
  6.9 0.7 log.3
  7.8 7.0 %fusion = f32[864]{0:T(1024)S(1)} fusion(bf16[864,9216]{1,0:T(8,128)(2,1)} %param.8), kind=kLoop, calls=%fused_computation.3 | loop fusion | flops 23887008 | bytes 15928704 | tf_op jit(solution)/shard_map/jp,jp->j/dot_general | solution.py:117
  15.4 1.1 constant_dynamic-update-slice_fusion.9
  16.5 13.3 %collective-permute-done = bf16[64,9216]{1,0:T(8,128)(2,1)S(1)} collective-permute-done((bf16[64,9216]{1,0:T(8,128)(2,1)}, bf16[64,9216]{1,0:T(8,128)(2,1)S(1)}, u32[]{:S(2)}, u32[]{:S(2)}) %collective-permute-start) | collective-permute-done | bytes 1179680 | tf_op jit(solution)/shard_map/ppermute | solution.py:90
  29.9 1.8 %collective-permute-start.2 = (bf16[32,9216]{1,0:T(8,128)(2,1)S(1)}, bf16[32,9216]{1,0:T(8,128)(2,1)S(1)}, u32[]{:S(2)}, u32[]{:S(2)}) collective-permute-start(bf16[32,9216]{1,0:T(8,128)(2,1)S(1)} %slice.29), channel_id=1, source_target_pairs={{0,2},{1,3},{2,6},{3,7},{4,0},{5,1},{6,4},{7,5},{8,10},{9,11},{10,... | collective-permute-start | bytes 1769480 | tf_op jit(solution)/shard_map/ppermute | solution.py:95
  32.6 1.1 constant_dynamic-update-slice_fusion.8
  33.7 1.1 constant_dynamic-update-slice_fusion.7
  34.8 9.6 %collective-permute-done.2 = bf16[32,9216]{1,0:T(8,128)(2,1)S(1)} collective-permute-done((bf16[32,9216]{1,0:T(8,128)(2,1)S(1)}, bf16[32,9216]{1,0:T(8,128)(2,1)S(1)}, u32[]{:S(2)}, u32[]{:S(2)}) %collective-permute-start.2) | collective-permute-done | bytes 589856 | tf_op jit(solution)/shard_map/ppermute | solution.py:95
  44.5 0.9 constant_dynamic-update-slice_fusion.6
  45.8 0.8 constant_dynamic-update-slice_fusion.5
  46.7 2.4 %constant_dynamic-update-slice_fusion.4 = bf16[512,9216]{1,0:T(8,128)(2,1)} fusion(bf16[512,9216]{1,0:T(8,128)(2,1)} %constant_dynamic-update-slice_fusion.5, bf16[64,9216]{1,0:T(8,128)(2,1)} %collective-permute-done.4), kind=kLoop, calls=%fused_computation.23 | loop fusion | bytes 2359296
  49.1 1.1 constant_dynamic-update-slice_fusion.3
  50.2 1.1 constant_dynamic-update-slice_fusion.2
  51.3 0.9 constant_dynamic-update-slice_fusion.1
  52.3 0.9 constant_dynamic-update-slice_fusion.images_ref
  53.2 11.6 %fusion.7 = (f32[512]{0:T(512)S(1)}, f32[512,864]{0,1:T(8,128)S(1)}) fusion(f32[864]{0:T(1024)S(1)} %copy-done.4, bf16[512,9216]{1,0:T(8,128)(2,1)} %constant_dynamic-update-slice_fusion.images_ref, bf16[864,9216]{1,0:T(8,128)(2,1)S(1)} %copy-done), kind=kOutput, calls=%fused_computation.48 | convolution fusion | flops 8154611200 | bytes 27137408 | tf_op jit(solution)/shard_map/dot_general | solution.py:126
  65.3 1.0 gather_fusion
  66.6 9.0 %all-gather.1 = f32[8,2,512]{2,1,0:T(2,128)S(1)} all-gather(f32[1,2,512]{2,1,0:T(2,128)S(1)} %copy.26), channel_id=2, replica_groups=mesh['img'=4,'ref'=8] {'ref'}, dimensions={0}, use_global_device_ids=true | all-gather | bytes 36864 | tf_op jit(solution)/shard_map/all_gather | solution.py:133
  75.8 1.0 gather_fusion.1
  78.0 1.6 %collective-permute-start.12 = (f32[24]{0:T(128)S(1)}, f32[24]{0:T(128)S(1)}, u32[]{:S(2)}, u32[]{:S(2)}) collective-permute-start(f32[24]{0:T(128)S(1)} %reduce_sum.39), channel_id=1, source_target_pairs={{0,8},{8,16},{16,24},{24,0},{1,9},{9,17},{17,25},{25,1},{2,10},{10... | collective-permute-start | bytes 296 | tf_op jit(solution)/shard_map/ppermute | solution.py:148
  79.6 2.6 %collective-permute-start.13 = (f32[24]{0:T(128)S(1)}, f32[24]{0:T(128)S(1)}, u32[]{:S(2)}, u32[]{:S(2)}) collective-permute-start(f32[24]{0:T(128)S(1)} %reduce_sum.39), channel_id=1, source_target_pairs={{0,16},{8,24},{16,0},{24,8},{1,17},{9,25},{17,1},{25,9},{2,18},{10... | collective-permute-start | bytes 296 | tf_op jit(solution)/shard_map/ppermute | solution.py:148
  82.2 1.3 %collective-permute-start.14 = (f32[24]{0:T(128)S(1)}, f32[24]{0:T(128)S(1)}, u32[]{:S(2)}, u32[]{:S(2)}) collective-permute-start(f32[24]{0:T(128)S(1)} %reduce_sum.39), channel_id=1, source_target_pairs={{0,24},{8,0},{16,8},{24,16},{1,25},{9,1},{17,9},{25,17},{2,26},{10... | collective-permute-start | bytes 296 | tf_op jit(solution)/shard_map/ppermute | solution.py:148
  83.7 1.2 copy.30
  84.9 14.5 %shard_map.68 = f32[4,24,2304]{2,1,0:T(8,128)} custom-call(bf16[864,512]{1,0:T(8,128)(2,1)} %bitcast.45, bf16[512,9216]{1,0:T(8,128)(2,1)} %constant_dynamic-update-slice_fusion.images_ref, s32[1,2304]{1,0:T(1,128)} %and_select_fusion.angle_ref), custom_call_target="tpu_custom_call" | custom-call | flops 8153726976 | bytes 11206656 | tf_op jit(solution)/shard_map/pallas_call | solution.py:45
  99.4 1.2 dynamic-slice_bitcast_fusion.2
  100.9 2.7 %collective-permute-start.11 = (f32[24,2304]{1,0:T(8,128)S(1)}, f32[24,2304]{1,0:T(8,128)S(1)}, u32[]{:S(2)}, u32[]{:S(2)}) collective-permute-start(f32[24,2304]{1,0:T(8,128)S(1)} %get-tuple-element.8), channel_id=1, source_target_pairs={{0,24},{8,0},{16,8},{24,16},{1,25},{9,1},{17,9},{25,17},{2,26},{10... | collective-permute-start | bytes 663560 | tf_op jit(solution)/shard_map/ppermute | solution.py:155
  104.2 10.6 %collective-permute-done.10 = f32[24,2304]{1,0:T(8,128)S(1)} collective-permute-done((f32[24,2304]{1,0:T(8,128)S(1)}, f32[24,2304]{1,0:T(8,128)S(1)}, u32[]{:S(2)}, u32[]{:S(2)}) %collective-permute-start.10) | collective-permute-done | bytes 221216 | tf_op jit(solution)/shard_map/ppermute | solution.py:155
  114.8 3.3 %collective-permute-done.9 = f32[24,2304]{1,0:T(8,128)S(1)} collective-permute-done((f32[24,2304]{1,0:T(8,128)S(1)}, f32[24,2304]{1,0:T(8,128)S(1)}, u32[]{:S(2)}, u32[]{:S(2)}) %collective-permute-start.9) | collective-permute-done | bytes 221216 | tf_op jit(solution)/shard_map/ppermute | solution.py:155
  118.1 1.7 %fusion.2 = f32[24,2304]{1,0:T(8,128)} fusion(f32[24,2304]{1,0:T(8,128)S(1)} %collective-permute-done.11, f32[24,2304]{1,0:T(8,128)S(1)} %collective-permute-done.10, f32[24,2304]{1,0:T(8,128)S(1)} %collective-permute-done.9, f32[4,24,2304]{2,1,0:T(8,128)} %shard_map.68, s32[]{:T(128)S(6)} %select_n.54), kind=kLoop, calls=%fused_computation.14 | loop fusion | flops 165888 | bytes 1105924 | tf_op jit(solution)/shard_map/add | solution.py:155
  (60 shorter events, 7.2 us)
Async XLA Ops:
  0.6 14.8 %copy-start.1 = (bf16[64,9216]{1,0:T(8,128)(2,1)S(1)}, bf16[64,9216]{1,0:T(8,128)(2,1)}, u32[]{:S(2)}) copy-start(bf16[64,9216]{1,0:T(8,128)(2,1)} %param.7) | copy-start | bytes 3538948
  0.6 29.2 %collective-permute-start = (bf16[64,9216]{1,0:T(8,128)(2,1)}, bf16[64,9216]{1,0:T(8,128)(2,1)S(1)}, u32[]{:S(2)}, u32[]{:S(2)}) collective-permute-start(bf16[64,9216]{1,0:T(8,128)(2,1)} %param.7), channel_id=1, source_target_pairs={{0,2},{1,3},{2,6},{3,7},{4,0},{5,1},{6,4},{7,5},{8,10},{9,11},{10,... | collective-permute-start | bytes 3538952 | tf_op jit(solution)/shard_map/ppermute | solution.py:90
  3.6 28.0 %collective-permute-start.1 = (bf16[64,9216]{1,0:T(8,128)(2,1)}, bf16[64,9216]{1,0:T(8,128)(2,1)S(1)}, u32[]{:S(2)}, u32[]{:S(2)}) collective-permute-start(bf16[64,9216]{1,0:T(8,128)(2,1)} %param.7), channel_id=1, source_target_pairs={{0,4},{1,5},{2,0},{3,1},{4,6},{5,7},{6,2},{7,3},{8,12},{9,13},{10,... | collective-permute-start | bytes 3538952 | tf_op jit(solution)/shard_map/ppermute | solution.py:91
  3.7 43.0 %collective-permute-start.4 = (bf16[64,9216]{1,0:T(8,128)(2,1)}, bf16[64,9216]{1,0:T(8,128)(2,1)}, u32[]{:S(2)}, u32[]{:S(2)}) collective-permute-start(bf16[64,9216]{1,0:T(8,128)(2,1)} %param.7), channel_id=1, source_target_pairs={{0,1},{1,0},{2,3},{3,2},{4,5},{5,4},{6,7},{7,6},{8,9},{9,8},{10,11... | collective-permute-start | bytes 3538952 | tf_op jit(solution)/shard_map/ppermute | solution.py:99
  7.7 7.6 %copy-start.3 = (s32[512]{0:T(512)S(1)}, s32[512]{0:T(512)}, u32[]{:S(2)}) copy-start(s32[512]{0:T(512)} %get-tuple-element.16) | copy-start | bytes 6148
  7.7 7.6 %copy-start.2 = (s32[512]{0:T(512)S(1)}, s32[512]{0:T(512)}, u32[]{:S(2)}) copy-start(s32[512]{0:T(512)} %get-tuple-element.15) | copy-start | bytes 6148
  16.5 36.7 %copy-start = (bf16[864,9216]{1,0:T(8,128)(2,1)S(1)}, bf16[864,9216]{1,0:T(8,128)(2,1)}, u32[]{:S(2)}) copy-start(bf16[864,9216]{1,0:T(8,128)(2,1)} %param.8) | copy-start | bytes 47775748
  16.5 36.7 %copy-start.4 = (f32[864]{0:T(1024)S(1)}, f32[864]{0:T(1024)}, u32[]{:S(2)}) copy-start(f32[864]{0:T(1024)} %multiply_subtract_fusion) | copy-start | bytes 10372
  29.9 14.6 %collective-permute-start.2 = (bf16[32,9216]{1,0:T(8,128)(2,1)S(1)}, bf16[32,9216]{1,0:T(8,128)(2,1)S(1)}, u32[]{:S(2)}, u32[]{:S(2)}) collective-permute-start(bf16[32,9216]{1,0:T(8,128)(2,1)S(1)} %slice.29), channel_id=1, source_target_pairs={{0,2},{1,3},{2,6},{3,7},{4,0},{5,1},{6,4},{7,5},{8,10},{9,11},{10,... | collective-permute-start | bytes 1769480 | tf_op jit(solution)/shard_map/ppermute | solution.py:95
  31.7 14.0 %collective-permute-start.3 = (bf16[32,9216]{1,0:T(8,128)(2,1)S(1)}, bf16[32,9216]{1,0:T(8,128)(2,1)S(1)}, u32[]{:S(2)}, u32[]{:S(2)}) collective-permute-start(bf16[32,9216]{1,0:T(8,128)(2,1)S(1)} %slice.30), channel_id=1, source_target_pairs={{0,4},{1,5},{2,0},{3,1},{4,6},{5,7},{6,2},{7,3},{8,12},{9,13},{10,... | collective-permute-start | bytes 1769480 | tf_op jit(solution)/shard_map/ppermute | solution.py:96
  32.1 17.0 %collective-permute-start.5 = (bf16[64,9216]{1,0:T(8,128)(2,1)S(1)}, bf16[64,9216]{1,0:T(8,128)(2,1)S(1)}, u32[]{:S(2)}, u32[]{:S(2)}) collective-permute-start(bf16[64,9216]{1,0:T(8,128)(2,1)S(1)} %collective-permute-done), channel_id=1, source_target_pairs={{0,1},{1,0},{2,3},{3,2},{4,5},{5,4},{6,7},{7,6},{8,9},{9,8},{10,11... | collective-permute-start | bytes 3538952 | tf_op jit(solution)/shard_map/ppermute | solution.py:99
  32.1 18.1 %collective-permute-start.6 = (bf16[64,9216]{1,0:T(8,128)(2,1)S(1)}, bf16[64,9216]{1,0:T(8,128)(2,1)S(1)}, u32[]{:S(2)}, u32[]{:S(2)}) collective-permute-start(bf16[64,9216]{1,0:T(8,128)(2,1)S(1)} %collective-permute-done.1), channel_id=1, source_target_pairs={{0,1},{1,0},{2,3},{3,2},{4,5},{5,4},{6,7},{7,6},{8,9},{9,8},{10,11... | collective-permute-start | bytes 3538952 | tf_op jit(solution)/shard_map/ppermute | solution.py:99
  44.5 6.9 %collective-permute-start.7 = (bf16[32,9216]{1,0:T(8,128)(2,1)S(1)}, bf16[32,9216]{1,0:T(8,128)(2,1)S(1)}, u32[]{:S(2)}, u32[]{:S(2)}) collective-permute-start(bf16[32,9216]{1,0:T(8,128)(2,1)S(1)} %collective-permute-done.2), channel_id=1, source_target_pairs={{0,1},{1,0},{2,3},{3,2},{4,5},{5,4},{6,7},{7,6},{8,9},{9,8},{10,11... | collective-permute-start | bytes 1769480 | tf_op jit(solution)/shard_map/ppermute | solution.py:99
  45.7 6.6 %collective-permute-start.8 = (bf16[32,9216]{1,0:T(8,128)(2,1)S(1)}, bf16[32,9216]{1,0:T(8,128)(2,1)S(1)}, u32[]{:S(2)}, u32[]{:S(2)}) collective-permute-start(bf16[32,9216]{1,0:T(8,128)(2,1)S(1)} %collective-permute-done.3), channel_id=1, source_target_pairs={{0,1},{1,0},{2,3},{3,2},{4,5},{5,4},{6,7},{7,6},{8,9},{9,8},{10,11... | collective-permute-start | bytes 1769480 | tf_op jit(solution)/shard_map/ppermute | solution.py:99
  53.2 13.2 %copy-start.6 = (pred[512]{0:T(512)(128)(4,1)S(1)}, pred[512]{0:T(512)(128)(4,1)}, u32[]{:S(2)}) copy-start(pred[512]{0:T(512)(128)(4,1)} %get-tuple-element.18) | copy-start | bytes 1540
  53.2 23.7 %copy-start.5 = (pred[512]{0:T(512)(128)(4,1)S(1)}, pred[512]{0:T(512)(128)(4,1)}, u32[]{:S(2)}) copy-start(pred[512]{0:T(512)(128)(4,1)} %get-tuple-element.17) | copy-start | bytes 1540
  78.0 25.7 %collective-permute-start.12 = (f32[24]{0:T(128)S(1)}, f32[24]{0:T(128)S(1)}, u32[]{:S(2)}, u32[]{:S(2)}) collective-permute-start(f32[24]{0:T(128)S(1)} %reduce_sum.39), channel_id=1, source_target_pairs={{0,8},{8,16},{16,24},{24,0},{1,9},{9,17},{17,25},{25,1},{2,10},{10... | collective-permute-start | bytes 296 | tf_op jit(solution)/shard_map/ppermute | solution.py:148
  79.6 24.1 %collective-permute-start.13 = (f32[24]{0:T(128)S(1)}, f32[24]{0:T(128)S(1)}, u32[]{:S(2)}, u32[]{:S(2)}) collective-permute-start(f32[24]{0:T(128)S(1)} %reduce_sum.39), channel_id=1, source_target_pairs={{0,16},{8,24},{16,0},{24,8},{1,17},{9,25},{17,1},{25,9},{2,18},{10... | collective-permute-start | bytes 296 | tf_op jit(solution)/shard_map/ppermute | solution.py:148
  82.2 21.5 %collective-permute-start.14 = (f32[24]{0:T(128)S(1)}, f32[24]{0:T(128)S(1)}, u32[]{:S(2)}, u32[]{:S(2)}) collective-permute-start(f32[24]{0:T(128)S(1)} %reduce_sum.39), channel_id=1, source_target_pairs={{0,24},{8,0},{16,8},{24,16},{1,25},{9,1},{17,9},{25,17},{2,26},{10... | collective-permute-start | bytes 296 | tf_op jit(solution)/shard_map/ppermute | solution.py:148
  100.5 14.2 %collective-permute-start.10 = (f32[24,2304]{1,0:T(8,128)S(1)}, f32[24,2304]{1,0:T(8,128)S(1)}, u32[]{:S(2)}, u32[]{:S(2)}) collective-permute-start(f32[24,2304]{1,0:T(8,128)S(1)} %get-tuple-element.9), channel_id=1, source_target_pairs={{0,16},{8,24},{16,0},{24,8},{1,17},{9,25},{17,1},{25,9},{2,18},{10... | collective-permute-start | bytes 663560 | tf_op jit(solution)/shard_map/ppermute | solution.py:155
  100.9 13.8 %collective-permute-start.11 = (f32[24,2304]{1,0:T(8,128)S(1)}, f32[24,2304]{1,0:T(8,128)S(1)}, u32[]{:S(2)}, u32[]{:S(2)}) collective-permute-start(f32[24,2304]{1,0:T(8,128)S(1)} %get-tuple-element.8), channel_id=1, source_target_pairs={{0,24},{8,0},{16,8},{24,16},{1,25},{9,1},{17,9},{25,17},{2,26},{10... | collective-permute-start | bytes 663560 | tf_op jit(solution)/shard_map/ppermute | solution.py:155
  103.6 14.4 %collective-permute-start.9 = (f32[24,2304]{1,0:T(8,128)S(1)}, f32[24,2304]{1,0:T(8,128)S(1)}, u32[]{:S(2)}, u32[]{:S(2)}) collective-permute-start(f32[24,2304]{1,0:T(8,128)S(1)} %get-tuple-element.7), channel_id=1, source_target_pairs={{0,8},{8,16},{16,24},{24,0},{1,9},{9,17},{17,25},{25,1},{2,10},{10... | collective-permute-start | bytes 663560 | tf_op jit(solution)/shard_map/ppermute | solution.py:155

commit v10 on v9

--- a/solution.py
+++ b/solution.py
@@ -35,6 +35,11 @@
                 every = ahead if every is None else every + ahead
             wrapped = every - (kept - products_ref[row0 : row0 + rows, col0 : col0 + cols])
             out_ref[0, row0 : row0 + rows, col0 : col0 + cols] = kept + pltpu.roll(wrapped, ANG, 1)
+    mass = jnp.sum(by_turn_ref[...].astype(jnp.float32), axis=1, keepdims=True)
+    class_mass = mass[0:classes_here]
+    for turn_index in range(1, rotations):
+        class_mass = class_mass + mass[turn_index * classes_here : (turn_index + 1) * classes_here]
+    out_ref[0, :, width:] = jnp.broadcast_to(class_mass, (classes_here, LANES))
 
 
 def turn_and_sum(by_turn, gathered, classes_here, rotations, chunks):
@@ -50,8 +55,8 @@
             pl.BlockSpec((n, width), lambda t: (0, t)),
             pl.BlockSpec((1, width), lambda t: (0, 0)),
         ],
-        out_specs=pl.BlockSpec((1, classes_here, width), lambda t: (t, 0, 0)),
-        out_shape=jax.ShapeDtypeStruct((chunks, classes_here, width), jnp.float32),
+        out_specs=pl.BlockSpec((1, classes_here, width + LANES), lambda t: (t, 0, 0)),
+        out_shape=jax.ShapeDtypeStruct((chunks, classes_here, width + LANES), jnp.float32),
         scratch_shapes=[pltpu.VMEM((local_refs, width), jnp.float32)],
         compiler_params=pltpu.CompilerParams(vmem_limit_bytes=60 * 1024 * 1024),
         cost_estimate=pl.CostEstimate(
@@ -139,20 +144,15 @@
 
     n = weights.shape[0]
     by_turn = weights.reshape(n, classes_here, rotations).transpose(2, 1, 0).reshape(local_refs, n)
-    local_mass = (
-        jnp.sum(weights.astype(jnp.float32), axis=0).reshape(classes_here, rotations).sum(axis=1)
-    )
-    class_weights = local_mass
-    for step in range(1, chunks):
-        perm = [(src, (src + step) % chunks) for src in range(chunks)]
-        class_weights = class_weights + lax.ppermute(local_mass, "img", perm)
     chunked = turn_and_sum(by_turn, gathered, classes_here, rotations, chunks)
     me = lax.axis_index("img")
-    class_sums = lax.dynamic_index_in_dim(chunked, me, 0, keepdims=False)
+    total = lax.dynamic_index_in_dim(chunked, me, 0, keepdims=False)
     for step in range(1, chunks):
         perm = [(src, (src + step) % chunks) for src in range(chunks)]
         outgoing = lax.dynamic_index_in_dim(chunked, (me + step) % chunks, 0, keepdims=False)
-        class_sums = class_sums + lax.ppermute(outgoing, "img", perm)
+        total = total + lax.ppermute(outgoing, "img", perm)
+    width = pixels // chunks
+    class_sums, class_weights = total[:, :width], total[:, width]
     return (class_sums, class_weights)
 
 def solution(mesh):

time: 122 us -> 120 us (0.984)
  the two profiles are of different devices: /device:TPU:0 before, /device:TPU:19 now
where the time goes in v10:
time: 120 us
  waiting for transfers between devices  40 us (33%)
  local copies, waits for them, and re-layouts  20.5 us (17%)
  Pallas kernels  14.6 us (12%)
  starting transfers between devices  11.9 us (10%)
  matrix products  11.6 us (10%)
  other arithmetic  11.3 us (9%)
  blocking collectives  8.93 us (7%)
    ppermute x3, waiting for transfers between devices, per_device(): total = total + lax.ppermute(outgoing, 'img', perm)  21.1 us
    pallas_call x1, Pallas kernels, turn_and_sum(): pl.pallas_call(functools.partial(turn_sum_kernel, classes_here, rotations...  14.6 us
    dot_general x1, matrix products, per_device(): lax.dot_general(gathered, references, (((1,), (1,)), ((), ())), preferred...  11.6 us
    ppermute x1, waiting for transfers between devices, ring_gather(): from_prev = lax.ppermute(from_prev, 'ref', to_next)  11.5 us
    unnamed x24, local copies, waits for them, and re-layouts  10.7 us
    all_gather x1, blocking collectives, per_device(): stats = lax.all_gather(in_group_order, 'ref', axis=0)  8.93 us
    ppermute x1, waiting for transfers between devices, ring_gather(): top = lax.ppermute(from_prev[:half], 'ref', to_next)  7.36 us
    dot_general x1, other arithmetic, per_device(): jnp.einsum('jp,jp->j', references, references, preferred_element_type=jnp...  7 us
  transfers between devices with their start and end apart: 12, of which 5 were waited for; matrix products, arithmetic and copies ran while one was open for 19% of the time, Pallas kernels for 0%

profile of v10, /device:TPU:19, one launch (start us, length us, event | category | flops | bytes accessed | tf_op | source)
XLA Modules:
  0.0 119.8 jit_solution(12414190524241978879)
XLA Ops:
  0.6 1.3 %collective-permute-start = (bf16[64,9216]{1,0:T(8,128)(2,1)}, bf16[64,9216]{1,0:T(8,128)(2,1)S(1)}, u32[]{:S(2)}, u32[]{:S(2)}) collective-permute-start(bf16[64,9216]{1,0:T(8,128)(2,1)} %param.7), channel_id=1, source_target_pairs={{0,2},{1,3},{2,6},{3,7},{4,0},{5,1},{6,4},{7,5},{8,10},{9,11},{10,... | collective-permute-start | bytes 3538952 | tf_op jit(solution)/shard_map/ppermute | solution.py:95
  2.2 1.2 %collective-permute-start.4 = (bf16[64,9216]{1,0:T(8,128)(2,1)}, bf16[64,9216]{1,0:T(8,128)(2,1)}, u32[]{:S(2)}, u32[]{:S(2)}) collective-permute-start(bf16[64,9216]{1,0:T(8,128)(2,1)} %param.7), channel_id=1, source_target_pairs={{0,1},{1,0},{2,3},{3,2},{4,5},{5,4},{6,7},{7,6},{8,9},{9,8},{10,11... | collective-permute-start | bytes 3538952 | tf_op jit(solution)/shard_map/ppermute | solution.py:104
  3.4 0.7 constant_dynamic-slice_fusion
  4.1 0.7 constant_dynamic-slice_fusion.1
  7.4 7.0 %fusion = f32[864]{0:T(1024)S(1)} fusion(bf16[864,9216]{1,0:T(8,128)(2,1)} %param.8), kind=kLoop, calls=%fused_computation.3 | loop fusion | flops 23887008 | bytes 15928704 | tf_op jit(solution)/shard_map/jp,jp->j/dot_general | solution.py:122
  15.1 1.1 constant_dynamic-update-slice_fusion.9
  16.2 11.5 %collective-permute-done = bf16[64,9216]{1,0:T(8,128)(2,1)S(1)} collective-permute-done((bf16[64,9216]{1,0:T(8,128)(2,1)}, bf16[64,9216]{1,0:T(8,128)(2,1)S(1)}, u32[]{:S(2)}, u32[]{:S(2)}) %collective-permute-start) | collective-permute-done | bytes 1179680 | tf_op jit(solution)/shard_map/ppermute | solution.py:95
  27.8 1.3 %collective-permute-start.2 = (bf16[32,9216]{1,0:T(8,128)(2,1)S(1)}, bf16[32,9216]{1,0:T(8,128)(2,1)S(1)}, u32[]{:S(2)}, u32[]{:S(2)}) collective-permute-start(bf16[32,9216]{1,0:T(8,128)(2,1)S(1)} %slice.37), channel_id=1, source_target_pairs={{0,2},{1,3},{2,6},{3,7},{4,0},{5,1},{6,4},{7,5},{8,10},{9,11},{10,... | collective-permute-start | bytes 1769480 | tf_op jit(solution)/shard_map/ppermute | solution.py:100
  29.4 2.1 %collective-permute-start.5 = (bf16[64,9216]{1,0:T(8,128)(2,1)S(1)}, bf16[64,9216]{1,0:T(8,128)(2,1)S(1)}, u32[]{:S(2)}, u32[]{:S(2)}) collective-permute-start(bf16[64,9216]{1,0:T(8,128)(2,1)S(1)} %collective-permute-done), channel_id=1, source_target_pairs={{0,1},{1,0},{2,3},{3,2},{4,5},{5,4},{6,7},{7,6},{8,9},{9,8},{10,11... | collective-permute-start | bytes 3538952 | tf_op jit(solution)/shard_map/ppermute | solution.py:104
  31.5 1.1 constant_dynamic-update-slice_fusion.8
  32.6 1.1 constant_dynamic-update-slice_fusion.7
  33.7 7.4 %collective-permute-done.2 = bf16[32,9216]{1,0:T(8,128)(2,1)S(1)} collective-permute-done((bf16[32,9216]{1,0:T(8,128)(2,1)S(1)}, bf16[32,9216]{1,0:T(8,128)(2,1)S(1)}, u32[]{:S(2)}, u32[]{:S(2)}) %collective-permute-start.2) | collective-permute-done | bytes 589856 | tf_op jit(solution)/shard_map/ppermute | solution.py:100
  41.1 2.5 %collective-permute-start.7 = (bf16[32,9216]{1,0:T(8,128)(2,1)S(1)}, bf16[32,9216]{1,0:T(8,128)(2,1)S(1)}, u32[]{:S(2)}, u32[]{:S(2)}) collective-permute-start(bf16[32,9216]{1,0:T(8,128)(2,1)S(1)} %collective-permute-done.2), channel_id=1, source_target_pairs={{0,1},{1,0},{2,3},{3,2},{4,5},{5,4},{6,7},{7,6},{8,9},{9,8},{10,11... | collective-permute-start | bytes 1769480 | tf_op jit(solution)/shard_map/ppermute | solution.py:104
  43.6 0.9 constant_dynamic-update-slice_fusion.6
  44.9 0.9 constant_dynamic-update-slice_fusion.5
  45.8 2.4 %constant_dynamic-update-slice_fusion.4 = bf16[512,9216]{1,0:T(8,128)(2,1)} fusion(bf16[512,9216]{1,0:T(8,128)(2,1)} %constant_dynamic-update-slice_fusion.5, bf16[64,9216]{1,0:T(8,128)(2,1)} %collective-permute-done.4), kind=kLoop, calls=%fused_computation.22 | loop fusion | bytes 2359296
  48.2 1.1 constant_dynamic-update-slice_fusion.3
  49.3 1.1 constant_dynamic-update-slice_fusion.2
  50.4 0.9 constant_dynamic-update-slice_fusion.1
  51.3 0.9 constant_dynamic-update-slice_fusion.images_ref
  52.3 11.6 %fusion.7 = (f32[512]{0:T(512)S(1)}, f32[512,864]{0,1:T(8,128)S(1)}) fusion(f32[864]{0:T(1024)S(1)} %copy-done.4, bf16[512,9216]{1,0:T(8,128)(2,1)} %constant_dynamic-update-slice_fusion.images_ref, bf16[864,9216]{1,0:T(8,128)(2,1)S(1)} %copy-done), kind=kOutput, calls=%fused_computation.47 | convolution fusion | flops 8154611200 | bytes 27137408 | tf_op jit(solution)/shard_map/dot_general | solution.py:131
  64.4 1.0 gather_fusion
  65.7 8.9 %all-gather.1 = f32[8,2,512]{2,1,0:T(2,128)S(1)} all-gather(f32[1,2,512]{2,1,0:T(2,128)S(1)} %copy.20), channel_id=2, replica_groups=mesh['img'=4,'ref'=8] {'ref'}, dimensions={0}, use_global_device_ids=true | all-gather | bytes 36864 | tf_op jit(solution)/shard_map/all_gather | solution.py:138
  74.8 1.0 gather_fusion.1
  76.8 1.2 copy.24
  78.0 14.6 %shard_map.68 = f32[4,24,2432]{2,1,0:T(8,128)} custom-call(bf16[864,512]{1,0:T(8,128)(2,1)} %bitcast.45, bf16[512,9216]{1,0:T(8,128)(2,1)} %constant_dynamic-update-slice_fusion.images_ref, s32[1,2304]{1,0:T(1,128)} %and_select_fusion.angle_ref), custom_call_target="tpu_custom_call" | custom-call | flops 8153726976 | bytes 11206656 | tf_op jit(solution)/shard_map/pallas_call | solution.py:50
  92.6 1.2 %dynamic-slice_bitcast_fusion.2 = (f32[24,2432]{1,0:T(8,128)S(1)}, f32[24,2432]{1,0:T(8,128)S(1)}, f32[24,2432]{1,0:T(8,128)S(1)}) fusion(f32[4,24,2432]{2,1,0:T(8,128)} %shard_map.68, s32[]{:T(128)S(6)} %select_n.56, s32[]{:T(128)S(6)} %select_n.60, s32[]{:T(128)S(6)} %select_n.58), kind=kLoop, calls=%fused_computation.16 | loop fusion | bytes 1400844 | tf_op jit(solution)/shard_map/jit(dynamic_index_in_dim)/squeeze | solution.py:152
  93.9 2.4 %collective-permute-start.11 = (f32[24,2432]{1,0:T(8,128)S(1)}, f32[24,2432]{1,0:T(8,128)S(1)}, u32[]{:S(2)}, u32[]{:S(2)}) collective-permute-start(f32[24,2432]{1,0:T(8,128)S(1)} %get-tuple-element.6), channel_id=1, source_target_pairs={{0,24},{8,0},{16,8},{24,16},{1,25},{9,1},{17,9},{25,17},{2,26},{10... | collective-permute-start | bytes 700424 | tf_op jit(solution)/shard_map/ppermute | solution.py:153
  96.4 7.5 %collective-permute-done.10 = f32[24,2432]{1,0:T(8,128)S(1)} collective-permute-done((f32[24,2432]{1,0:T(8,128)S(1)}, f32[24,2432]{1,0:T(8,128)S(1)}, u32[]{:S(2)}, u32[]{:S(2)}) %collective-permute-start.10) | collective-permute-done | bytes 233504 | tf_op jit(solution)/shard_map/ppermute | solution.py:153
  103.9 10.0 %collective-permute-done.11 = f32[24,2432]{1,0:T(8,128)S(1)} collective-permute-done((f32[24,2432]{1,0:T(8,128)S(1)}, f32[24,2432]{1,0:T(8,128)S(1)}, u32[]{:S(2)}, u32[]{:S(2)}) %collective-permute-start.11) | collective-permute-done | bytes 233504 | tf_op jit(solution)/shard_map/ppermute | solution.py:153
  113.9 3.6 %collective-permute-done.9 = f32[24,2432]{1,0:T(8,128)S(1)} collective-permute-done((f32[24,2432]{1,0:T(8,128)S(1)}, f32[24,2432]{1,0:T(8,128)S(1)}, u32[]{:S(2)}, u32[]{:S(2)}) %collective-permute-start.9) | collective-permute-done | bytes 233504 | tf_op jit(solution)/shard_map/ppermute | solution.py:153
  117.5 1.0 fusion.2
  (53 shorter events, 7.5 us)
Async XLA Ops:
  0.6 14.5 %copy-start.1 = (bf16[64,9216]{1,0:T(8,128)(2,1)S(1)}, bf16[64,9216]{1,0:T(8,128)(2,1)}, u32[]{:S(2)}) copy-start(bf16[64,9216]{1,0:T(8,128)(2,1)} %param.7) | copy-start | bytes 3538948
  0.6 27.1 %collective-permute-start = (bf16[64,9216]{1,0:T(8,128)(2,1)}, bf16[64,9216]{1,0:T(8,128)(2,1)S(1)}, u32[]{:S(2)}, u32[]{:S(2)}) collective-permute-start(bf16[64,9216]{1,0:T(8,128)(2,1)} %param.7), channel_id=1, source_target_pairs={{0,2},{1,3},{2,6},{3,7},{4,0},{5,1},{6,4},{7,5},{8,10},{9,11},{10,... | collective-permute-start | bytes 3538952 | tf_op jit(solution)/shard_map/ppermute | solution.py:95
  1.9 27.1 %collective-permute-start.1 = (bf16[64,9216]{1,0:T(8,128)(2,1)}, bf16[64,9216]{1,0:T(8,128)(2,1)S(1)}, u32[]{:S(2)}, u32[]{:S(2)}) collective-permute-start(bf16[64,9216]{1,0:T(8,128)(2,1)} %param.7), channel_id=1, source_target_pairs={{0,4},{1,5},{2,0},{3,1},{4,6},{5,7},{6,2},{7,3},{8,12},{9,13},{10,... | collective-permute-start | bytes 3538952 | tf_op jit(solution)/shard_map/ppermute | solution.py:96
  2.2 43.6 %collective-permute-start.4 = (bf16[64,9216]{1,0:T(8,128)(2,1)}, bf16[64,9216]{1,0:T(8,128)(2,1)}, u32[]{:S(2)}, u32[]{:S(2)}) collective-permute-start(bf16[64,9216]{1,0:T(8,128)(2,1)} %param.7), channel_id=1, source_target_pairs={{0,1},{1,0},{2,3},{3,2},{4,5},{5,4},{6,7},{7,6},{8,9},{9,8},{10,11... | collective-permute-start | bytes 3538952 | tf_op jit(solution)/shard_map/ppermute | solution.py:104
  7.4 7.6 %copy-start.3 = (s32[512]{0:T(512)S(1)}, s32[512]{0:T(512)}, u32[]{:S(2)}) copy-start(s32[512]{0:T(512)} %get-tuple-element.14) | copy-start | bytes 6148
  7.4 7.7 %copy-start.2 = (s32[512]{0:T(512)S(1)}, s32[512]{0:T(512)}, u32[]{:S(2)}) copy-start(s32[512]{0:T(512)} %get-tuple-element.13) | copy-start | bytes 6148
  16.2 36.0 %copy-start = (bf16[864,9216]{1,0:T(8,128)(2,1)S(1)}, bf16[864,9216]{1,0:T(8,128)(2,1)}, u32[]{:S(2)}) copy-start(bf16[864,9216]{1,0:T(8,128)(2,1)} %param.8) | copy-start | bytes 47775748
  16.2 36.0 %copy-start.4 = (f32[864]{0:T(1024)S(1)}, f32[864]{0:T(1024)}, u32[]{:S(2)}) copy-start(f32[864]{0:T(1024)} %multiply_subtract_fusion) | copy-start | bytes 10372
  27.8 13.3 %collective-permute-start.2 = (bf16[32,9216]{1,0:T(8,128)(2,1)S(1)}, bf16[32,9216]{1,0:T(8,128)(2,1)S(1)}, u32[]{:S(2)}, u32[]{:S(2)}) collective-permute-start(bf16[32,9216]{1,0:T(8,128)(2,1)S(1)} %slice.37), channel_id=1, source_target_pairs={{0,2},{1,3},{2,6},{3,7},{4,0},{5,1},{6,4},{7,5},{8,10},{9,11},{10,... | collective-permute-start | bytes 1769480 | tf_op jit(solution)/shard_map/ppermute | solution.py:100
  29.1 15.3 %collective-permute-start.3 = (bf16[32,9216]{1,0:T(8,128)(2,1)S(1)}, bf16[32,9216]{1,0:T(8,128)(2,1)S(1)}, u32[]{:S(2)}, u32[]{:S(2)}) collective-permute-start(bf16[32,9216]{1,0:T(8,128)(2,1)S(1)} %slice.38), channel_id=1, source_target_pairs={{0,4},{1,5},{2,0},{3,1},{4,6},{5,7},{6,2},{7,3},{8,12},{9,13},{10,... | collective-permute-start | bytes 1769480 | tf_op jit(solution)/shard_map/ppermute | solution.py:101
  29.4 18.8 %collective-permute-start.5 = (bf16[64,9216]{1,0:T(8,128)(2,1)S(1)}, bf16[64,9216]{1,0:T(8,128)(2,1)S(1)}, u32[]{:S(2)}, u32[]{:S(2)}) collective-permute-start(bf16[64,9216]{1,0:T(8,128)(2,1)S(1)} %collective-permute-done), channel_id=1, source_target_pairs={{0,1},{1,0},{2,3},{3,2},{4,5},{5,4},{6,7},{7,6},{8,9},{9,8},{10,11... | collective-permute-start | bytes 3538952 | tf_op jit(solution)/shard_map/ppermute | solution.py:104
  31.5 17.8 %collective-permute-start.6 = (bf16[64,9216]{1,0:T(8,128)(2,1)S(1)}, bf16[64,9216]{1,0:T(8,128)(2,1)S(1)}, u32[]{:S(2)}, u32[]{:S(2)}) collective-permute-start(bf16[64,9216]{1,0:T(8,128)(2,1)S(1)} %collective-permute-done.1), channel_id=1, source_target_pairs={{0,1},{1,0},{2,3},{3,2},{4,5},{5,4},{6,7},{7,6},{8,9},{9,8},{10,11... | collective-permute-start | bytes 3538952 | tf_op jit(solution)/shard_map/ppermute | solution.py:104
  41.1 9.3 %collective-permute-start.7 = (bf16[32,9216]{1,0:T(8,128)(2,1)S(1)}, bf16[32,9216]{1,0:T(8,128)(2,1)S(1)}, u32[]{:S(2)}, u32[]{:S(2)}) collective-permute-start(bf16[32,9216]{1,0:T(8,128)(2,1)S(1)} %collective-permute-done.2), channel_id=1, source_target_pairs={{0,1},{1,0},{2,3},{3,2},{4,5},{5,4},{6,7},{7,6},{8,9},{9,8},{10,11... | collective-permute-start | bytes 1769480 | tf_op jit(solution)/shard_map/ppermute | solution.py:104
  44.4 6.9 %collective-permute-start.8 = (bf16[32,9216]{1,0:T(8,128)(2,1)S(1)}, bf16[32,9216]{1,0:T(8,128)(2,1)S(1)}, u32[]{:S(2)}, u32[]{:S(2)}) collective-permute-start(bf16[32,9216]{1,0:T(8,128)(2,1)S(1)} %collective-permute-done.3), channel_id=1, source_target_pairs={{0,1},{1,0},{2,3},{3,2},{4,5},{5,4},{6,7},{7,6},{8,9},{9,8},{10,11... | collective-permute-start | bytes 1769480 | tf_op jit(solution)/shard_map/ppermute | solution.py:104
  52.2 13.2 %copy-start.6 = (pred[512]{0:T(512)(128)(4,1)S(1)}, pred[512]{0:T(512)(128)(4,1)}, u32[]{:S(2)}) copy-start(pred[512]{0:T(512)(128)(4,1)} %get-tuple-element.16) | copy-start | bytes 1540
  52.2 23.6 %copy-start.5 = (pred[512]{0:T(512)(128)(4,1)S(1)}, pred[512]{0:T(512)(128)(4,1)}, u32[]{:S(2)}) copy-start(pred[512]{0:T(512)(128)(4,1)} %get-tuple-element.15) | copy-start | bytes 1540
  93.8 10.1 %collective-permute-start.10 = (f32[24,2432]{1,0:T(8,128)S(1)}, f32[24,2432]{1,0:T(8,128)S(1)}, u32[]{:S(2)}, u32[]{:S(2)}) collective-permute-start(f32[24,2432]{1,0:T(8,128)S(1)} %get-tuple-element.7), channel_id=1, source_target_pairs={{0,16},{8,24},{16,0},{24,8},{1,17},{9,25},{17,1},{25,9},{2,18},{10... | collective-permute-start | bytes 700424 | tf_op jit(solution)/shard_map/ppermute | solution.py:153
  93.9 20.0 %collective-permute-start.11 = (f32[24,2432]{1,0:T(8,128)S(1)}, f32[24,2432]{1,0:T(8,128)S(1)}, u32[]{:S(2)}, u32[]{:S(2)}) collective-permute-start(f32[24,2432]{1,0:T(8,128)S(1)} %get-tuple-element.6), channel_id=1, source_target_pairs={{0,24},{8,0},{16,8},{24,16},{1,25},{9,1},{17,9},{25,17},{2,26},{10... | collective-permute-start | bytes 700424 | tf_op jit(solution)/shard_map/ppermute | solution.py:153
  96.4 21.1 %collective-permute-start.9 = (f32[24,2432]{1,0:T(8,128)S(1)}, f32[24,2432]{1,0:T(8,128)S(1)}, u32[]{:S(2)}, u32[]{:S(2)}) collective-permute-start(f32[24,2432]{1,0:T(8,128)S(1)} %get-tuple-element.5), channel_id=1, source_target_pairs={{0,8},{8,16},{16,24},{24,0},{1,9},{9,17},{17,25},{25,1},{2,10},{10... | collective-permute-start | bytes 700424 | tf_op jit(solution)/shard_map/ppermute | solution.py:153

commit v11 on v10

--- a/solution.py
+++ b/solution.py
@@ -105,13 +105,16 @@
     table = []
     for device in range(n_ref):
         chip, core = device // 2, device % 2
-        rows = []
+        starts = []
         for side in (core, 1 - core):
-            for _, hops, first, count in pieces:
-                origin = 2 * ahead(chip, hops) + side
-                rows += list(range(origin * block + first, origin * block + first + count))
-        table.append(rows)
-    return jnp.concatenate(arrays, axis=0), np.array(table, np.int32)
+            for _, hops, first, _ in pieces:
+                starts.append((2 * ahead(chip, hops) + side) * block + first)
+        table.append(starts)
+    starts = jnp.asarray(np.array(table, np.int32))[lax.axis_index("ref")]
+    gathered = jnp.zeros((n_ref * block,) + images.shape[1:], images.dtype)
+    for index, array in enumerate(arrays):
+        gathered = lax.dynamic_update_slice(gathered, array, (starts[index], 0))
+    return gathered
 
 
 def per_device(chunks, n_ref, images, references, class_prior):
@@ -125,21 +128,16 @@
     offsets = (jnp.log(class_prior)[:, None] - half_norm.reshape(classes_here, rotations)).reshape(
         local_refs
     )
-    gathered, table = ring_gather(images, n_ref)
-    to_group = jnp.asarray(table)[lax.axis_index("ref")]
-    from_group = jnp.asarray(np.argsort(table, axis=1).astype(np.int32))[lax.axis_index("ref")]
+    gathered = ring_gather(images, n_ref)
     products = lax.dot_general(
         gathered, references, (((1,), (1,)), ((), ())), preferred_element_type=jnp.float32
     )
     scores = products + offsets
     local_max = jnp.max(scores, axis=1)
     local_sum = jnp.sum(jnp.exp(scores - local_max[:, None]), axis=1)
-    in_group_order = jnp.take(jnp.stack([local_max, local_sum]), from_group, axis=1)
-    stats = lax.all_gather(in_group_order, "ref", axis=0)
+    stats = lax.all_gather(jnp.stack([local_max, local_sum]), "ref", axis=0)
     top_score = jnp.max(stats[:, 0], axis=0)
     denominator = jnp.sum(stats[:, 1] * jnp.exp(stats[:, 0] - top_score[None, :]), axis=0)
-    norm = jnp.take(jnp.stack([top_score, denominator]), to_group, axis=1)
-    top_score, denominator = norm[0], norm[1]
     weights = (jnp.exp(scores - top_score[:, None]) / denominator[:, None]).astype(jnp.bfloat16)
 
     n = weights.shape[0]

time: 120 us -> 239 us (1.99)
  the two profiles are of different devices: /device:TPU:19 before, /device:TPU:17 now
where the time goes in v11:
time: 239 us; the launch traced here: 235 us
  local copies, waits for them, and re-layouts  108 us (45%)
  waiting for transfers between devices  47 us (20%)
  between operations  19.6 us (8%)
  Pallas kernels  14.6 us (6%)
  matrix products  14.1 us (6%)
  starting transfers between devices  13.4 us (6%)
  other arithmetic  9.29 us (4%)
  blocking collectives  9.09 us (4%)
    dynamic_update_slice x10, local copies, waits for them, and re-layouts, ring_gather(): gathered = lax.dynamic_update_slice(gathered, array, (starts[index], 0))  95.6 us
    ppermute x1, waiting for transfers between devices, ring_gather(): from_prev = lax.ppermute(from_prev, 'ref', to_next)  24.3 us
    ppermute x3, waiting for transfers between devices, per_device(): total = total + lax.ppermute(outgoing, 'img', perm)  21.1 us
    pallas_call x1, Pallas kernels, turn_and_sum(): pl.pallas_call(functools.partial(turn_sum_kernel, classes_here, rotations...  14.6 us
    dot_general x1, matrix products, per_device(): lax.dot_general(gathered, references, (((1,), (1,)), ((), ())), preferred...  14.1 us
    all_gather x1, blocking collectives, per_device(): stats = lax.all_gather(jnp.stack([local_max, local_sum]), 'ref', axis=0)  9.09 us
    ppermute x5, starting transfers between devices, ring_gather(): arrays += [lax.ppermute(piece[0], 'ref', to_partner) for piece in pieces]  7.87 us
    dot_general x1, other arithmetic, per_device(): jnp.einsum('jp,jp->j', references, references, preferred_element_type=jnp...  6.99 us
  transfers between devices with their start and end apart: 12, of which 5 were waited for; matrix products, arithmetic and copies ran while one was open for 45% of the time, Pallas kernels for 0%

profile of v11, /device:TPU:17, one launch (start us, length us, event | category | flops | bytes accessed | tf_op | source)
XLA Modules:
  0.0 235.2 jit_solution(13564332629736338096)
XLA Ops:
  0.6 1.3 collective-permute-start
  2.2 1.2 collective-permute-start.4
  3.4 24.3 %collective-permute-done = bf16[64,9216]{1,0:T(8,128)(2,1)S(1)} collective-permute-done((bf16[64,9216]{1,0:T(8,128)(2,1)}, bf16[64,9216]{1,0:T(8,128)(2,1)S(1)}, u32[]{:S(2)}, u32[]{:S(2)}) %collective-permute-start) | collective-permute-done | bytes 1179680 | tf_op jit(solution)/shard_map/ppermute | solution.py:95
  27.7 0.8 slice.75
  28.6 1.2 collective-permute-start.2
  29.8 0.8 slice.76
  30.9 2.1 collective-permute-start.5
  33.0 7.0 %fusion = f32[864]{0:T(1024)S(1)} fusion(bf16[864,9216]{1,0:T(8,128)(2,1)} %param.5), kind=kLoop, calls=%fused_computation.1 | loop fusion | flops 23887008 | bytes 15928704 | tf_op jit(solution)/shard_map/jp,jp->j/dot_general | solution.py:125
  40.7 1.5 collective-permute-done.2
  42.2 2.5 %collective-permute-start.7 = (bf16[32,9216]{1,0:T(8,128)(2,1)}, bf16[32,9216]{1,0:T(8,128)(2,1)}, u32[]{:S(2)}, u32[]{:S(2)}) collective-permute-start(bf16[32,9216]{1,0:T(8,128)(2,1)} %collective-permute-done.2), channel_id=1, source_target_pairs={{0,1},{1,0},{2,3},{3,2},{4,5},{5,4},{6,7},{7,6},{8,9},{9,8},{10,11... | collective-permute-start | bytes 1769480 | tf_op jit(solution)/shard_map/ppermute | solution.py:104
  44.6 2.1 collective-permute-start.8
  61.4 4.8 %broadcast_in_dim.2 = bf16[512,9216]{1,0:T(8,128)(2,1)} broadcast(bf16[]{:T(256)} %constant.56.clone.1), dimensions={} | broadcast | bytes 9437186 | tf_op jit(solution)/shard_map/broadcast_in_dim | solution.py:114
  66.2 10.9 %dynamic_update_slice.30 = bf16[512,9216]{1,0:T(8,128)(2,1)} dynamic-update-slice(bf16[512,9216]{1,0:T(8,128)(2,1)} %broadcast_in_dim.2, bf16[64,9216]{1,0:T(8,128)(2,1)S(1)} %copy-done, s32[]{:T(128)S(6)} %select_n.75, s32[]{:T(128)} %constant.58.clone.1) | dynamic-update-slice | bytes 2359300 | tf_op jit(solution)/shard_map/dynamic_update_slice | solution.py:116
  83.4 10.9 %dynamic_update_slice.31 = bf16[512,9216]{1,0:T(8,128)(2,1)} dynamic-update-slice(bf16[512,9216]{1,0:T(8,128)(2,1)} %dynamic_update_slice.30, bf16[64,9216]{1,0:T(8,128)(2,1)S(1)} %collective-permute-done, s32[]{:T(128)S(6)} %select_n.76, s32[]{:T(128)} %constant.58.clone.1) | dynamic-update-slice | bytes 2359300 | tf_op jit(solution)/shard_map/dynamic_update_slice | solution.py:116
  94.4 10.9 %dynamic_update_slice.32 = bf16[512,9216]{1,0:T(8,128)(2,1)} dynamic-update-slice(bf16[512,9216]{1,0:T(8,128)(2,1)} %dynamic_update_slice.31, bf16[64,9216]{1,0:T(8,128)(2,1)S(1)} %collective-permute-done.1, s32[]{:T(128)S(6)} %select_n.77, s32[]{:T(128)} %constant.58.clone.1) | dynamic-update-slice | bytes 2359300 | tf_op jit(solution)/shard_map/dynamic_update_slice | solution.py:116
  105.3 6.9 %dynamic_update_slice.33 = bf16[512,9216]{1,0:T(8,128)(2,1)} dynamic-update-slice(bf16[512,9216]{1,0:T(8,128)(2,1)} %dynamic_update_slice.32, bf16[32,9216]{1,0:T(8,128)(2,1)} %collective-permute-done.2, s32[]{:T(128)S(6)} %select_n.78, s32[]{:T(128)} %constant.58.clone.1) | dynamic-update-slice | bytes 1179652 | tf_op jit(solution)/shard_map/dynamic_update_slice | solution.py:116
  112.3 6.3 %dynamic_update_slice.34 = bf16[512,9216]{1,0:T(8,128)(2,1)} dynamic-update-slice(bf16[512,9216]{1,0:T(8,128)(2,1)} %dynamic_update_slice.33, bf16[32,9216]{1,0:T(8,128)(2,1)} %collective-permute-done.3, s32[]{:T(128)S(6)} %select_n.79, s32[]{:T(128)} %constant.58.clone.1) | dynamic-update-slice | bytes 1179652 | tf_op jit(solution)/shard_map/dynamic_update_slice | solution.py:116
  118.6 11.9 %dynamic_update_slice.35 = bf16[512,9216]{1,0:T(8,128)(2,1)} dynamic-update-slice(bf16[512,9216]{1,0:T(8,128)(2,1)} %dynamic_update_slice.34, bf16[64,9216]{1,0:T(8,128)(2,1)} %collective-permute-done.4, s32[]{:T(128)S(6)} %select_n.80, s32[]{:T(128)} %constant.58.clone.1) | dynamic-update-slice | bytes 2359300 | tf_op jit(solution)/shard_map/dynamic_update_slice | solution.py:116
  130.5 11.8 %dynamic_update_slice.36 = bf16[512,9216]{1,0:T(8,128)(2,1)} dynamic-update-slice(bf16[512,9216]{1,0:T(8,128)(2,1)} %dynamic_update_slice.35, bf16[64,9216]{1,0:T(8,128)(2,1)} %collective-permute-done.5, s32[]{:T(128)S(6)} %select_n.81, s32[]{:T(128)} %constant.58.clone.1) | dynamic-update-slice | bytes 2359300 | tf_op jit(solution)/shard_map/dynamic_update_slice | solution.py:116
  142.3 11.9 %dynamic_update_slice.37 = bf16[512,9216]{1,0:T(8,128)(2,1)} dynamic-update-slice(bf16[512,9216]{1,0:T(8,128)(2,1)} %dynamic_update_slice.36, bf16[64,9216]{1,0:T(8,128)(2,1)} %collective-permute-done.6, s32[]{:T(128)S(6)} %select_n.82, s32[]{:T(128)} %constant.58.clone.1) | dynamic-update-slice | bytes 2359300 | tf_op jit(solution)/shard_map/dynamic_update_slice | solution.py:116
  154.2 7.0 %dynamic_update_slice.38 = bf16[512,9216]{1,0:T(8,128)(2,1)} dynamic-update-slice(bf16[512,9216]{1,0:T(8,128)(2,1)} %dynamic_update_slice.37, bf16[32,9216]{1,0:T(8,128)(2,1)} %collective-permute-done.7, s32[]{:T(128)S(6)} %select_n.83, s32[]{:T(128)} %constant.58.clone.1) | dynamic-update-slice | bytes 1179652 | tf_op jit(solution)/shard_map/dynamic_update_slice | solution.py:116
  161.1 6.9 %dynamic_update_slice.39.images_ref = bf16[512,9216]{1,0:T(8,128)(2,1)} dynamic-update-slice(bf16[512,9216]{1,0:T(8,128)(2,1)} %dynamic_update_slice.38, bf16[32,9216]{1,0:T(8,128)(2,1)} %collective-permute-done.8, s32[]{:T(128)S(6)} %select_n.84, s32[]{:T(128)} %constant.58.clone.1) | dynamic-update-slice | bytes 1179652 | tf_op jit(solution)/shard_map/dynamic_update_slice | solution.py:116
  168.1 14.1 %fusion.7 = (f32[512]{0:T(512)S(1)}, f32[512,864]{0,1:T(8,128)S(1)}) fusion(f32[864]{0:T(1024)S(1)} %multiply_subtract_fusion, bf16[512,9216]{1,0:T(8,128)(2,1)} %dynamic_update_slice.39.images_ref, bf16[864,9216]{1,0:T(8,128)(2,1)} %param.5), kind=kOutput, calls=%fused_computation.23 | convolution fusion | flops 8154611200 | bytes 27137408 | tf_op jit(solution)/shard_map/dot_general | solution.py:132
  182.6 9.1 %all-gather.1 = f32[8,2,512]{2,1,0:T(2,128)S(1)} all-gather(f32[1,2,512]{2,1,0:T(2,128)S(1)} %maximum_bitcast_fusion), channel_id=2, replica_groups=mesh['img'=4,'ref'=8] {'ref'}, dimensions={0}, use_global_device_ids=true | all-gather | bytes 36864 | tf_op jit(solution)/shard_map/all_gather | solution.py:138
  192.2 1.2 copy.11
  193.4 14.6 %shard_map.59 = f32[4,24,2432]{2,1,0:T(8,128)} custom-call(bf16[864,512]{1,0:T(8,128)(2,1)} %bitcast.45, bf16[512,9216]{1,0:T(8,128)(2,1)} %dynamic_update_slice.39.images_ref, s32[1,2304]{1,0:T(1,128)} %and_select_fusion.angle_ref), custom_call_target="tpu_custom_call" | custom-call | flops 8153726976 | bytes 11206656 | tf_op jit(solution)/shard_map/pallas_call | solution.py:50
  208.0 1.2 dynamic-slice_bitcast_fusion.2
  209.3 2.4 %collective-permute-start.11 = (f32[24,2432]{1,0:T(8,128)S(1)}, f32[24,2432]{1,0:T(8,128)S(1)}, u32[]{:S(2)}, u32[]{:S(2)}) collective-permute-start(f32[24,2432]{1,0:T(8,128)S(1)} %get-tuple-element.3), channel_id=1, source_target_pairs={{0,24},{8,0},{16,8},{24,16},{1,25},{9,1},{17,9},{25,17},{2,26},{10... | collective-permute-start | bytes 700424 | tf_op jit(solution)/shard_map/ppermute | solution.py:151
  211.8 7.5 %collective-permute-done.10 = f32[24,2432]{1,0:T(8,128)S(1)} collective-permute-done((f32[24,2432]{1,0:T(8,128)S(1)}, f32[24,2432]{1,0:T(8,128)S(1)}, u32[]{:S(2)}, u32[]{:S(2)}) %collective-permute-start.10) | collective-permute-done | bytes 233504 | tf_op jit(solution)/shard_map/ppermute | solution.py:151
  219.3 10.0 %collective-permute-done.11 = f32[24,2432]{1,0:T(8,128)S(1)} collective-permute-done((f32[24,2432]{1,0:T(8,128)S(1)}, f32[24,2432]{1,0:T(8,128)S(1)}, u32[]{:S(2)}, u32[]{:S(2)}) %collective-permute-start.11) | collective-permute-done | bytes 233504 | tf_op jit(solution)/shard_map/ppermute | solution.py:151
  229.3 3.6 %collective-permute-done.9 = f32[24,2432]{1,0:T(8,128)S(1)} collective-permute-done((f32[24,2432]{1,0:T(8,128)S(1)}, f32[24,2432]{1,0:T(8,128)S(1)}, u32[]{:S(2)}, u32[]{:S(2)}) %collective-permute-start.9) | collective-permute-done | bytes 233504 | tf_op jit(solution)/shard_map/ppermute | solution.py:151
  232.9 1.0 fusion.2
  (33 shorter events, 5.6 us)
Async XLA Ops:
  0.6 59.3 %copy-start.2 = (f32[24]{0:T(128)S(1)}, f32[24]{0:T(128)}, u32[]{:S(2)}) copy-start(f32[24]{0:T(128)} %param.6) | copy-start | bytes 292
  0.6 27.1 %collective-permute-start = (bf16[64,9216]{1,0:T(8,128)(2,1)}, bf16[64,9216]{1,0:T(8,128)(2,1)S(1)}, u32[]{:S(2)}, u32[]{:S(2)}) collective-permute-start(bf16[64,9216]{1,0:T(8,128)(2,1)} %param.4), channel_id=1, source_target_pairs={{0,2},{1,3},{2,6},{3,7},{4,0},{5,1},{6,4},{7,5},{8,10},{9,11},{10,... | collective-permute-start | bytes 3538952 | tf_op jit(solution)/shard_map/ppermute | solution.py:95
  1.9 27.9 %collective-permute-start.1 = (bf16[64,9216]{1,0:T(8,128)(2,1)}, bf16[64,9216]{1,0:T(8,128)(2,1)S(1)}, u32[]{:S(2)}, u32[]{:S(2)}) collective-permute-start(bf16[64,9216]{1,0:T(8,128)(2,1)} %param.4), channel_id=1, source_target_pairs={{0,4},{1,5},{2,0},{3,1},{4,6},{5,7},{6,2},{7,3},{8,12},{9,13},{10,... | collective-permute-start | bytes 3538952 | tf_op jit(solution)/shard_map/ppermute | solution.py:96
  2.2 116.4 %collective-permute-start.4 = (bf16[64,9216]{1,0:T(8,128)(2,1)}, bf16[64,9216]{1,0:T(8,128)(2,1)}, u32[]{:S(2)}, u32[]{:S(2)}) collective-permute-start(bf16[64,9216]{1,0:T(8,128)(2,1)} %param.4), channel_id=1, source_target_pairs={{0,1},{1,0},{2,3},{3,2},{4,5},{5,4},{6,7},{7,6},{8,9},{9,8},{10,11... | collective-permute-start | bytes 3538952 | tf_op jit(solution)/shard_map/ppermute | solution.py:104
  28.6 13.6 %collective-permute-start.2 = (bf16[32,9216]{1,0:T(8,128)(2,1)}, bf16[32,9216]{1,0:T(8,128)(2,1)}, u32[]{:S(2)}, u32[]{:S(2)}) collective-permute-start(bf16[32,9216]{1,0:T(8,128)(2,1)} %slice.75), channel_id=1, source_target_pairs={{0,2},{1,3},{2,6},{3,7},{4,0},{5,1},{6,4},{7,5},{8,10},{9,11},{10,... | collective-permute-start | bytes 1769480 | tf_op jit(solution)/shard_map/ppermute | solution.py:100
  30.6 35.5 %copy-start = (bf16[64,9216]{1,0:T(8,128)(2,1)S(1)}, bf16[64,9216]{1,0:T(8,128)(2,1)}, u32[]{:S(2)}) copy-start(bf16[64,9216]{1,0:T(8,128)(2,1)} %param.4) | copy-start | bytes 3538948
  30.6 14.0 %collective-permute-start.3 = (bf16[32,9216]{1,0:T(8,128)(2,1)}, bf16[32,9216]{1,0:T(8,128)(2,1)}, u32[]{:S(2)}, u32[]{:S(2)}) collective-permute-start(bf16[32,9216]{1,0:T(8,128)(2,1)} %slice.76), channel_id=1, source_target_pairs={{0,4},{1,5},{2,0},{3,1},{4,6},{5,7},{6,2},{7,3},{8,12},{9,13},{10,... | collective-permute-start | bytes 1769480 | tf_op jit(solution)/shard_map/ppermute | solution.py:101
  30.9 99.6 %collective-permute-start.5 = (bf16[64,9216]{1,0:T(8,128)(2,1)S(1)}, bf16[64,9216]{1,0:T(8,128)(2,1)}, u32[]{:S(2)}, u32[]{:S(2)}) collective-permute-start(bf16[64,9216]{1,0:T(8,128)(2,1)S(1)} %collective-permute-done), channel_id=1, source_target_pairs={{0,1},{1,0},{2,3},{3,2},{4,5},{5,4},{6,7},{7,6},{8,9},{9,8},{10,11... | collective-permute-start | bytes 3538952 | tf_op jit(solution)/shard_map/ppermute | solution.py:104
  33.0 109.3 %collective-permute-start.6 = (bf16[64,9216]{1,0:T(8,128)(2,1)S(1)}, bf16[64,9216]{1,0:T(8,128)(2,1)}, u32[]{:S(2)}, u32[]{:S(2)}) collective-permute-start(bf16[64,9216]{1,0:T(8,128)(2,1)S(1)} %collective-permute-done.1), channel_id=1, source_target_pairs={{0,1},{1,0},{2,3},{3,2},{4,5},{5,4},{6,7},{7,6},{8,9},{9,8},{10,11... | collective-permute-start | bytes 3538952 | tf_op jit(solution)/shard_map/ppermute | solution.py:104
  42.2 112.0 %collective-permute-start.7 = (bf16[32,9216]{1,0:T(8,128)(2,1)}, bf16[32,9216]{1,0:T(8,128)(2,1)}, u32[]{:S(2)}, u32[]{:S(2)}) collective-permute-start(bf16[32,9216]{1,0:T(8,128)(2,1)} %collective-permute-done.2), channel_id=1, source_target_pairs={{0,1},{1,0},{2,3},{3,2},{4,5},{5,4},{6,7},{7,6},{8,9},{9,8},{10,11... | collective-permute-start | bytes 1769480 | tf_op jit(solution)/shard_map/ppermute | solution.py:104
  44.6 116.5 %collective-permute-start.8 = (bf16[32,9216]{1,0:T(8,128)(2,1)}, bf16[32,9216]{1,0:T(8,128)(2,1)}, u32[]{:S(2)}, u32[]{:S(2)}) collective-permute-start(bf16[32,9216]{1,0:T(8,128)(2,1)} %collective-permute-done.3), channel_id=1, source_target_pairs={{0,1},{1,0},{2,3},{3,2},{4,5},{5,4},{6,7},{7,6},{8,9},{9,8},{10,11... | collective-permute-start | bytes 1769480 | tf_op jit(solution)/shard_map/ppermute | solution.py:104
  60.8 22.0 %copy-start.1 = (f32[864]{0:T(1024)S(1)}, f32[864]{0:T(1024)}, u32[]{:S(2)}) copy-start(f32[864]{0:T(1024)} %sub.37) | copy-start | bytes 10372
  209.2 10.1 %collective-permute-start.10 = (f32[24,2432]{1,0:T(8,128)S(1)}, f32[24,2432]{1,0:T(8,128)S(1)}, u32[]{:S(2)}, u32[]{:S(2)}) collective-permute-start(f32[24,2432]{1,0:T(8,128)S(1)} %get-tuple-element.4), channel_id=1, source_target_pairs={{0,16},{8,24},{16,0},{24,8},{1,17},{9,25},{17,1},{25,9},{2,18},{10... | collective-permute-start | bytes 700424 | tf_op jit(solution)/shard_map/ppermute | solution.py:151
  209.3 20.0 %collective-permute-start.11 = (f32[24,2432]{1,0:T(8,128)S(1)}, f32[24,2432]{1,0:T(8,128)S(1)}, u32[]{:S(2)}, u32[]{:S(2)}) collective-permute-start(f32[24,2432]{1,0:T(8,128)S(1)} %get-tuple-element.3), channel_id=1, source_target_pairs={{0,24},{8,0},{16,8},{24,16},{1,25},{9,1},{17,9},{25,17},{2,26},{10... | collective-permute-start | bytes 700424 | tf_op jit(solution)/shard_map/ppermute | solution.py:151
  211.8 21.1 %collective-permute-start.9 = (f32[24,2432]{1,0:T(8,128)S(1)}, f32[24,2432]{1,0:T(8,128)S(1)}, u32[]{:S(2)}, u32[]{:S(2)}) collective-permute-start(f32[24,2432]{1,0:T(8,128)S(1)} %get-tuple-element.2), channel_id=1, source_target_pairs={{0,8},{8,16},{16,24},{24,0},{1,9},{9,17},{17,25},{25,1},{2,10},{10... | collective-permute-start | bytes 700424 | tf_op jit(solution)/shard_map/ppermute | solution.py:151

commit v12 on v10

--- a/solution.py
+++ b/solution.py
@@ -13,12 +13,15 @@
 GROUP_COLS = 1152
 
 
-def turn_sum_kernel(classes_here, rotations, by_turn_ref, images_ref, angle_ref, out_ref, products_ref):
+def turn_sum_kernel(
+    classes_here, rotations, by_turn_ref, early_ref, late_ref, angle_ref, out_ref, products_ref
+):
     shift = ANG // rotations
-    width = images_ref.shape[1]
+    width = early_ref.shape[1]
+    split = early_ref.shape[0]
     products_ref[...] = jnp.dot(
-        by_turn_ref[...], images_ref[...], preferred_element_type=jnp.float32
-    )
+        by_turn_ref[:, :split], early_ref[...], preferred_element_type=jnp.float32
+    ) + jnp.dot(by_turn_ref[:, split:], late_ref[...], preferred_element_type=jnp.float32)
     rows = 8 if classes_here % 8 == 0 else classes_here
     cols = GROUP_COLS if width % GROUP_COLS == 0 else width
     for row0 in range(0, classes_here, rows):
@@ -42,9 +45,9 @@
     out_ref[0, :, width:] = jnp.broadcast_to(class_mass, (classes_here, LANES))
 
 
-def turn_and_sum(by_turn, gathered, classes_here, rotations, chunks):
+def turn_and_sum(by_turn, early, late, classes_here, rotations, chunks):
     local_refs, n = by_turn.shape
-    pixels = gathered.shape[1]
+    pixels = early.shape[1]
     width = pixels // chunks
     angle = (jnp.arange(width, dtype=jnp.int32) % ANG).reshape(1, width)
     return pl.pallas_call(
@@ -52,7 +55,8 @@
         grid=(chunks,),
         in_specs=[
             pl.BlockSpec((local_refs, n), lambda t: (0, 0)),
-            pl.BlockSpec((n, width), lambda t: (0, t)),
+            pl.BlockSpec((early.shape[0], width), lambda t: (0, t)),
+            pl.BlockSpec((late.shape[0], width), lambda t: (0, t)),
             pl.BlockSpec((1, width), lambda t: (0, 0)),
         ],
         out_specs=pl.BlockSpec((1, classes_here, width + LANES), lambda t: (t, 0, 0)),
@@ -64,7 +68,7 @@
             bytes_accessed=2 * local_refs * n + 2 * n * pixels + 4 * classes_here * pixels,
             transcendentals=0,
         ),
-    )(by_turn, gathered, angle)
+    )(by_turn, early, late, angle)
 
 
 def ring_order(chips):
@@ -100,18 +104,25 @@
         top = lax.ppermute(from_prev[:half], "ref", to_next)
         bottom = lax.ppermute(from_next[half:], "ref", to_prev)
         pieces += [(top, chips // 2, 0, half), (bottom, chips // 2, half, block - half)]
-    arrays = [piece[0] for piece in pieces]
-    arrays += [lax.ppermute(piece[0], "ref", to_partner) for piece in pieces]
+    partner_pieces = [(lax.ppermute(piece[0], "ref", to_partner),) + piece[1:] for piece in pieces]
+    full = [piece for piece in pieces if piece[3] == block]
+    early = full + partner_pieces[:1]
+    late = [piece for piece in pieces if piece[3] != block] + partner_pieces[1:]
     table = []
     for device in range(n_ref):
         chip, core = device // 2, device % 2
         rows = []
-        for side in (core, 1 - core):
-            for _, hops, first, count in pieces:
+        for group in (early, late):
+            for index, (_, hops, first, count) in enumerate(group):
+                side = 1 - core if any(group[index] is p for p in partner_pieces) else core
                 origin = 2 * ahead(chip, hops) + side
                 rows += list(range(origin * block + first, origin * block + first + count))
         table.append(rows)
-    return jnp.concatenate(arrays, axis=0), np.array(table, np.int32)
+    return (
+        jnp.concatenate([piece[0] for piece in early], axis=0),
+        jnp.concatenate([piece[0] for piece in late], axis=0),
+        np.array(table, np.int32),
+    )
 
 
 def per_device(chunks, n_ref, images, references, class_prior):
@@ -125,13 +136,18 @@
     offsets = (jnp.log(class_prior)[:, None] - half_norm.reshape(classes_here, rotations)).reshape(
         local_refs
     )
-    gathered, table = ring_gather(images, n_ref)
+    early, late, table = ring_gather(images, n_ref)
     to_group = jnp.asarray(table)[lax.axis_index("ref")]
     from_group = jnp.asarray(np.argsort(table, axis=1).astype(np.int32))[lax.axis_index("ref")]
-    products = lax.dot_general(
-        gathered, references, (((1,), (1,)), ((), ())), preferred_element_type=jnp.float32
-    )
-    scores = products + offsets
+    scores = jnp.concatenate(
+        [
+            lax.dot_general(
+                group, references, (((1,), (1,)), ((), ())), preferred_element_type=jnp.float32
+            )
+            for group in (early, late)
+        ],
+        axis=0,
+    ) + offsets
     local_max = jnp.max(scores, axis=1)
     local_sum = jnp.sum(jnp.exp(scores - local_max[:, None]), axis=1)
     in_group_order = jnp.take(jnp.stack([local_max, local_sum]), from_group, axis=1)
@@ -144,7 +160,7 @@
 
     n = weights.shape[0]
     by_turn = weights.reshape(n, classes_here, rotations).transpose(2, 1, 0).reshape(local_refs, n)
-    chunked = turn_and_sum(by_turn, gathered, classes_here, rotations, chunks)
+    chunked = turn_and_sum(by_turn, early, late, classes_here, rotations, chunks)
     me = lax.axis_index("img")
     total = lax.dynamic_index_in_dim(chunked, me, 0, keepdims=False)
     for step in range(1, chunks):

time: 120 us -> 122 us (1.017)
  the two profiles are of different devices: /device:TPU:19 before, /device:TPU:17 now
where the time goes in v12:
time: 122 us
  waiting for transfers between devices  34.9 us (29%)
  local copies, waits for them, and re-layouts  17.9 us (15%)
  matrix products  17.3 us (14%)
  Pallas kernels  16.8 us (14%)
  other arithmetic  14.3 us (12%)
  starting transfers between devices  9.89 us (8%)
  blocking collectives  9.45 us (8%)
    ppermute x3, waiting for transfers between devices, per_device(): total = total + lax.ppermute(outgoing, 'img', perm)  21.1 us
    dot_general x2, matrix products, per_device(): lax.dot_general(group, references, (((1,), (1,)), ((), ())), preferred_el...  17.3 us
    pallas_call x1, Pallas kernels, turn_and_sum(): pl.pallas_call(functools.partial(turn_sum_kernel, classes_here, rotations...  16.8 us
    ppermute x1, waiting for transfers between devices, ring_gather(): from_prev = lax.ppermute(from_prev, 'ref', to_next)  11.1 us
    all_gather x1, blocking collectives, per_device(): stats = lax.all_gather(in_group_order, 'ref', axis=0)  9.45 us
    dot_general x1, other arithmetic, per_device(): jnp.einsum('jp,jp->j', references, references, preferred_element_type=jnp...  7.11 us
    unnamed x25, local copies, waits for them, and re-layouts  4.88 us
    ppermute x5, starting transfers between devices, ring_gather(): lax.ppermute(piece[0], 'ref', to_partner)  4.36 us
  transfers between devices with their start and end apart: 12, of which 8 were waited for; matrix products, arithmetic and copies ran while one was open for 22% of the time, Pallas kernels for 0%

profile of v12, /device:TPU:17, one launch (start us, length us, event | category | flops | bytes accessed | tf_op | source)
XLA Modules:
  0.0 121.6 jit_solution(11263700377274627472)
XLA Ops:
  0.6 1.3 %collective-permute-start = (bf16[64,9216]{1,0:T(8,128)(2,1)}, bf16[64,9216]{1,0:T(8,128)(2,1)S(1)}, u32[]{:S(2)}, u32[]{:S(2)}) collective-permute-start(bf16[64,9216]{1,0:T(8,128)(2,1)} %param.7), channel_id=1, source_target_pairs={{0,2},{1,3},{2,6},{3,7},{4,0},{5,1},{6,4},{7,5},{8,10},{9,11},{10,... | collective-permute-start | bytes 3538952 | tf_op jit(solution)/shard_map/ppermute | solution.py:99
  2.1 1.2 %collective-permute-start.2 = (bf16[64,9216]{1,0:T(8,128)(2,1)}, bf16[64,9216]{1,0:T(8,128)(2,1)}, u32[]{:S(2)}, u32[]{:S(2)}) collective-permute-start(bf16[64,9216]{1,0:T(8,128)(2,1)} %param.7), channel_id=1, source_target_pairs={{0,1},{1,0},{2,3},{3,2},{4,5},{5,4},{6,7},{7,6},{8,9},{9,8},{10,11... | collective-permute-start | bytes 3538952 | tf_op jit(solution)/shard_map/ppermute | solution.py:107
  3.4 0.7 constant_dynamic-slice_fusion
  4.1 0.7 constant_dynamic-slice_fusion.1
  7.5 7.1 %fusion = f32[864]{0:T(1024)S(1)} fusion(bf16[864,9216]{1,0:T(8,128)(2,1)} %param.8), kind=kLoop, calls=%fused_computation.3 | loop fusion | flops 23887008 | bytes 15928704 | tf_op jit(solution)/shard_map/jp,jp->j/dot_general | solution.py:133
  15.3 1.2 %pad_clamp_fusion = s32[1024]{0:T(1024)} fusion(s32[512]{0:T(512)} %get-tuple-element.11), kind=kLoop, calls=%fused_computation.43 | loop fusion | flops 1024 | bytes 6144 | tf_op gather
  16.6 11.1 %collective-permute-done = bf16[64,9216]{1,0:T(8,128)(2,1)S(1)} collective-permute-done((bf16[64,9216]{1,0:T(8,128)(2,1)}, bf16[64,9216]{1,0:T(8,128)(2,1)S(1)}, u32[]{:S(2)}, u32[]{:S(2)}) %collective-permute-start) | collective-permute-done | bytes 1179680 | tf_op jit(solution)/shard_map/ppermute | solution.py:99
  27.7 0.9 slice.37
  28.6 1.2 collective-permute-start.3
  29.9 0.9 slice.38
  31.1 1.3 %constant_dynamic-update-slice_fusion.early_ref = bf16[256,9216]{1,0:T(8,128)(2,1)S(1)} fusion(bf16[256,9216]{1,0:T(8,128)(2,1)S(1)} %constant_dynamic-update-slice_fusion.1, bf16[64,9216]{1,0:T(8,128)(2,1)} %collective-permute-done.2), kind=kLoop, calls=%fused_computation.24 | loop fusion | bytes 2359296 | tf_op jit(solution)/shard_map/concatenate | solution.py:122
  32.5 2.1 %copy-done.2 = bf16[256,9216]{1,0:T(8,128)(2,1)} copy-done((bf16[256,9216]{1,0:T(8,128)(2,1)}, bf16[256,9216]{1,0:T(8,128)(2,1)S(1)}, u32[]{:S(2)}) %copy-start.2) | copy-done | bytes 4718616
  34.6 7.8 %fusion.13 = f32[256,864]{0,1:T(8,128)S(1)} fusion(bf16[256,9216]{1,0:T(8,128)(2,1)S(1)} %constant_dynamic-update-slice_fusion.early_ref, bf16[864,9216]{1,0:T(8,128)(2,1)} %param.8), kind=kOutput, calls=%fused_computation.53 | convolution fusion | flops 4076863488 | bytes 21528576 | tf_op jit(solution)/shard_map/dot_general | solution.py:144
  42.5 2.2 %collective-permute-start.5 = (bf16[64,9216]{1,0:T(8,128)(2,1)}, bf16[64,9216]{1,0:T(8,128)(2,1)S(1)}, u32[]{:S(2)}, u32[]{:S(2)}) collective-permute-start(bf16[64,9216]{1,0:T(8,128)(2,1)} %copy-done), channel_id=1, source_target_pairs={{0,1},{1,0},{2,3},{3,2},{4,5},{5,4},{6,7},{7,6},{8,9},{9,8},{10,11... | collective-permute-start | bytes 3538952 | tf_op jit(solution)/shard_map/ppermute | solution.py:107
  44.8 1.1 constant_dynamic-update-slice_fusion.9
  46.8 1.1 constant_dynamic-update-slice_fusion.8
  48.4 1.3 %collective-permute-done.6 = bf16[64,9216]{1,0:T(8,128)(2,1)S(1)} collective-permute-done((bf16[64,9216]{1,0:T(8,128)(2,1)S(1)}, bf16[64,9216]{1,0:T(8,128)(2,1)S(1)}, u32[]{:S(2)}, u32[]{:S(2)}) %collective-permute-start.6) | collective-permute-done | bytes 1179680 | tf_op jit(solution)/shard_map/ppermute | solution.py:107
  49.9 0.8 collective-permute-done.8
  50.8 9.5 %fusion.14 = f32[256,864]{0,1:T(8,128)S(1)} fusion(bf16[256,9216]{1,0:T(8,128)(2,1)S(1)} %constant_dynamic-update-slice_fusion.4.late_ref, bf16[864,9216]{1,0:T(8,128)(2,1)} %param.8), kind=kOutput, calls=%fused_computation.54 | convolution fusion | flops 4076863488 | bytes 21528576 | tf_op jit(solution)/shard_map/dot_general | solution.py:144
  60.6 1.0 concatenate.19
  62.2 1.0 gather_fusion
  63.5 9.4 %all-gather.1 = f32[8,2,512]{2,1,0:T(2,128)S(1)} all-gather(f32[1,2,512]{2,1,0:T(2,128)S(1)} %copy.21), channel_id=2, replica_groups=mesh['img'=4,'ref'=8] {'ref'}, dimensions={0}, use_global_device_ids=true | all-gather | bytes 36864 | tf_op jit(solution)/shard_map/all_gather | solution.py:154
  73.2 1.0 gather_fusion.1
  74.7 1.6 %fusion.6 = bf16[36,24,512]{2,0,1:T(8,128)(2,1)S(1)} fusion(f32[512]{0:T(512)S(1)} %get-tuple-element.4, f32[512]{0:T(512)S(1)} %get-tuple-element.3, f32[24,36]{1,0:T(8,128)S(1)} %add.79, f32[256,24,36]{0,2,1:T(8,128)} %concatenate.19, f32[256,24,36]{0,2,1:T(8,128)S(1)} %concatenate.17), kind=kLoop, calls=%fused_computation.12 | loop fusion | flops 2211840 | bytes 2661760 | tf_op jit(solution)/shard_map/transpose | solution.py:162
  76.3 1.2 copy.25
  77.5 16.8 %shard_map.68 = f32[4,24,2432]{2,1,0:T(8,128)} custom-call(bf16[864,512]{1,0:T(8,128)(2,1)} %bitcast.49, bf16[256,9216]{1,0:T(8,128)(2,1)} %copy-done.2, bf16[256,9216]{1,0:T(8,128)(2,1)} %copy-done.3, s32[1,2304]{1,0:T(1,128)} %and_select_fusion.angle_ref), custom_call_target="tpu_custom_call" | custom-call | flops 8153726976 | bytes 11206656 | tf_op jit(solution)/shard_map/pallas_call | solution.py:53
  94.4 1.2 dynamic-slice_bitcast_fusion.2
  95.7 2.4 %collective-permute-start.11 = (f32[24,2432]{1,0:T(8,128)S(1)}, f32[24,2432]{1,0:T(8,128)S(1)}, u32[]{:S(2)}, u32[]{:S(2)}) collective-permute-start(f32[24,2432]{1,0:T(8,128)S(1)} %get-tuple-element.6), channel_id=1, source_target_pairs={{0,24},{8,0},{16,8},{24,16},{1,25},{9,1},{17,9},{25,17},{2,26},{10... | collective-permute-start | bytes 700424 | tf_op jit(solution)/shard_map/ppermute | solution.py:169
  98.1 7.5 %collective-permute-done.10 = f32[24,2432]{1,0:T(8,128)S(1)} collective-permute-done((f32[24,2432]{1,0:T(8,128)S(1)}, f32[24,2432]{1,0:T(8,128)S(1)}, u32[]{:S(2)}, u32[]{:S(2)}) %collective-permute-start.10) | collective-permute-done | bytes 233504 | tf_op jit(solution)/shard_map/ppermute | solution.py:169
  105.6 10.0 %collective-permute-done.11 = f32[24,2432]{1,0:T(8,128)S(1)} collective-permute-done((f32[24,2432]{1,0:T(8,128)S(1)}, f32[24,2432]{1,0:T(8,128)S(1)}, u32[]{:S(2)}, u32[]{:S(2)}) %collective-permute-start.11) | collective-permute-done | bytes 233504 | tf_op jit(solution)/shard_map/ppermute | solution.py:169
  115.6 3.6 %collective-permute-done.9 = f32[24,2432]{1,0:T(8,128)S(1)} collective-permute-done((f32[24,2432]{1,0:T(8,128)S(1)}, f32[24,2432]{1,0:T(8,128)S(1)}, u32[]{:S(2)}, u32[]{:S(2)}) %collective-permute-start.9) | collective-permute-done | bytes 233504 | tf_op jit(solution)/shard_map/ppermute | solution.py:169
  119.2 1.0 fusion.8
  (59 shorter events, 9.0 us)
Async XLA Ops:
  0.6 27.1 %collective-permute-start = (bf16[64,9216]{1,0:T(8,128)(2,1)}, bf16[64,9216]{1,0:T(8,128)(2,1)S(1)}, u32[]{:S(2)}, u32[]{:S(2)}) collective-permute-start(bf16[64,9216]{1,0:T(8,128)(2,1)} %param.7), channel_id=1, source_target_pairs={{0,2},{1,3},{2,6},{3,7},{4,0},{5,1},{6,4},{7,5},{8,10},{9,11},{10,... | collective-permute-start | bytes 3538952 | tf_op jit(solution)/shard_map/ppermute | solution.py:99
  1.9 28.0 %collective-permute-start.1 = (bf16[64,9216]{1,0:T(8,128)(2,1)}, bf16[64,9216]{1,0:T(8,128)(2,1)S(1)}, u32[]{:S(2)}, u32[]{:S(2)}) collective-permute-start(bf16[64,9216]{1,0:T(8,128)(2,1)} %param.7), channel_id=1, source_target_pairs={{0,4},{1,5},{2,0},{3,1},{4,6},{5,7},{6,2},{7,3},{8,12},{9,13},{10,... | collective-permute-start | bytes 3538952 | tf_op jit(solution)/shard_map/ppermute | solution.py:100
  2.1 29.0 %collective-permute-start.2 = (bf16[64,9216]{1,0:T(8,128)(2,1)}, bf16[64,9216]{1,0:T(8,128)(2,1)}, u32[]{:S(2)}, u32[]{:S(2)}) collective-permute-start(bf16[64,9216]{1,0:T(8,128)(2,1)} %param.7), channel_id=1, source_target_pairs={{0,1},{1,0},{2,3},{3,2},{4,5},{5,4},{6,7},{7,6},{8,9},{9,8},{10,11... | collective-permute-start | bytes 3538952 | tf_op jit(solution)/shard_map/ppermute | solution.py:107
  7.4 9.1 %copy-start.1 = (bf16[64,9216]{1,0:T(8,128)(2,1)S(1)}, bf16[64,9216]{1,0:T(8,128)(2,1)}, u32[]{:S(2)}) copy-start(bf16[64,9216]{1,0:T(8,128)(2,1)} %param.7) | copy-start | bytes 3538948
  27.7 3.4 %copy-start = (bf16[64,9216]{1,0:T(8,128)(2,1)}, bf16[64,9216]{1,0:T(8,128)(2,1)S(1)}, u32[]{:S(2)}) copy-start(bf16[64,9216]{1,0:T(8,128)(2,1)S(1)} %collective-permute-done) | copy-start | bytes 3538948
  28.6 16.1 %collective-permute-start.3 = (bf16[32,9216]{1,0:T(8,128)(2,1)}, bf16[32,9216]{1,0:T(8,128)(2,1)}, u32[]{:S(2)}, u32[]{:S(2)}) collective-permute-start(bf16[32,9216]{1,0:T(8,128)(2,1)} %slice.37), channel_id=1, source_target_pairs={{0,2},{1,3},{2,6},{3,7},{4,0},{5,1},{6,4},{7,5},{8,10},{9,11},{10,... | collective-permute-start | bytes 1769480 | tf_op jit(solution)/shard_map/ppermute | solution.py:104
  30.7 15.7 %collective-permute-start.4 = (bf16[32,9216]{1,0:T(8,128)(2,1)}, bf16[32,9216]{1,0:T(8,128)(2,1)}, u32[]{:S(2)}, u32[]{:S(2)}) collective-permute-start(bf16[32,9216]{1,0:T(8,128)(2,1)} %slice.38), channel_id=1, source_target_pairs={{0,4},{1,5},{2,0},{3,1},{4,6},{5,7},{6,2},{7,3},{8,12},{9,13},{10,... | collective-permute-start | bytes 1769480 | tf_op jit(solution)/shard_map/ppermute | solution.py:105
  32.5 2.1 %copy-start.2 = (bf16[256,9216]{1,0:T(8,128)(2,1)}, bf16[256,9216]{1,0:T(8,128)(2,1)S(1)}, u32[]{:S(2)}) copy-start(bf16[256,9216]{1,0:T(8,128)(2,1)S(1)} %constant_dynamic-update-slice_fusion.early_ref) | copy-start | bytes 14155780
  42.5 5.8 %collective-permute-start.5 = (bf16[64,9216]{1,0:T(8,128)(2,1)}, bf16[64,9216]{1,0:T(8,128)(2,1)S(1)}, u32[]{:S(2)}, u32[]{:S(2)}) collective-permute-start(bf16[64,9216]{1,0:T(8,128)(2,1)} %copy-done), channel_id=1, source_target_pairs={{0,1},{1,0},{2,3},{3,2},{4,5},{5,4},{6,7},{7,6},{8,9},{9,8},{10,11... | collective-permute-start | bytes 3538952 | tf_op jit(solution)/shard_map/ppermute | solution.py:107
  44.7 4.9 %collective-permute-start.6 = (bf16[64,9216]{1,0:T(8,128)(2,1)S(1)}, bf16[64,9216]{1,0:T(8,128)(2,1)S(1)}, u32[]{:S(2)}, u32[]{:S(2)}) collective-permute-start(bf16[64,9216]{1,0:T(8,128)(2,1)S(1)} %collective-permute-done.1), channel_id=1, source_target_pairs={{0,1},{1,0},{2,3},{3,2},{4,5},{5,4},{6,7},{7,6},{8,9},{9,8},{10,11... | collective-permute-start | bytes 3538952 | tf_op jit(solution)/shard_map/ppermute | solution.py:107
  45.9 4.0 %collective-permute-start.7 = (bf16[32,9216]{1,0:T(8,128)(2,1)}, bf16[32,9216]{1,0:T(8,128)(2,1)S(1)}, u32[]{:S(2)}, u32[]{:S(2)}) collective-permute-start(bf16[32,9216]{1,0:T(8,128)(2,1)} %collective-permute-done.3), channel_id=1, source_target_pairs={{0,1},{1,0},{2,3},{3,2},{4,5},{5,4},{6,7},{7,6},{8,9},{9,8},{10,11... | collective-permute-start | bytes 1769480 | tf_op jit(solution)/shard_map/ppermute | solution.py:107
  46.4 4.4 %collective-permute-start.8 = (bf16[32,9216]{1,0:T(8,128)(2,1)}, bf16[32,9216]{1,0:T(8,128)(2,1)S(1)}, u32[]{:S(2)}, u32[]{:S(2)}) collective-permute-start(bf16[32,9216]{1,0:T(8,128)(2,1)} %collective-permute-done.4), channel_id=1, source_target_pairs={{0,1},{1,0},{2,3},{3,2},{4,5},{5,4},{6,7},{7,6},{8,9},{9,8},{10,11... | collective-permute-start | bytes 1769480 | tf_op jit(solution)/shard_map/ppermute | solution.py:107
  50.8 9.5 %copy-start.3 = (bf16[256,9216]{1,0:T(8,128)(2,1)}, bf16[256,9216]{1,0:T(8,128)(2,1)S(1)}, u32[]{:S(2)}) copy-start(bf16[256,9216]{1,0:T(8,128)(2,1)S(1)} %constant_dynamic-update-slice_fusion.4.late_ref) | copy-start | bytes 14155780
  60.3 1.8 %copy-start.4 = (s32[1024]{0:T(1024)S(1)}, s32[1024]{0:T(1024)}, u32[]{:S(2)}) copy-start(s32[1024]{0:T(1024)} %pad_clamp_fusion.1) | copy-start | bytes 12292
  60.3 2.9 %copy-start.7 = (pred[512]{0:T(512)(128)(4,1)S(1)}, pred[512]{0:T(512)(128)(4,1)}, u32[]{:S(2)}) copy-start(pred[512]{0:T(512)(128)(4,1)} %get-tuple-element.14) | copy-start | bytes 1540
  60.4 12.8 %copy-start.5 = (s32[1024]{0:T(1024)S(1)}, s32[1024]{0:T(1024)}, u32[]{:S(2)}) copy-start(s32[1024]{0:T(1024)} %pad_clamp_fusion) | copy-start | bytes 12292
  60.4 13.8 %copy-start.6 = (pred[512]{0:T(512)(128)(4,1)S(1)}, pred[512]{0:T(512)(128)(4,1)}, u32[]{:S(2)}) copy-start(pred[512]{0:T(512)(128)(4,1)} %get-tuple-element.13) | copy-start | bytes 1540
  95.6 10.1 %collective-permute-start.10 = (f32[24,2432]{1,0:T(8,128)S(1)}, f32[24,2432]{1,0:T(8,128)S(1)}, u32[]{:S(2)}, u32[]{:S(2)}) collective-permute-start(f32[24,2432]{1,0:T(8,128)S(1)} %get-tuple-element.7), channel_id=1, source_target_pairs={{0,16},{8,24},{16,0},{24,8},{1,17},{9,25},{17,1},{25,9},{2,18},{10... | collective-permute-start | bytes 700424 | tf_op jit(solution)/shard_map/ppermute | solution.py:169
  95.7 20.0 %collective-permute-start.11 = (f32[24,2432]{1,0:T(8,128)S(1)}, f32[24,2432]{1,0:T(8,128)S(1)}, u32[]{:S(2)}, u32[]{:S(2)}) collective-permute-start(f32[24,2432]{1,0:T(8,128)S(1)} %get-tuple-element.6), channel_id=1, source_target_pairs={{0,24},{8,0},{16,8},{24,16},{1,25},{9,1},{17,9},{25,17},{2,26},{10... | collective-permute-start | bytes 700424 | tf_op jit(solution)/shard_map/ppermute | solution.py:169
  98.1 21.1 %collective-permute-start.9 = (f32[24,2432]{1,0:T(8,128)S(1)}, f32[24,2432]{1,0:T(8,128)S(1)}, u32[]{:S(2)}, u32[]{:S(2)}) collective-permute-start(f32[24,2432]{1,0:T(8,128)S(1)} %get-tuple-element.5), channel_id=1, source_target_pairs={{0,8},{8,16},{16,24},{24,0},{1,9},{9,17},{17,25},{25,1},{2,10},{10... | collective-permute-start | bytes 700424 | tf_op jit(solution)/shard_map/ppermute | solution.py:169

commit v13 on v10

--- a/solution.py
+++ b/solution.py
@@ -13,7 +13,9 @@
 GROUP_COLS = 1152
 
 
-def turn_sum_kernel(classes_here, rotations, by_turn_ref, images_ref, angle_ref, out_ref, products_ref):
+def turn_sum_kernel(
+    classes_here, rotations, me_ref, by_turn_ref, images_ref, angle_ref, out_ref, products_ref
+):
     shift = ANG // rotations
     width = images_ref.shape[1]
     products_ref[...] = jnp.dot(
@@ -42,30 +44,36 @@
     out_ref[0, :, width:] = jnp.broadcast_to(class_mass, (classes_here, LANES))
 
 
-def turn_and_sum(by_turn, gathered, classes_here, rotations, chunks):
+def turn_and_sum(by_turn, gathered, classes_here, rotations, chunks, me, first, count):
     local_refs, n = by_turn.shape
     pixels = gathered.shape[1]
     width = pixels // chunks
     angle = (jnp.arange(width, dtype=jnp.int32) % ANG).reshape(1, width)
+
+    def chunk_of(t, me_ref):
+        return (0, (me_ref[0] + first + t) % chunks)
+
     return pl.pallas_call(
         functools.partial(turn_sum_kernel, classes_here, rotations),
-        grid=(chunks,),
-        in_specs=[
-            pl.BlockSpec((local_refs, n), lambda t: (0, 0)),
-            pl.BlockSpec((n, width), lambda t: (0, t)),
-            pl.BlockSpec((1, width), lambda t: (0, 0)),
-        ],
-        out_specs=pl.BlockSpec((1, classes_here, width + LANES), lambda t: (t, 0, 0)),
-        out_shape=jax.ShapeDtypeStruct((chunks, classes_here, width + LANES), jnp.float32),
-        scratch_shapes=[pltpu.VMEM((local_refs, width), jnp.float32)],
+        grid_spec=pltpu.PrefetchScalarGridSpec(
+            num_scalar_prefetch=1,
+            grid=(count,),
+            in_specs=[
+                pl.BlockSpec((local_refs, n), lambda t, me_ref: (0, 0)),
+                pl.BlockSpec((n, width), chunk_of),
+                pl.BlockSpec((1, width), lambda t, me_ref: (0, 0)),
+            ],
+            out_specs=pl.BlockSpec((1, classes_here, width + LANES), lambda t, me_ref: (t, 0, 0)),
+            scratch_shapes=[pltpu.VMEM((local_refs, width), jnp.float32)],
+        ),
+        out_shape=jax.ShapeDtypeStruct((count, classes_here, width + LANES), jnp.float32),
         compiler_params=pltpu.CompilerParams(vmem_limit_bytes=60 * 1024 * 1024),
         cost_estimate=pl.CostEstimate(
-            flops=2 * local_refs * n * pixels,
-            bytes_accessed=2 * local_refs * n + 2 * n * pixels + 4 * classes_here * pixels,
+            flops=2 * local_refs * n * width * count,
+            bytes_accessed=2 * local_refs * n + 2 * n * width * count + 4 * classes_here * width * count,
             transcendentals=0,
         ),
-    )(by_turn, gathered, angle)
-
+    )(jnp.reshape(me, (1,)).astype(jnp.int32), by_turn, gathered, angle)
 
 def ring_order(chips):
     if chips == 4:
@@ -144,13 +152,17 @@
 
     n = weights.shape[0]
     by_turn = weights.reshape(n, classes_here, rotations).transpose(2, 1, 0).reshape(local_refs, n)
-    chunked = turn_and_sum(by_turn, gathered, classes_here, rotations, chunks)
     me = lax.axis_index("img")
-    total = lax.dynamic_index_in_dim(chunked, me, 0, keepdims=False)
-    for step in range(1, chunks):
-        perm = [(src, (src + step) % chunks) for src in range(chunks)]
-        outgoing = lax.dynamic_index_in_dim(chunked, (me + step) % chunks, 0, keepdims=False)
-        total = total + lax.ppermute(outgoing, "img", perm)
+    received = []
+    if chunks > 1:
+        outgoing = turn_and_sum(by_turn, gathered, classes_here, rotations, chunks, me, 1, chunks - 1)
+        received = [
+            lax.ppermute(outgoing[step - 1], "img", [(src, (src + step) % chunks) for src in range(chunks)])
+            for step in range(1, chunks)
+        ]
+    total = turn_and_sum(by_turn, gathered, classes_here, rotations, chunks, me, 0, 1)[0]
+    for part in received:
+        total = total + part
     width = pixels // chunks
     class_sums, class_weights = total[:, :width], total[:, width]
     return (class_sums, class_weights)

time: 120 us -> 115 us (0.958)
  the two profiles are of different devices: /device:TPU:19 before, /device:TPU:17 now
where the time goes in v13:
time: 115 us
  waiting for transfers between devices  37.1 us (32%)
  Pallas kernels  17.2 us (15%)
  matrix products  15.2 us (13%)
  starting transfers between devices  12.7 us (11%)
  other arithmetic  12.5 us (11%)
  local copies, waits for them, and re-layouts  10.2 us (9%)
  blocking collectives  9.22 us (8%)
    pallas_call x2, Pallas kernels, turn_and_sum(): pl.pallas_call(functools.partial(turn_sum_kernel, classes_here, rotations...  17.2 us
    ppermute x3, waiting for transfers between devices, per_device(): lax.ppermute(outgoing[step - 1], 'img', [(src, (src + step) % chunks) for...  15.6 us
    dot_general x1, matrix products, per_device(): lax.dot_general(gathered, references, (((1,), (1,)), ((), ())), preferred...  15.2 us
    ppermute x1, waiting for transfers between devices, ring_gather(): from_prev = lax.ppermute(from_prev, 'ref', to_next)  12.1 us
    ppermute x1, waiting for transfers between devices, ring_gather(): top = lax.ppermute(from_prev[:half], 'ref', to_next)  9.43 us
    all_gather x1, blocking collectives, per_device(): stats = lax.all_gather(in_group_order, 'ref', axis=0)  9.22 us
    ppermute x5, starting transfers between devices, ring_gather(): arrays += [lax.ppermute(piece[0], 'ref', to_partner) for piece in pieces]  7.07 us
    dot_general x1, other arithmetic, per_device(): jnp.einsum('jp,jp->j', references, references, preferred_element_type=jnp...  7 us
  transfers between devices with their start and end apart: 12, of which 5 were waited for; matrix products, arithmetic and copies ran while one was open for 12% of the time, Pallas kernels for 5%

profile of v13, /device:TPU:17, one launch (start us, length us, event | category | flops | bytes accessed | tf_op | source)
XLA Modules:
  0.0 115.1 jit_solution(1306250489864899625)
XLA Ops:
  0.6 1.3 %collective-permute-start = (bf16[64,9216]{1,0:T(8,128)(2,1)}, bf16[64,9216]{1,0:T(8,128)(2,1)S(1)}, u32[]{:S(2)}, u32[]{:S(2)}) collective-permute-start(bf16[64,9216]{1,0:T(8,128)(2,1)} %param.7), channel_id=1, source_target_pairs={{0,2},{1,3},{2,6},{3,7},{4,0},{5,1},{6,4},{7,5},{8,10},{9,11},{10,... | collective-permute-start | bytes 3538952 | tf_op jit(solution)/shard_map/ppermute | solution.py:103
  2.2 1.2 %collective-permute-start.4 = (bf16[64,9216]{1,0:T(8,128)(2,1)}, bf16[64,9216]{1,0:T(8,128)(2,1)}, u32[]{:S(2)}, u32[]{:S(2)}) collective-permute-start(bf16[64,9216]{1,0:T(8,128)(2,1)} %param.7), channel_id=1, source_target_pairs={{0,1},{1,0},{2,3},{3,2},{4,5},{5,4},{6,7},{7,6},{8,9},{9,8},{10,11... | collective-permute-start | bytes 3538952 | tf_op jit(solution)/shard_map/ppermute | solution.py:112
  3.4 0.7 constant_dynamic-slice_fusion
  4.7 0.6 compare_and_fusion.1
  5.3 0.6 compare_select_fusion
  5.9 0.6 compare_and_fusion
  6.5 0.6 and_select_fusion.angle_ref
  7.1 0.7 log.3
  7.9 7.0 %fusion = f32[864]{0:T(1024)S(1)} fusion(bf16[864,9216]{1,0:T(8,128)(2,1)} %param.8), kind=kLoop, calls=%fused_computation.3 | loop fusion | flops 23887008 | bytes 15928704 | tf_op jit(solution)/shard_map/jp,jp->j/dot_general | solution.py:130
  14.9 0.6 multiply_subtract_fusion
  15.7 12.1 %collective-permute-done = bf16[64,9216]{1,0:T(8,128)(2,1)S(1)} collective-permute-done((bf16[64,9216]{1,0:T(8,128)(2,1)}, bf16[64,9216]{1,0:T(8,128)(2,1)S(1)}, u32[]{:S(2)}, u32[]{:S(2)}) %collective-permute-start) | collective-permute-done | bytes 1179680 | tf_op jit(solution)/shard_map/ppermute | solution.py:103
  27.8 1.3 %collective-permute-start.2 = (bf16[32,9216]{1,0:T(8,128)(2,1)S(1)}, bf16[32,9216]{1,0:T(8,128)(2,1)S(1)}, u32[]{:S(2)}, u32[]{:S(2)}) collective-permute-start(bf16[32,9216]{1,0:T(8,128)(2,1)S(1)} %slice.49), channel_id=1, source_target_pairs={{0,2},{1,3},{2,6},{3,7},{4,0},{5,1},{6,4},{7,5},{8,10},{9,11},{10,... | collective-permute-start | bytes 1769480 | tf_op jit(solution)/shard_map/ppermute | solution.py:108
  29.4 2.1 %collective-permute-start.5 = (bf16[64,9216]{1,0:T(8,128)(2,1)S(1)}, bf16[64,9216]{1,0:T(8,128)(2,1)S(1)}, u32[]{:S(2)}, u32[]{:S(2)}) collective-permute-start(bf16[64,9216]{1,0:T(8,128)(2,1)S(1)} %collective-permute-done), channel_id=1, source_target_pairs={{0,1},{1,0},{2,3},{3,2},{4,5},{5,4},{6,7},{7,6},{8,9},{9,8},{10,11... | collective-permute-start | bytes 3538952 | tf_op jit(solution)/shard_map/ppermute | solution.py:112
  31.7 9.4 %collective-permute-done.2 = bf16[32,9216]{1,0:T(8,128)(2,1)S(1)} collective-permute-done((bf16[32,9216]{1,0:T(8,128)(2,1)S(1)}, bf16[32,9216]{1,0:T(8,128)(2,1)S(1)}, u32[]{:S(2)}, u32[]{:S(2)}) %collective-permute-start.2) | collective-permute-done | bytes 589856 | tf_op jit(solution)/shard_map/ppermute | solution.py:108
  41.1 2.5 %collective-permute-start.7 = (bf16[32,9216]{1,0:T(8,128)(2,1)S(1)}, bf16[32,9216]{1,0:T(8,128)(2,1)S(1)}, u32[]{:S(2)}, u32[]{:S(2)}) collective-permute-start(bf16[32,9216]{1,0:T(8,128)(2,1)S(1)} %collective-permute-done.2), channel_id=1, source_target_pairs={{0,1},{1,0},{2,3},{3,2},{4,5},{5,4},{6,7},{7,6},{8,9},{9,8},{10,11... | collective-permute-start | bytes 1769480 | tf_op jit(solution)/shard_map/ppermute | solution.py:112
  43.6 1.3 %collective-permute-start.8 = (bf16[32,9216]{1,0:T(8,128)(2,1)S(1)}, bf16[32,9216]{1,0:T(8,128)(2,1)S(1)}, u32[]{:S(2)}, u32[]{:S(2)}) collective-permute-start(bf16[32,9216]{1,0:T(8,128)(2,1)S(1)} %collective-permute-done.3), channel_id=1, source_target_pairs={{0,1},{1,0},{2,3},{3,2},{4,5},{5,4},{6,7},{7,6},{8,9},{9,8},{10,11... | collective-permute-start | bytes 1769480 | tf_op jit(solution)/shard_map/ppermute | solution.py:112
  44.9 1.3 %constant_dynamic-update-slice_fusion.4 = bf16[512,9216]{1,0:T(8,128)(2,1)S(1)} fusion(bf16[512,9216]{1,0:T(8,128)(2,1)S(1)} %constant_dynamic-update-slice_fusion.5, bf16[64,9216]{1,0:T(8,128)(2,1)} %collective-permute-done.4), kind=kLoop, calls=%fused_computation.22 | loop fusion | bytes 2359296
  46.6 15.2 %fusion.7 = (f32[512]{0:T(512)S(1)}, f32[512,864]{0,1:T(8,128)S(1)}) fusion(f32[864]{0:T(1024)S(1)} %copy-done.4, bf16[512,9216]{1,0:T(8,128)(2,1)S(1)} %constant_dynamic-update-slice_fusion.images_ref, bf16[864,9216]{1,0:T(8,128)(2,1)} %param.8), kind=kOutput, calls=%fused_computation.47 | convolution fusion | flops 8154611200 | bytes 27137408 | tf_op jit(solution)/shard_map/dot_general | solution.py:139
  62.4 1.0 gather_fusion
  63.7 9.2 %all-gather.1 = f32[8,2,512]{2,1,0:T(2,128)S(1)} all-gather(f32[1,2,512]{2,1,0:T(2,128)S(1)} %copy.20), channel_id=2, replica_groups=mesh['img'=4,'ref'=8] {'ref'}, dimensions={0}, use_global_device_ids=true | all-gather | bytes 36864 | tf_op jit(solution)/shard_map/all_gather | solution.py:146
  73.1 1.0 gather_fusion.1
  75.1 1.2 %copy.24 = bf16[36,24,512]{2,1,0:T(8,128)(2,1)} copy(bf16[36,24,512]{2,0,1:T(8,128)(2,1)S(1)} %bitcast.45) | data formatting | bytes 1769472 | tf_op jit(solution)/shard_map/transpose | solution.py:154
  76.3 11.6 %shard_map.69 = f32[3,24,2432]{2,1,0:T(8,128)} custom-call(s32[1]{0:T(128)} %bitcast.me_ref, bf16[864,512]{1,0:T(8,128)(2,1)} %bitcast.46, bf16[512,9216]{1,0:T(8,128)(2,1)} %copy-done, s32[1,2304]{1,0:T(1,128)} %and_select_fusion.angle_ref), custom_call_target="tpu_custom_call" | custom-call | flops 6115295232 | bytes 8626176 | tf_op jit(solution)/shard_map/pallas_call | solution.py:56
  87.9 1.2 %slice_bitcast_fusion.2 = (f32[24,2432]{1,0:T(8,128)S(1)}, f32[24,2432]{1,0:T(8,128)S(1)}, f32[24,2432]{1,0:T(8,128)S(1)}) fusion(f32[3,24,2432]{2,1,0:T(8,128)} %shard_map.69), kind=kLoop, calls=%fused_computation.13 | loop fusion | bytes 1400832 | tf_op jit(solution)/shard_map/squeeze | solution.py:160
  89.2 2.4 %collective-permute-start.11 = (f32[24,2432]{1,0:T(8,128)S(1)}, f32[24,2432]{1,0:T(8,128)S(1)}, u32[]{:S(2)}, u32[]{:S(2)}) collective-permute-start(f32[24,2432]{1,0:T(8,128)S(1)} %get-tuple-element.6), channel_id=1, source_target_pairs={{0,24},{8,0},{16,8},{24,16},{1,25},{9,1},{17,9},{25,17},{2,26},{10... | collective-permute-start | bytes 700424 | tf_op jit(solution)/shard_map/ppermute | solution.py:160
  91.7 5.5 %shard_map.68 = f32[1,24,2432]{2,1,0:T(8,128)} custom-call(s32[1]{0:T(128)} %bitcast.me_ref, bf16[864,512]{1,0:T(8,128)(2,1)} %bitcast.47, bf16[512,9216]{1,0:T(8,128)(2,1)} %copy-done, s32[1,2304]{1,0:T(1,128)} %and_select_fusion.angle_ref), custom_call_target="tpu_custom_call" | custom-call | flops 2038431744 | bytes 3465216 | tf_op jit(solution)/shard_map/pallas_call | solution.py:56
  97.2 2.0 %collective-permute-done.10 = f32[24,2432]{1,0:T(8,128)S(1)} collective-permute-done((f32[24,2432]{1,0:T(8,128)S(1)}, f32[24,2432]{1,0:T(8,128)S(1)}, u32[]{:S(2)}, u32[]{:S(2)}) %collective-permute-start.10) | collective-permute-done | bytes 233504 | tf_op jit(solution)/shard_map/ppermute | solution.py:160
  99.2 10.0 %collective-permute-done.11 = f32[24,2432]{1,0:T(8,128)S(1)} collective-permute-done((f32[24,2432]{1,0:T(8,128)S(1)}, f32[24,2432]{1,0:T(8,128)S(1)}, u32[]{:S(2)}, u32[]{:S(2)}) %collective-permute-start.11) | collective-permute-done | bytes 233504 | tf_op jit(solution)/shard_map/ppermute | solution.py:160
  109.2 3.6 %collective-permute-done.9 = f32[24,2432]{1,0:T(8,128)S(1)} collective-permute-done((f32[24,2432]{1,0:T(8,128)S(1)}, f32[24,2432]{1,0:T(8,128)S(1)}, u32[]{:S(2)}, u32[]{:S(2)}) %collective-permute-start.9) | collective-permute-done | bytes 233504 | tf_op jit(solution)/shard_map/ppermute | solution.py:160
  112.8 1.0 fusion.2
  113.8 0.7 slice.58
  114.5 0.6 slice_reduce_fusion.2
  (55 shorter events, 3.9 us)
Async XLA Ops:
  0.6 15.0 %copy-start.1 = (bf16[64,9216]{1,0:T(8,128)(2,1)S(1)}, bf16[64,9216]{1,0:T(8,128)(2,1)}, u32[]{:S(2)}) copy-start(bf16[64,9216]{1,0:T(8,128)(2,1)} %param.7) | copy-start | bytes 3538948
  0.6 27.1 %collective-permute-start = (bf16[64,9216]{1,0:T(8,128)(2,1)}, bf16[64,9216]{1,0:T(8,128)(2,1)S(1)}, u32[]{:S(2)}, u32[]{:S(2)}) collective-permute-start(bf16[64,9216]{1,0:T(8,128)(2,1)} %param.7), channel_id=1, source_target_pairs={{0,2},{1,3},{2,6},{3,7},{4,0},{5,1},{6,4},{7,5},{8,10},{9,11},{10,... | collective-permute-start | bytes 3538952 | tf_op jit(solution)/shard_map/ppermute | solution.py:103
  1.9 27.1 %collective-permute-start.1 = (bf16[64,9216]{1,0:T(8,128)(2,1)}, bf16[64,9216]{1,0:T(8,128)(2,1)S(1)}, u32[]{:S(2)}, u32[]{:S(2)}) collective-permute-start(bf16[64,9216]{1,0:T(8,128)(2,1)} %param.7), channel_id=1, source_target_pairs={{0,4},{1,5},{2,0},{3,1},{4,6},{5,7},{6,2},{7,3},{8,12},{9,13},{10,... | collective-permute-start | bytes 3538952 | tf_op jit(solution)/shard_map/ppermute | solution.py:104
  2.2 42.8 %collective-permute-start.4 = (bf16[64,9216]{1,0:T(8,128)(2,1)}, bf16[64,9216]{1,0:T(8,128)(2,1)}, u32[]{:S(2)}, u32[]{:S(2)}) collective-permute-start(bf16[64,9216]{1,0:T(8,128)(2,1)} %param.7), channel_id=1, source_target_pairs={{0,1},{1,0},{2,3},{3,2},{4,5},{5,4},{6,7},{7,6},{8,9},{9,8},{10,11... | collective-permute-start | bytes 3538952 | tf_op jit(solution)/shard_map/ppermute | solution.py:112
  7.9 7.6 %copy-start.3 = (s32[512]{0:T(512)S(1)}, s32[512]{0:T(512)}, u32[]{:S(2)}) copy-start(s32[512]{0:T(512)} %compare_select_fusion.1) | copy-start | bytes 6148
  7.9 7.6 %copy-start.2 = (s32[512]{0:T(512)S(1)}, s32[512]{0:T(512)}, u32[]{:S(2)}) copy-start(s32[512]{0:T(512)} %compare_select_fusion) | copy-start | bytes 6148
  15.7 30.9 %copy-start.4 = (f32[864]{0:T(1024)S(1)}, f32[864]{0:T(1024)}, u32[]{:S(2)}) copy-start(f32[864]{0:T(1024)} %multiply_subtract_fusion) | copy-start | bytes 10372
  27.8 13.3 %collective-permute-start.2 = (bf16[32,9216]{1,0:T(8,128)(2,1)S(1)}, bf16[32,9216]{1,0:T(8,128)(2,1)S(1)}, u32[]{:S(2)}, u32[]{:S(2)}) collective-permute-start(bf16[32,9216]{1,0:T(8,128)(2,1)S(1)} %slice.49), channel_id=1, source_target_pairs={{0,2},{1,3},{2,6},{3,7},{4,0},{5,1},{6,4},{7,5},{8,10},{9,11},{10,... | collective-permute-start | bytes 1769480 | tf_op jit(solution)/shard_map/ppermute | solution.py:108
  29.1 14.5 %collective-permute-start.3 = (bf16[32,9216]{1,0:T(8,128)(2,1)S(1)}, bf16[32,9216]{1,0:T(8,128)(2,1)S(1)}, u32[]{:S(2)}, u32[]{:S(2)}) collective-permute-start(bf16[32,9216]{1,0:T(8,128)(2,1)S(1)} %slice.50), channel_id=1, source_target_pairs={{0,4},{1,5},{2,0},{3,1},{4,6},{5,7},{6,2},{7,3},{8,12},{9,13},{10,... | collective-permute-start | bytes 1769480 | tf_op jit(solution)/shard_map/ppermute | solution.py:109
  29.4 16.9 %collective-permute-start.5 = (bf16[64,9216]{1,0:T(8,128)(2,1)S(1)}, bf16[64,9216]{1,0:T(8,128)(2,1)S(1)}, u32[]{:S(2)}, u32[]{:S(2)}) collective-permute-start(bf16[64,9216]{1,0:T(8,128)(2,1)S(1)} %collective-permute-done), channel_id=1, source_target_pairs={{0,1},{1,0},{2,3},{3,2},{4,5},{5,4},{6,7},{7,6},{8,9},{9,8},{10,11... | collective-permute-start | bytes 3538952 | tf_op jit(solution)/shard_map/ppermute | solution.py:112
  31.5 14.9 %collective-permute-start.6 = (bf16[64,9216]{1,0:T(8,128)(2,1)S(1)}, bf16[64,9216]{1,0:T(8,128)(2,1)S(1)}, u32[]{:S(2)}, u32[]{:S(2)}) collective-permute-start(bf16[64,9216]{1,0:T(8,128)(2,1)S(1)} %collective-permute-done.1), channel_id=1, source_target_pairs={{0,1},{1,0},{2,3},{3,2},{4,5},{5,4},{6,7},{7,6},{8,9},{9,8},{10,11... | collective-permute-start | bytes 3538952 | tf_op jit(solution)/shard_map/ppermute | solution.py:112
  41.1 5.4 %collective-permute-start.7 = (bf16[32,9216]{1,0:T(8,128)(2,1)S(1)}, bf16[32,9216]{1,0:T(8,128)(2,1)S(1)}, u32[]{:S(2)}, u32[]{:S(2)}) collective-permute-start(bf16[32,9216]{1,0:T(8,128)(2,1)S(1)} %collective-permute-done.2), channel_id=1, source_target_pairs={{0,1},{1,0},{2,3},{3,2},{4,5},{5,4},{6,7},{7,6},{8,9},{9,8},{10,11... | collective-permute-start | bytes 1769480 | tf_op jit(solution)/shard_map/ppermute | solution.py:112
  43.6 2.9 %collective-permute-start.8 = (bf16[32,9216]{1,0:T(8,128)(2,1)S(1)}, bf16[32,9216]{1,0:T(8,128)(2,1)S(1)}, u32[]{:S(2)}, u32[]{:S(2)}) collective-permute-start(bf16[32,9216]{1,0:T(8,128)(2,1)S(1)} %collective-permute-done.3), channel_id=1, source_target_pairs={{0,1},{1,0},{2,3},{3,2},{4,5},{5,4},{6,7},{7,6},{8,9},{9,8},{10,11... | collective-permute-start | bytes 1769480 | tf_op jit(solution)/shard_map/ppermute | solution.py:112
  46.6 15.3 %copy-start = (bf16[512,9216]{1,0:T(8,128)(2,1)}, bf16[512,9216]{1,0:T(8,128)(2,1)S(1)}, u32[]{:S(2)}) copy-start(bf16[512,9216]{1,0:T(8,128)(2,1)S(1)} %constant_dynamic-update-slice_fusion.images_ref) | copy-start | bytes 28311556
  46.6 16.8 %copy-start.6 = (pred[512]{0:T(512)(128)(4,1)S(1)}, pred[512]{0:T(512)(128)(4,1)}, u32[]{:S(2)}) copy-start(pred[512]{0:T(512)(128)(4,1)} %compare_and_fusion.1) | copy-start | bytes 1540
  46.6 27.5 %copy-start.5 = (pred[512]{0:T(512)(128)(4,1)S(1)}, pred[512]{0:T(512)(128)(4,1)}, u32[]{:S(2)}) copy-start(pred[512]{0:T(512)(128)(4,1)} %compare_and_fusion) | copy-start | bytes 1540
  89.1 10.1 %collective-permute-start.10 = (f32[24,2432]{1,0:T(8,128)S(1)}, f32[24,2432]{1,0:T(8,128)S(1)}, u32[]{:S(2)}, u32[]{:S(2)}) collective-permute-start(f32[24,2432]{1,0:T(8,128)S(1)} %get-tuple-element.7), channel_id=1, source_target_pairs={{0,16},{8,24},{16,0},{24,8},{1,17},{9,25},{17,1},{25,9},{2,18},{10... | collective-permute-start | bytes 700424 | tf_op jit(solution)/shard_map/ppermute | solution.py:160
  89.2 20.0 %collective-permute-start.11 = (f32[24,2432]{1,0:T(8,128)S(1)}, f32[24,2432]{1,0:T(8,128)S(1)}, u32[]{:S(2)}, u32[]{:S(2)}) collective-permute-start(f32[24,2432]{1,0:T(8,128)S(1)} %get-tuple-element.6), channel_id=1, source_target_pairs={{0,24},{8,0},{16,8},{24,16},{1,25},{9,1},{17,9},{25,17},{2,26},{10... | collective-permute-start | bytes 700424 | tf_op jit(solution)/shard_map/ppermute | solution.py:160
  91.7 21.1 %collective-permute-start.9 = (f32[24,2432]{1,0:T(8,128)S(1)}, f32[24,2432]{1,0:T(8,128)S(1)}, u32[]{:S(2)}, u32[]{:S(2)}) collective-permute-start(f32[24,2432]{1,0:T(8,128)S(1)} %get-tuple-element.5), channel_id=1, source_target_pairs={{0,8},{8,16},{16,24},{24,0},{1,9},{9,17},{17,25},{25,1},{2,10},{10... | collective-permute-start | bytes 700424 | tf_op jit(solution)/shard_map/ppermute | solution.py:160

commit v14 on v13

--- a/solution.py
+++ b/solution.py
@@ -13,9 +13,8 @@
 GROUP_COLS = 1152
 
 
-def turn_sum_kernel(
-    classes_here, rotations, me_ref, by_turn_ref, images_ref, angle_ref, out_ref, products_ref
-):
+def turn_sum_kernel(classes_here, rotations, count, me_ref, by_turn_ref, images_ref, angle_ref, *rest):
+    out_refs, products_ref, out_ref = rest[:count], rest[count], rest[count + 1]
     shift = ANG // rotations
     width = images_ref.shape[1]
     products_ref[...] = jnp.dot(
@@ -36,12 +35,18 @@
                 kept = kept + jnp.where(angle < ANG - step, ahead, 0.0)
                 every = ahead if every is None else every + ahead
             wrapped = every - (kept - products_ref[row0 : row0 + rows, col0 : col0 + cols])
-            out_ref[0, row0 : row0 + rows, col0 : col0 + cols] = kept + pltpu.roll(wrapped, ANG, 1)
+            out_ref[row0 : row0 + rows, col0 : col0 + cols] = kept + pltpu.roll(wrapped, ANG, 1)
     mass = jnp.sum(by_turn_ref[...].astype(jnp.float32), axis=1, keepdims=True)
     class_mass = mass[0:classes_here]
     for turn_index in range(1, rotations):
         class_mass = class_mass + mass[turn_index * classes_here : (turn_index + 1) * classes_here]
-    out_ref[0, :, width:] = jnp.broadcast_to(class_mass, (classes_here, LANES))
+    out_ref[:, width:] = jnp.broadcast_to(class_mass, (classes_here, LANES))
+    step = pl.program_id(0)
+    for index, target in enumerate(out_refs):
+
+        @pl.when(step == index)
+        def _():
+            target[...] = out_ref[...]
 
 
 def turn_and_sum(by_turn, gathered, classes_here, rotations, chunks, me, first, count):
@@ -54,7 +59,7 @@
         return (0, (me_ref[0] + first + t) % chunks)
 
     return pl.pallas_call(
-        functools.partial(turn_sum_kernel, classes_here, rotations),
+        functools.partial(turn_sum_kernel, classes_here, rotations, count),
         grid_spec=pltpu.PrefetchScalarGridSpec(
             num_scalar_prefetch=1,
             grid=(count,),
@@ -63,10 +68,18 @@
                 pl.BlockSpec((n, width), chunk_of),
                 pl.BlockSpec((1, width), lambda t, me_ref: (0, 0)),
             ],
-            out_specs=pl.BlockSpec((1, classes_here, width + LANES), lambda t, me_ref: (t, 0, 0)),
-            scratch_shapes=[pltpu.VMEM((local_refs, width), jnp.float32)],
+            out_specs=[
+                pl.BlockSpec((classes_here, width + LANES), lambda t, me_ref: (0, 0))
+                for _ in range(count)
+            ],
+            scratch_shapes=[
+                pltpu.VMEM((local_refs, width), jnp.float32),
+                pltpu.VMEM((classes_here, width + LANES), jnp.float32),
+            ],
         ),
-        out_shape=jax.ShapeDtypeStruct((count, classes_here, width + LANES), jnp.float32),
+        out_shape=[
+            jax.ShapeDtypeStruct((classes_here, width + LANES), jnp.float32) for _ in range(count)
+        ],
         compiler_params=pltpu.CompilerParams(vmem_limit_bytes=60 * 1024 * 1024),
         cost_estimate=pl.CostEstimate(
             flops=2 * local_refs * n * width * count,

time: 115 us -> 115 us (level)
  local copies, waits for them, and re-layouts: 10.2 us -> 9.01 us
    squeeze x1 -> x0, local copies, waits for them, and re-layouts: 1.21 us -> none  [per_device(): outgoing[step - 1]]
where the time goes in v14:
time: 115 us; the launch traced here: 114 us
  waiting for transfers between devices  37.3 us (32%)
  Pallas kernels  17.4 us (15%)
  matrix products  15.2 us (13%)
  starting transfers between devices  12.6 us (11%)
  other arithmetic  12.5 us (11%)
  blocking collectives  9.22 us (8%)
  local copies, waits for them, and re-layouts  9.01 us (8%)
    pallas_call x2, Pallas kernels, turn_and_sum(): pl.pallas_call(functools.partial(turn_sum_kernel, classes_here, rotations...  17.4 us
    ppermute x3, waiting for transfers between devices, per_device(): lax.ppermute(outgoing[step - 1], 'img', [(src, (src + step) % chunks) for...  15.8 us
    dot_general x1, matrix products, per_device(): lax.dot_general(gathered, references, (((1,), (1,)), ((), ())), preferred...  15.2 us
    ppermute x1, waiting for transfers between devices, ring_gather(): from_prev = lax.ppermute(from_prev, 'ref', to_next)  12.1 us
    ppermute x1, waiting for transfers between devices, ring_gather(): top = lax.ppermute(from_prev[:half], 'ref', to_next)  9.43 us
    all_gather x1, blocking collectives, per_device(): stats = lax.all_gather(in_group_order, 'ref', axis=0)  9.22 us
    ppermute x5, starting transfers between devices, ring_gather(): arrays += [lax.ppermute(piece[0], 'ref', to_partner) for piece in pieces]  7.07 us
    dot_general x1, other arithmetic, per_device(): jnp.einsum('jp,jp->j', references, references, preferred_element_type=jnp...  7 us
  transfers between devices with their start and end apart: 12, of which 5 were waited for; matrix products, arithmetic and copies ran while one was open for 12% of the time, Pallas kernels for 5%

profile of v14, /device:TPU:17, one launch (start us, length us, event | category | flops | bytes accessed | tf_op | source)
XLA Modules:
  0.0 114.3 jit_solution(3796399945176196373)
XLA Ops:
  0.6 1.3 %collective-permute-start = (bf16[64,9216]{1,0:T(8,128)(2,1)}, bf16[64,9216]{1,0:T(8,128)(2,1)S(1)}, u32[]{:S(2)}, u32[]{:S(2)}) collective-permute-start(bf16[64,9216]{1,0:T(8,128)(2,1)} %param.7), channel_id=1, source_target_pairs={{0,2},{1,3},{2,6},{3,7},{4,0},{5,1},{6,4},{7,5},{8,10},{9,11},{10,... | collective-permute-start | bytes 3538952 | tf_op jit(solution)/shard_map/ppermute | solution.py:116
  2.2 1.2 %collective-permute-start.4 = (bf16[64,9216]{1,0:T(8,128)(2,1)}, bf16[64,9216]{1,0:T(8,128)(2,1)}, u32[]{:S(2)}, u32[]{:S(2)}) collective-permute-start(bf16[64,9216]{1,0:T(8,128)(2,1)} %param.7), channel_id=1, source_target_pairs={{0,1},{1,0},{2,3},{3,2},{4,5},{5,4},{6,7},{7,6},{8,9},{9,8},{10,11... | collective-permute-start | bytes 3538952 | tf_op jit(solution)/shard_map/ppermute | solution.py:125
  3.4 0.7 constant_dynamic-slice_fusion
  4.1 0.6 compare_select_fusion.1
  4.7 0.6 compare_and_fusion.1
  5.3 0.6 compare_select_fusion
  5.9 0.6 compare_and_fusion
  6.5 0.6 and_select_fusion.angle_ref
  7.1 0.7 log.3
  7.9 7.0 %fusion = f32[864]{0:T(1024)S(1)} fusion(bf16[864,9216]{1,0:T(8,128)(2,1)} %param.8), kind=kLoop, calls=%fused_computation.3 | loop fusion | flops 23887008 | bytes 15928704 | tf_op jit(solution)/shard_map/jp,jp->j/dot_general | solution.py:143
  14.9 0.6 multiply_subtract_fusion
  15.7 12.1 %collective-permute-done = bf16[64,9216]{1,0:T(8,128)(2,1)S(1)} collective-permute-done((bf16[64,9216]{1,0:T(8,128)(2,1)}, bf16[64,9216]{1,0:T(8,128)(2,1)S(1)}, u32[]{:S(2)}, u32[]{:S(2)}) %collective-permute-start) | collective-permute-done | bytes 1179680 | tf_op jit(solution)/shard_map/ppermute | solution.py:116
  27.8 1.3 %collective-permute-start.2 = (bf16[32,9216]{1,0:T(8,128)(2,1)S(1)}, bf16[32,9216]{1,0:T(8,128)(2,1)S(1)}, u32[]{:S(2)}, u32[]{:S(2)}) collective-permute-start(bf16[32,9216]{1,0:T(8,128)(2,1)S(1)} %slice.37), channel_id=1, source_target_pairs={{0,2},{1,3},{2,6},{3,7},{4,0},{5,1},{6,4},{7,5},{8,10},{9,11},{10,... | collective-permute-start | bytes 1769480 | tf_op jit(solution)/shard_map/ppermute | solution.py:121
  29.4 2.1 %collective-permute-start.5 = (bf16[64,9216]{1,0:T(8,128)(2,1)S(1)}, bf16[64,9216]{1,0:T(8,128)(2,1)S(1)}, u32[]{:S(2)}, u32[]{:S(2)}) collective-permute-start(bf16[64,9216]{1,0:T(8,128)(2,1)S(1)} %collective-permute-done), channel_id=1, source_target_pairs={{0,1},{1,0},{2,3},{3,2},{4,5},{5,4},{6,7},{7,6},{8,9},{9,8},{10,11... | collective-permute-start | bytes 3538952 | tf_op jit(solution)/shard_map/ppermute | solution.py:125
  31.7 9.4 %collective-permute-done.2 = bf16[32,9216]{1,0:T(8,128)(2,1)S(1)} collective-permute-done((bf16[32,9216]{1,0:T(8,128)(2,1)S(1)}, bf16[32,9216]{1,0:T(8,128)(2,1)S(1)}, u32[]{:S(2)}, u32[]{:S(2)}) %collective-permute-start.2) | collective-permute-done | bytes 589856 | tf_op jit(solution)/shard_map/ppermute | solution.py:121
  41.1 2.5 %collective-permute-start.7 = (bf16[32,9216]{1,0:T(8,128)(2,1)S(1)}, bf16[32,9216]{1,0:T(8,128)(2,1)S(1)}, u32[]{:S(2)}, u32[]{:S(2)}) collective-permute-start(bf16[32,9216]{1,0:T(8,128)(2,1)S(1)} %collective-permute-done.2), channel_id=1, source_target_pairs={{0,1},{1,0},{2,3},{3,2},{4,5},{5,4},{6,7},{7,6},{8,9},{9,8},{10,11... | collective-permute-start | bytes 1769480 | tf_op jit(solution)/shard_map/ppermute | solution.py:125
  43.6 1.3 %collective-permute-start.8 = (bf16[32,9216]{1,0:T(8,128)(2,1)S(1)}, bf16[32,9216]{1,0:T(8,128)(2,1)S(1)}, u32[]{:S(2)}, u32[]{:S(2)}) collective-permute-start(bf16[32,9216]{1,0:T(8,128)(2,1)S(1)} %collective-permute-done.3), channel_id=1, source_target_pairs={{0,1},{1,0},{2,3},{3,2},{4,5},{5,4},{6,7},{7,6},{8,9},{9,8},{10,11... | collective-permute-start | bytes 1769480 | tf_op jit(solution)/shard_map/ppermute | solution.py:125
  44.9 1.3 %constant_dynamic-update-slice_fusion.4 = bf16[512,9216]{1,0:T(8,128)(2,1)S(1)} fusion(bf16[512,9216]{1,0:T(8,128)(2,1)S(1)} %constant_dynamic-update-slice_fusion.5, bf16[64,9216]{1,0:T(8,128)(2,1)} %collective-permute-done.4), kind=kLoop, calls=%fused_computation.17 | loop fusion | bytes 2359296
  46.6 15.2 %fusion.5 = (f32[512]{0:T(512)S(1)}, f32[512,864]{0,1:T(8,128)S(1)}) fusion(f32[864]{0:T(1024)S(1)} %copy-done.4, bf16[512,9216]{1,0:T(8,128)(2,1)S(1)} %constant_dynamic-update-slice_fusion.images_ref, bf16[864,9216]{1,0:T(8,128)(2,1)} %param.8), kind=kOutput, calls=%fused_computation.42 | convolution fusion | flops 8154611200 | bytes 27137408 | tf_op jit(solution)/shard_map/dot_general | solution.py:152
  62.4 1.0 gather_fusion
  63.7 9.2 %all-gather.1 = f32[8,2,512]{2,1,0:T(2,128)S(1)} all-gather(f32[1,2,512]{2,1,0:T(2,128)S(1)} %copy.20), channel_id=2, replica_groups=mesh['img'=4,'ref'=8] {'ref'}, dimensions={0}, use_global_device_ids=true | all-gather | bytes 36864 | tf_op jit(solution)/shard_map/all_gather | solution.py:159
  73.1 1.0 gather_fusion.1
  75.1 1.2 %copy.24 = bf16[36,24,512]{2,1,0:T(8,128)(2,1)} copy(bf16[36,24,512]{2,0,1:T(8,128)(2,1)S(1)} %bitcast.33) | data formatting | bytes 1769472 | tf_op jit(solution)/shard_map/transpose | solution.py:167
  76.3 11.9 %shard_map.69 = (f32[24,2432]{1,0:T(8,128)}, f32[24,2432]{1,0:T(8,128)}, f32[24,2432]{1,0:T(8,128)}) custom-call(s32[1]{0:T(128)} %bitcast.me_ref, bf16[864,512]{1,0:T(8,128)(2,1)} %bitcast.34, bf16[512,9216]{1,0:T(8,128)(2,1)} %copy-done, s32[1,2304]{1,0:T(1,128)} %and_select_fusion.angle_ref), custom_call_target="tpu_custom_call" | custom-call | flops 6115295232 | bytes 8626176 | tf_op jit(solution)/shard_map/pallas_call | solution.py:61
  88.2 2.4 %collective-permute-start.11 = (f32[24,2432]{1,0:T(8,128)}, f32[24,2432]{1,0:T(8,128)S(1)}, u32[]{:S(2)}, u32[]{:S(2)}) collective-permute-start(f32[24,2432]{1,0:T(8,128)} %get-tuple-element.8), channel_id=1, source_target_pairs={{0,24},{8,0},{16,8},{24,16},{1,25},{9,1},{17,9},{25,17},{2,26},{10... | collective-permute-start | bytes 700424 | tf_op jit(solution)/shard_map/ppermute | solution.py:173
  90.6 5.6 %shard_map.68 = f32[24,2432]{1,0:T(8,128)} custom-call(s32[1]{0:T(128)} %bitcast.me_ref, bf16[864,512]{1,0:T(8,128)(2,1)} %bitcast.35, bf16[512,9216]{1,0:T(8,128)(2,1)} %copy-done, s32[1,2304]{1,0:T(1,128)} %and_select_fusion.angle_ref), custom_call_target="tpu_custom_call" | custom-call | flops 2038431744 | bytes 3465216 | tf_op jit(solution)/shard_map/pallas_call | solution.py:61
  96.2 2.3 %collective-permute-done.10 = f32[24,2432]{1,0:T(8,128)S(1)} collective-permute-done((f32[24,2432]{1,0:T(8,128)}, f32[24,2432]{1,0:T(8,128)S(1)}, u32[]{:S(2)}, u32[]{:S(2)}) %collective-permute-start.10) | collective-permute-done | bytes 233504 | tf_op jit(solution)/shard_map/ppermute | solution.py:173
  98.5 10.0 %collective-permute-done.11 = f32[24,2432]{1,0:T(8,128)S(1)} collective-permute-done((f32[24,2432]{1,0:T(8,128)}, f32[24,2432]{1,0:T(8,128)S(1)}, u32[]{:S(2)}, u32[]{:S(2)}) %collective-permute-start.11) | collective-permute-done | bytes 233504 | tf_op jit(solution)/shard_map/ppermute | solution.py:173
  108.5 3.5 %collective-permute-done.9 = f32[24,2432]{1,0:T(8,128)S(1)} collective-permute-done((f32[24,2432]{1,0:T(8,128)}, f32[24,2432]{1,0:T(8,128)S(1)}, u32[]{:S(2)}, u32[]{:S(2)}) %collective-permute-start.9) | collective-permute-done | bytes 233504 | tf_op jit(solution)/shard_map/ppermute | solution.py:173
  112.0 1.0 add_add_fusion
  113.0 0.7 slice.43
  113.7 0.6 slice_reduce_fusion.2
  (54 shorter events, 3.3 us)
Async XLA Ops:
  0.6 15.0 %copy-start.1 = (bf16[64,9216]{1,0:T(8,128)(2,1)S(1)}, bf16[64,9216]{1,0:T(8,128)(2,1)}, u32[]{:S(2)}) copy-start(bf16[64,9216]{1,0:T(8,128)(2,1)} %param.7) | copy-start | bytes 3538948
  0.6 27.1 %collective-permute-start = (bf16[64,9216]{1,0:T(8,128)(2,1)}, bf16[64,9216]{1,0:T(8,128)(2,1)S(1)}, u32[]{:S(2)}, u32[]{:S(2)}) collective-permute-start(bf16[64,9216]{1,0:T(8,128)(2,1)} %param.7), channel_id=1, source_target_pairs={{0,2},{1,3},{2,6},{3,7},{4,0},{5,1},{6,4},{7,5},{8,10},{9,11},{10,... | collective-permute-start | bytes 3538952 | tf_op jit(solution)/shard_map/ppermute | solution.py:116
  1.9 27.1 %collective-permute-start.1 = (bf16[64,9216]{1,0:T(8,128)(2,1)}, bf16[64,9216]{1,0:T(8,128)(2,1)S(1)}, u32[]{:S(2)}, u32[]{:S(2)}) collective-permute-start(bf16[64,9216]{1,0:T(8,128)(2,1)} %param.7), channel_id=1, source_target_pairs={{0,4},{1,5},{2,0},{3,1},{4,6},{5,7},{6,2},{7,3},{8,12},{9,13},{10,... | collective-permute-start | bytes 3538952 | tf_op jit(solution)/shard_map/ppermute | solution.py:117
  2.2 42.8 %collective-permute-start.4 = (bf16[64,9216]{1,0:T(8,128)(2,1)}, bf16[64,9216]{1,0:T(8,128)(2,1)}, u32[]{:S(2)}, u32[]{:S(2)}) collective-permute-start(bf16[64,9216]{1,0:T(8,128)(2,1)} %param.7), channel_id=1, source_target_pairs={{0,1},{1,0},{2,3},{3,2},{4,5},{5,4},{6,7},{7,6},{8,9},{9,8},{10,11... | collective-permute-start | bytes 3538952 | tf_op jit(solution)/shard_map/ppermute | solution.py:125
  7.9 7.6 %copy-start.3 = (s32[512]{0:T(512)S(1)}, s32[512]{0:T(512)}, u32[]{:S(2)}) copy-start(s32[512]{0:T(512)} %compare_select_fusion.1) | copy-start | bytes 6148
  7.9 7.6 %copy-start.2 = (s32[512]{0:T(512)S(1)}, s32[512]{0:T(512)}, u32[]{:S(2)}) copy-start(s32[512]{0:T(512)} %compare_select_fusion) | copy-start | bytes 6148
  15.7 30.9 %copy-start.4 = (f32[864]{0:T(1024)S(1)}, f32[864]{0:T(1024)}, u32[]{:S(2)}) copy-start(f32[864]{0:T(1024)} %multiply_subtract_fusion) | copy-start | bytes 10372
  27.8 13.3 %collective-permute-start.2 = (bf16[32,9216]{1,0:T(8,128)(2,1)S(1)}, bf16[32,9216]{1,0:T(8,128)(2,1)S(1)}, u32[]{:S(2)}, u32[]{:S(2)}) collective-permute-start(bf16[32,9216]{1,0:T(8,128)(2,1)S(1)} %slice.37), channel_id=1, source_target_pairs={{0,2},{1,3},{2,6},{3,7},{4,0},{5,1},{6,4},{7,5},{8,10},{9,11},{10,... | collective-permute-start | bytes 1769480 | tf_op jit(solution)/shard_map/ppermute | solution.py:121
  29.1 14.5 %collective-permute-start.3 = (bf16[32,9216]{1,0:T(8,128)(2,1)S(1)}, bf16[32,9216]{1,0:T(8,128)(2,1)S(1)}, u32[]{:S(2)}, u32[]{:S(2)}) collective-permute-start(bf16[32,9216]{1,0:T(8,128)(2,1)S(1)} %slice.38), channel_id=1, source_target_pairs={{0,4},{1,5},{2,0},{3,1},{4,6},{5,7},{6,2},{7,3},{8,12},{9,13},{10,... | collective-permute-start | bytes 1769480 | tf_op jit(solution)/shard_map/ppermute | solution.py:122
  29.4 16.9 %collective-permute-start.5 = (bf16[64,9216]{1,0:T(8,128)(2,1)S(1)}, bf16[64,9216]{1,0:T(8,128)(2,1)S(1)}, u32[]{:S(2)}, u32[]{:S(2)}) collective-permute-start(bf16[64,9216]{1,0:T(8,128)(2,1)S(1)} %collective-permute-done), channel_id=1, source_target_pairs={{0,1},{1,0},{2,3},{3,2},{4,5},{5,4},{6,7},{7,6},{8,9},{9,8},{10,11... | collective-permute-start | bytes 3538952 | tf_op jit(solution)/shard_map/ppermute | solution.py:125
  31.5 14.9 %collective-permute-start.6 = (bf16[64,9216]{1,0:T(8,128)(2,1)S(1)}, bf16[64,9216]{1,0:T(8,128)(2,1)S(1)}, u32[]{:S(2)}, u32[]{:S(2)}) collective-permute-start(bf16[64,9216]{1,0:T(8,128)(2,1)S(1)} %collective-permute-done.1), channel_id=1, source_target_pairs={{0,1},{1,0},{2,3},{3,2},{4,5},{5,4},{6,7},{7,6},{8,9},{9,8},{10,11... | collective-permute-start | bytes 3538952 | tf_op jit(solution)/shard_map/ppermute | solution.py:125
  41.1 5.4 %collective-permute-start.7 = (bf16[32,9216]{1,0:T(8,128)(2,1)S(1)}, bf16[32,9216]{1,0:T(8,128)(2,1)S(1)}, u32[]{:S(2)}, u32[]{:S(2)}) collective-permute-start(bf16[32,9216]{1,0:T(8,128)(2,1)S(1)} %collective-permute-done.2), channel_id=1, source_target_pairs={{0,1},{1,0},{2,3},{3,2},{4,5},{5,4},{6,7},{7,6},{8,9},{9,8},{10,11... | collective-permute-start | bytes 1769480 | tf_op jit(solution)/shard_map/ppermute | solution.py:125
  43.6 2.9 %collective-permute-start.8 = (bf16[32,9216]{1,0:T(8,128)(2,1)S(1)}, bf16[32,9216]{1,0:T(8,128)(2,1)S(1)}, u32[]{:S(2)}, u32[]{:S(2)}) collective-permute-start(bf16[32,9216]{1,0:T(8,128)(2,1)S(1)} %collective-permute-done.3), channel_id=1, source_target_pairs={{0,1},{1,0},{2,3},{3,2},{4,5},{5,4},{6,7},{7,6},{8,9},{9,8},{10,11... | collective-permute-start | bytes 1769480 | tf_op jit(solution)/shard_map/ppermute | solution.py:125
  46.6 15.3 %copy-start = (bf16[512,9216]{1,0:T(8,128)(2,1)}, bf16[512,9216]{1,0:T(8,128)(2,1)S(1)}, u32[]{:S(2)}) copy-start(bf16[512,9216]{1,0:T(8,128)(2,1)S(1)} %constant_dynamic-update-slice_fusion.images_ref) | copy-start | bytes 28311556
  46.6 16.8 %copy-start.6 = (pred[512]{0:T(512)(128)(4,1)S(1)}, pred[512]{0:T(512)(128)(4,1)}, u32[]{:S(2)}) copy-start(pred[512]{0:T(512)(128)(4,1)} %compare_and_fusion.1) | copy-start | bytes 1540
  46.6 27.5 %copy-start.5 = (pred[512]{0:T(512)(128)(4,1)S(1)}, pred[512]{0:T(512)(128)(4,1)}, u32[]{:S(2)}) copy-start(pred[512]{0:T(512)(128)(4,1)} %compare_and_fusion) | copy-start | bytes 1540
  88.1 10.3 %collective-permute-start.10 = (f32[24,2432]{1,0:T(8,128)}, f32[24,2432]{1,0:T(8,128)S(1)}, u32[]{:S(2)}, u32[]{:S(2)}) collective-permute-start(f32[24,2432]{1,0:T(8,128)} %get-tuple-element.7), channel_id=1, source_target_pairs={{0,16},{8,24},{16,0},{24,8},{1,17},{9,25},{17,1},{25,9},{2,18},{10... | collective-permute-start | bytes 700424 | tf_op jit(solution)/shard_map/ppermute | solution.py:173
  88.2 20.3 %collective-permute-start.11 = (f32[24,2432]{1,0:T(8,128)}, f32[24,2432]{1,0:T(8,128)S(1)}, u32[]{:S(2)}, u32[]{:S(2)}) collective-permute-start(f32[24,2432]{1,0:T(8,128)} %get-tuple-element.8), channel_id=1, source_target_pairs={{0,24},{8,0},{16,8},{24,16},{1,25},{9,1},{17,9},{25,17},{2,26},{10... | collective-permute-start | bytes 700424 | tf_op jit(solution)/shard_map/ppermute | solution.py:173
  90.6 21.3 %collective-permute-start.9 = (f32[24,2432]{1,0:T(8,128)}, f32[24,2432]{1,0:T(8,128)S(1)}, u32[]{:S(2)}, u32[]{:S(2)}) collective-permute-start(f32[24,2432]{1,0:T(8,128)} %get-tuple-element.6), channel_id=1, source_target_pairs={{0,8},{8,16},{16,24},{24,0},{1,9},{9,17},{17,25},{25,1},{2,10},{10... | collective-permute-start | bytes 700424 | tf_op jit(solution)/shard_map/ppermute | solution.py:173

commit v15 on v14

--- a/solution.py
+++ b/solution.py
@@ -147,20 +147,19 @@
         local_refs
     )
     gathered, table = ring_gather(images, n_ref)
-    to_group = jnp.asarray(table)[lax.axis_index("ref")]
-    from_group = jnp.asarray(np.argsort(table, axis=1).astype(np.int32))[lax.axis_index("ref")]
+    where = np.argsort(table, axis=1)
+    same_image = np.stack([where[:, table[device]] for device in range(n_ref)]).astype(np.int32)
+    peer_rows = jnp.asarray(same_image)[lax.axis_index("ref")]
     products = lax.dot_general(
         gathered, references, (((1,), (1,)), ((), ())), preferred_element_type=jnp.float32
     )
     scores = products + offsets
     local_max = jnp.max(scores, axis=1)
     local_sum = jnp.sum(jnp.exp(scores - local_max[:, None]), axis=1)
-    in_group_order = jnp.take(jnp.stack([local_max, local_sum]), from_group, axis=1)
-    stats = lax.all_gather(in_group_order, "ref", axis=0)
+    stats = lax.all_gather(jnp.stack([local_max, local_sum]), "ref", axis=0)
+    stats = jnp.take_along_axis(stats, jnp.broadcast_to(peer_rows[:, None, :], stats.shape), axis=2)
     top_score = jnp.max(stats[:, 0], axis=0)
     denominator = jnp.sum(stats[:, 1] * jnp.exp(stats[:, 0] - top_score[None, :]), axis=0)
-    norm = jnp.take(jnp.stack([top_score, denominator]), to_group, axis=1)
-    top_score, denominator = norm[0], norm[1]
     weights = (jnp.exp(scores - top_score[:, None]) / denominator[:, None]).astype(jnp.bfloat16)
 
     n = weights.shape[0]

time: 115 us -> 194 us (1.69)
  the two profiles are of different devices: /device:TPU:17 before, /device:TPU:0 now
where the time goes in v15:
time: 194 us; the launch traced here: 191 us
  local copies, waits for them, and re-layouts  97.3 us (50%)
  waiting for transfers between devices  33.1 us (17%)
  Pallas kernels  17.4 us (9%)
  matrix products  11.6 us (6%)
  other arithmetic  10.8 us (6%)
  starting transfers between devices  10.5 us (5%)
  blocking collectives  8.98 us (5%)
    gather x2, local copies, waits for them, and re-layouts, per_device(): jnp.take_along_axis(stats, jnp.broadcast_to(peer_rows[:, None, :], stats....  80.3 us
    pallas_call x2, Pallas kernels, turn_and_sum(): pl.pallas_call(functools.partial(turn_sum_kernel, classes_here, rotations...  17.4 us
    ppermute x1, waiting for transfers between devices, ring_gather(): from_prev = lax.ppermute(from_prev, 'ref', to_next)  13 us
    unnamed x12, local copies, waits for them, and re-layouts  11.8 us
    dot_general x1, matrix products, per_device(): lax.dot_general(gathered, references, (((1,), (1,)), ((), ())), preferred...  11.6 us
    ppermute x3, waiting for transfers between devices, per_device(): lax.ppermute(outgoing[step - 1], 'img', [(src, (src + step) % chunks) for...  10 us
    ppermute x1, waiting for transfers between devices, ring_gather(): top = lax.ppermute(from_prev[:half], 'ref', to_next)  9.66 us
    all_gather x1, blocking collectives, per_device(): stats = lax.all_gather(jnp.stack([local_max, local_sum]), 'ref', axis=0)  8.98 us
  transfers between devices with their start and end apart: 12, of which 5 were waited for; matrix products, arithmetic and copies ran while one was open for 12% of the time, Pallas kernels for 3%

profile of v15, /device:TPU:0, one launch (start us, length us, event | category | flops | bytes accessed | tf_op | source)
XLA Modules:
  0.0 190.5 jit_solution(4971804981411745549)
XLA Ops:
  0.6 3.0 %collective-permute-start = (bf16[64,9216]{1,0:T(8,128)(2,1)}, bf16[64,9216]{1,0:T(8,128)(2,1)S(1)}, u32[]{:S(2)}, u32[]{:S(2)}) collective-permute-start(bf16[64,9216]{1,0:T(8,128)(2,1)} %param.4), channel_id=1, source_target_pairs={{0,2},{1,3},{2,6},{3,7},{4,0},{5,1},{6,4},{7,5},{8,10},{9,11},{10,... | collective-permute-start | bytes 3538952 | tf_op jit(solution)/shard_map/ppermute | solution.py:116
  3.7 0.7 dynamic-slice_bitcast_fusion
  4.4 0.7 fusion.5
  5.2 0.7 fusion.6
  6.5 0.7 log.3
  7.3 7.0 %fusion = f32[864]{0:T(1024)S(1)} fusion(bf16[864,9216]{1,0:T(8,128)(2,1)} %param.5), kind=kLoop, calls=%fused_computation.2 | loop fusion | flops 23887008 | bytes 15928704 | tf_op jit(solution)/shard_map/jp,jp->j/dot_general | solution.py:143
  14.4 2.4 %constant_dynamic-update-slice_fusion.9 = bf16[512,9216]{1,0:T(8,128)(2,1)} fusion(bf16[64,9216]{1,0:T(8,128)(2,1)} %param.4), kind=kLoop, calls=%fused_computation.19 | loop fusion | bytes 2359296
  16.8 13.0 %collective-permute-done = bf16[64,9216]{1,0:T(8,128)(2,1)S(1)} collective-permute-done((bf16[64,9216]{1,0:T(8,128)(2,1)}, bf16[64,9216]{1,0:T(8,128)(2,1)S(1)}, u32[]{:S(2)}, u32[]{:S(2)}) %collective-permute-start) | collective-permute-done | bytes 1179680 | tf_op jit(solution)/shard_map/ppermute | solution.py:116
  29.9 1.8 collective-permute-start.2
  32.6 1.1 constant_dynamic-update-slice_fusion.8
  33.7 1.1 constant_dynamic-update-slice_fusion.7
  34.8 9.7 %collective-permute-done.2 = bf16[32,9216]{1,0:T(8,128)(2,1)S(1)} collective-permute-done((bf16[32,9216]{1,0:T(8,128)(2,1)S(1)}, bf16[32,9216]{1,0:T(8,128)(2,1)S(1)}, u32[]{:S(2)}, u32[]{:S(2)}) %collective-permute-start.2) | collective-permute-done | bytes 589856 | tf_op jit(solution)/shard_map/ppermute | solution.py:121
  44.4 0.9 constant_dynamic-update-slice_fusion.6
  45.8 0.9 constant_dynamic-update-slice_fusion.5
  46.7 2.4 %constant_dynamic-update-slice_fusion.4 = bf16[512,9216]{1,0:T(8,128)(2,1)} fusion(bf16[512,9216]{1,0:T(8,128)(2,1)} %constant_dynamic-update-slice_fusion.5, bf16[64,9216]{1,0:T(8,128)(2,1)} %collective-permute-done.4), kind=kLoop, calls=%fused_computation.14 | loop fusion | bytes 2359296
  49.1 1.1 constant_dynamic-update-slice_fusion.3
  50.2 1.1 constant_dynamic-update-slice_fusion.2
  51.3 0.9 constant_dynamic-update-slice_fusion.1
  52.2 0.9 constant_dynamic-update-slice_fusion.images_ref
  53.1 11.6 %fusion.7 = (f32[512]{0:T(512)S(1)}, f32[512,864]{0,1:T(8,128)S(1)}) fusion(f32[864]{0:T(1024)S(1)} %multiply_subtract_fusion, bf16[512,9216]{1,0:T(8,128)(2,1)} %constant_dynamic-update-slice_fusion.images_ref, bf16[864,9216]{1,0:T(8,128)(2,1)S(1)} %copy-done), kind=kOutput, calls=%fused_computation.32 | convolution fusion | flops 8154611200 | bytes 27137408 | tf_op jit(solution)/shard_map/dot_general | solution.py:153
  65.1 9.0 %all-gather.1 = f32[8,2,512]{2,1,0:T(2,128)S(1)} all-gather(f32[1,2,512]{2,1,0:T(2,128)S(1)} %maximum_bitcast_fusion), channel_id=2, replica_groups=mesh['img'=4,'ref'=8] {'ref'}, dimensions={0}, use_global_device_ids=true | all-gather | bytes 36864 | tf_op jit(solution)/shard_map/all_gather | solution.py:159
  74.0 80.3 %gather_fusion = f32[8192]{0:T(1024)S(1)} fusion(f32[8,2,512]{2,1,0:T(2,128)S(1)} %all-gather.1, s32[8192]{0:T(1024)S(1)} %bitcast.33), kind=kCustom, calls=%fused_computation | custom fusion | bytes 163840 | tf_op jit(solution)/shard_map/jit(take_along_axis)/gather | solution.py:160
  155.0 1.2 copy.14
  156.1 11.9 %shard_map.60 = (f32[24,2432]{1,0:T(8,128)}, f32[24,2432]{1,0:T(8,128)}, f32[24,2432]{1,0:T(8,128)}) custom-call(s32[1]{0:T(128)} %bitcast.me_ref, bf16[864,512]{1,0:T(8,128)(2,1)} %bitcast.35, bf16[512,9216]{1,0:T(8,128)(2,1)} %constant_dynamic-update-slice_fusion.images_ref, s32[1,2304]{1,0:T(1,128)} %and_select_fusion.1.angle_ref), custom_call_target="tpu_custom_call" | custom-call | flops 6115295232 | bytes 8626176 | tf_op jit(solution)/shard_map/pallas_call | solution.py:61
  168.0 2.6 %collective-permute-start.10 = (f32[24,2432]{1,0:T(8,128)}, f32[24,2432]{1,0:T(8,128)S(1)}, u32[]{:S(2)}, u32[]{:S(2)}) collective-permute-start(f32[24,2432]{1,0:T(8,128)} %get-tuple-element.6), channel_id=1, source_target_pairs={{0,16},{8,24},{16,0},{24,8},{1,17},{9,25},{17,1},{25,9},{2,18},{10... | collective-permute-start | bytes 700424 | tf_op jit(solution)/shard_map/ppermute | solution.py:172
  170.6 1.3 collective-permute-start.11
  171.9 0.7 collective-permute-start.9
  172.6 5.6 %shard_map.59 = f32[24,2432]{1,0:T(8,128)} custom-call(s32[1]{0:T(128)} %bitcast.me_ref, bf16[864,512]{1,0:T(8,128)(2,1)} %bitcast.36, bf16[512,9216]{1,0:T(8,128)(2,1)} %constant_dynamic-update-slice_fusion.images_ref, s32[1,2304]{1,0:T(1,128)} %and_select_fusion.1.angle_ref), custom_call_target="tpu_custom_call" | custom-call | flops 2038431744 | bytes 3465216 | tf_op jit(solution)/shard_map/pallas_call | solution.py:61
  178.2 4.7 %collective-permute-done.10 = f32[24,2432]{1,0:T(8,128)S(1)} collective-permute-done((f32[24,2432]{1,0:T(8,128)}, f32[24,2432]{1,0:T(8,128)S(1)}, u32[]{:S(2)}, u32[]{:S(2)}) %collective-permute-start.10) | collective-permute-done | bytes 233504 | tf_op jit(solution)/shard_map/ppermute | solution.py:172
  182.8 5.4 %collective-permute-done.9 = f32[24,2432]{1,0:T(8,128)S(1)} collective-permute-done((f32[24,2432]{1,0:T(8,128)}, f32[24,2432]{1,0:T(8,128)S(1)}, u32[]{:S(2)}, u32[]{:S(2)}) %collective-permute-start.9) | collective-permute-done | bytes 233504 | tf_op jit(solution)/shard_map/ppermute | solution.py:172
  188.2 1.0 add_add_fusion
  189.2 0.7 slice.32
  (34 shorter events, 4.0 us)
Async XLA Ops:
  0.6 29.2 %collective-permute-start = (bf16[64,9216]{1,0:T(8,128)(2,1)}, bf16[64,9216]{1,0:T(8,128)(2,1)S(1)}, u32[]{:S(2)}, u32[]{:S(2)}) collective-permute-start(bf16[64,9216]{1,0:T(8,128)(2,1)} %param.4), channel_id=1, source_target_pairs={{0,2},{1,3},{2,6},{3,7},{4,0},{5,1},{6,4},{7,5},{8,10},{9,11},{10,... | collective-permute-start | bytes 3538952 | tf_op jit(solution)/shard_map/ppermute | solution.py:116
  3.6 28.0 %collective-permute-start.1 = (bf16[64,9216]{1,0:T(8,128)(2,1)}, bf16[64,9216]{1,0:T(8,128)(2,1)S(1)}, u32[]{:S(2)}, u32[]{:S(2)}) collective-permute-start(bf16[64,9216]{1,0:T(8,128)(2,1)} %param.4), channel_id=1, source_target_pairs={{0,4},{1,5},{2,0},{3,1},{4,6},{5,7},{6,2},{7,3},{8,12},{9,13},{10,... | collective-permute-start | bytes 3538952 | tf_op jit(solution)/shard_map/ppermute | solution.py:117
  3.7 42.9 %collective-permute-start.4 = (bf16[64,9216]{1,0:T(8,128)(2,1)}, bf16[64,9216]{1,0:T(8,128)(2,1)}, u32[]{:S(2)}, u32[]{:S(2)}) collective-permute-start(bf16[64,9216]{1,0:T(8,128)(2,1)} %param.4), channel_id=1, source_target_pairs={{0,1},{1,0},{2,3},{3,2},{4,5},{5,4},{6,7},{7,6},{8,9},{9,8},{10,11... | collective-permute-start | bytes 3538952 | tf_op jit(solution)/shard_map/ppermute | solution.py:125
  29.9 14.6 %collective-permute-start.2 = (bf16[32,9216]{1,0:T(8,128)(2,1)S(1)}, bf16[32,9216]{1,0:T(8,128)(2,1)S(1)}, u32[]{:S(2)}, u32[]{:S(2)}) collective-permute-start(bf16[32,9216]{1,0:T(8,128)(2,1)S(1)} %slice.28), channel_id=1, source_target_pairs={{0,2},{1,3},{2,6},{3,7},{4,0},{5,1},{6,4},{7,5},{8,10},{9,11},{10,... | collective-permute-start | bytes 1769480 | tf_op jit(solution)/shard_map/ppermute | solution.py:121
  31.7 14.0 %collective-permute-start.3 = (bf16[32,9216]{1,0:T(8,128)(2,1)S(1)}, bf16[32,9216]{1,0:T(8,128)(2,1)S(1)}, u32[]{:S(2)}, u32[]{:S(2)}) collective-permute-start(bf16[32,9216]{1,0:T(8,128)(2,1)S(1)} %slice.29), channel_id=1, source_target_pairs={{0,4},{1,5},{2,0},{3,1},{4,6},{5,7},{6,2},{7,3},{8,12},{9,13},{10,... | collective-permute-start | bytes 1769480 | tf_op jit(solution)/shard_map/ppermute | solution.py:122
  32.0 17.0 %collective-permute-start.5 = (bf16[64,9216]{1,0:T(8,128)(2,1)S(1)}, bf16[64,9216]{1,0:T(8,128)(2,1)S(1)}, u32[]{:S(2)}, u32[]{:S(2)}) collective-permute-start(bf16[64,9216]{1,0:T(8,128)(2,1)S(1)} %collective-permute-done), channel_id=1, source_target_pairs={{0,1},{1,0},{2,3},{3,2},{4,5},{5,4},{6,7},{7,6},{8,9},{9,8},{10,11... | collective-permute-start | bytes 3538952 | tf_op jit(solution)/shard_map/ppermute | solution.py:125
  32.1 18.1 %collective-permute-start.6 = (bf16[64,9216]{1,0:T(8,128)(2,1)S(1)}, bf16[64,9216]{1,0:T(8,128)(2,1)S(1)}, u32[]{:S(2)}, u32[]{:S(2)}) collective-permute-start(bf16[64,9216]{1,0:T(8,128)(2,1)S(1)} %collective-permute-done.1), channel_id=1, source_target_pairs={{0,1},{1,0},{2,3},{3,2},{4,5},{5,4},{6,7},{7,6},{8,9},{9,8},{10,11... | collective-permute-start | bytes 3538952 | tf_op jit(solution)/shard_map/ppermute | solution.py:125
  32.6 20.6 %copy-start = (bf16[864,9216]{1,0:T(8,128)(2,1)S(1)}, bf16[864,9216]{1,0:T(8,128)(2,1)}, u32[]{:S(2)}) copy-start(bf16[864,9216]{1,0:T(8,128)(2,1)} %param.5) | copy-start | bytes 47775748
  44.4 6.8 %collective-permute-start.7 = (bf16[32,9216]{1,0:T(8,128)(2,1)S(1)}, bf16[32,9216]{1,0:T(8,128)(2,1)S(1)}, u32[]{:S(2)}, u32[]{:S(2)}) collective-permute-start(bf16[32,9216]{1,0:T(8,128)(2,1)S(1)} %collective-permute-done.2), channel_id=1, source_target_pairs={{0,1},{1,0},{2,3},{3,2},{4,5},{5,4},{6,7},{7,6},{8,9},{9,8},{10,11... | collective-permute-start | bytes 1769480 | tf_op jit(solution)/shard_map/ppermute | solution.py:125
  45.6 6.5 %collective-permute-start.8 = (bf16[32,9216]{1,0:T(8,128)(2,1)S(1)}, bf16[32,9216]{1,0:T(8,128)(2,1)S(1)}, u32[]{:S(2)}, u32[]{:S(2)}) collective-permute-start(bf16[32,9216]{1,0:T(8,128)(2,1)S(1)} %collective-permute-done.3), channel_id=1, source_target_pairs={{0,1},{1,0},{2,3},{3,2},{4,5},{5,4},{6,7},{7,6},{8,9},{9,8},{10,11... | collective-permute-start | bytes 1769480 | tf_op jit(solution)/shard_map/ppermute | solution.py:125
  168.0 14.8 %collective-permute-start.10 = (f32[24,2432]{1,0:T(8,128)}, f32[24,2432]{1,0:T(8,128)S(1)}, u32[]{:S(2)}, u32[]{:S(2)}) collective-permute-start(f32[24,2432]{1,0:T(8,128)} %get-tuple-element.6), channel_id=1, source_target_pairs={{0,16},{8,24},{16,0},{24,8},{1,17},{9,25},{17,1},{25,9},{2,18},{10... | collective-permute-start | bytes 700424 | tf_op jit(solution)/shard_map/ppermute | solution.py:172
  170.6 12.2 %collective-permute-start.11 = (f32[24,2432]{1,0:T(8,128)}, f32[24,2432]{1,0:T(8,128)S(1)}, u32[]{:S(2)}, u32[]{:S(2)}) collective-permute-start(f32[24,2432]{1,0:T(8,128)} %get-tuple-element.7), channel_id=1, source_target_pairs={{0,24},{8,0},{16,8},{24,16},{1,25},{9,1},{17,9},{25,17},{2,26},{10... | collective-permute-start | bytes 700424 | tf_op jit(solution)/shard_map/ppermute | solution.py:172
  171.9 16.3 %collective-permute-start.9 = (f32[24,2432]{1,0:T(8,128)}, f32[24,2432]{1,0:T(8,128)S(1)}, u32[]{:S(2)}, u32[]{:S(2)}) collective-permute-start(f32[24,2432]{1,0:T(8,128)} %get-tuple-element.5), channel_id=1, source_target_pairs={{0,8},{8,16},{16,24},{24,0},{1,9},{9,17},{17,25},{25,1},{2,10},{10... | collective-permute-start | bytes 700424 | tf_op jit(solution)/shard_map/ppermute | solution.py:172

commit v16 on v14

--- a/solution.py
+++ b/solution.py
@@ -171,7 +171,7 @@
         outgoing = turn_and_sum(by_turn, gathered, classes_here, rotations, chunks, me, 1, chunks - 1)
         received = [
             lax.ppermute(outgoing[step - 1], "img", [(src, (src + step) % chunks) for src in range(chunks)])
-            for step in range(1, chunks)
+            for step in reversed(range(1, chunks))
         ]
     total = turn_and_sum(by_turn, gathered, classes_here, rotations, chunks, me, 0, 1)[0]
     for part in received:

time: 115 us -> 115 us (level)
  transfers between devices with their start and end apart: 12 -> 12, of which waited for: 5 -> 4; matrix products, arithmetic and copies ran while one was open for 12% -> 12% of each run, Pallas kernels for 5% -> 5%
where the time goes in v16:
time: 115 us; the launch traced here: 114 us
  waiting for transfers between devices  37.2 us (32%)
  Pallas kernels  17.4 us (15%)
  matrix products  15.2 us (13%)
  starting transfers between devices  12.6 us (11%)
  other arithmetic  12.5 us (11%)
  blocking collectives  9.22 us (8%)
  local copies, waits for them, and re-layouts  9.01 us (8%)
    pallas_call x2, Pallas kernels, turn_and_sum(): pl.pallas_call(functools.partial(turn_sum_kernel, classes_here, rotations...  17.4 us
    ppermute x3, waiting for transfers between devices, per_device(): lax.ppermute(outgoing[step - 1], 'img', [(src, (src + step) % chunks) for...  15.7 us
    dot_general x1, matrix products, per_device(): lax.dot_general(gathered, references, (((1,), (1,)), ((), ())), preferred...  15.2 us
    ppermute x1, waiting for transfers between devices, ring_gather(): from_prev = lax.ppermute(from_prev, 'ref', to_next)  12.1 us
    ppermute x1, waiting for transfers between devices, ring_gather(): top = lax.ppermute(from_prev[:half], 'ref', to_next)  9.43 us
    all_gather x1, blocking collectives, per_device(): stats = lax.all_gather(in_group_order, 'ref', axis=0)  9.22 us
    ppermute x5, starting transfers between devices, ring_gather(): arrays += [lax.ppermute(piece[0], 'ref', to_partner) for piece in pieces]  7.07 us
    dot_general x1, other arithmetic, per_device(): jnp.einsum('jp,jp->j', references, references, preferred_element_type=jnp...  7 us
  transfers between devices with their start and end apart: 12, of which 4 were waited for; matrix products, arithmetic and copies ran while one was open for 12% of the time, Pallas kernels for 5%

profile of v16, /device:TPU:17, one launch (start us, length us, event | category | flops | bytes accessed | tf_op | source)
XLA Modules:
  0.0 114.2 jit_solution(15832201763716664172)
XLA Ops:
  0.6 1.3 %collective-permute-start = (bf16[64,9216]{1,0:T(8,128)(2,1)}, bf16[64,9216]{1,0:T(8,128)(2,1)S(1)}, u32[]{:S(2)}, u32[]{:S(2)}) collective-permute-start(bf16[64,9216]{1,0:T(8,128)(2,1)} %param.7), channel_id=1, source_target_pairs={{0,2},{1,3},{2,6},{3,7},{4,0},{5,1},{6,4},{7,5},{8,10},{9,11},{10,... | collective-permute-start | bytes 3538952 | tf_op jit(solution)/shard_map/ppermute | solution.py:116
  2.2 1.2 %collective-permute-start.4 = (bf16[64,9216]{1,0:T(8,128)(2,1)}, bf16[64,9216]{1,0:T(8,128)(2,1)}, u32[]{:S(2)}, u32[]{:S(2)}) collective-permute-start(bf16[64,9216]{1,0:T(8,128)(2,1)} %param.7), channel_id=1, source_target_pairs={{0,1},{1,0},{2,3},{3,2},{4,5},{5,4},{6,7},{7,6},{8,9},{9,8},{10,11... | collective-permute-start | bytes 3538952 | tf_op jit(solution)/shard_map/ppermute | solution.py:125
  3.4 0.7 constant_dynamic-slice_fusion
  4.1 0.6 compare_select_fusion.1
  4.7 0.6 compare_and_fusion.1
  5.3 0.6 compare_select_fusion
  5.9 0.6 compare_and_fusion
  6.5 0.6 and_select_fusion.angle_ref
  7.1 0.7 log.3
  7.9 7.0 %fusion = f32[864]{0:T(1024)S(1)} fusion(bf16[864,9216]{1,0:T(8,128)(2,1)} %param.8), kind=kLoop, calls=%fused_computation.3 | loop fusion | flops 23887008 | bytes 15928704 | tf_op jit(solution)/shard_map/jp,jp->j/dot_general | solution.py:143
  14.9 0.6 multiply_subtract_fusion
  15.7 12.1 %collective-permute-done = bf16[64,9216]{1,0:T(8,128)(2,1)S(1)} collective-permute-done((bf16[64,9216]{1,0:T(8,128)(2,1)}, bf16[64,9216]{1,0:T(8,128)(2,1)S(1)}, u32[]{:S(2)}, u32[]{:S(2)}) %collective-permute-start) | collective-permute-done | bytes 1179680 | tf_op jit(solution)/shard_map/ppermute | solution.py:116
  27.8 1.3 %collective-permute-start.2 = (bf16[32,9216]{1,0:T(8,128)(2,1)S(1)}, bf16[32,9216]{1,0:T(8,128)(2,1)S(1)}, u32[]{:S(2)}, u32[]{:S(2)}) collective-permute-start(bf16[32,9216]{1,0:T(8,128)(2,1)S(1)} %slice.37), channel_id=1, source_target_pairs={{0,2},{1,3},{2,6},{3,7},{4,0},{5,1},{6,4},{7,5},{8,10},{9,11},{10,... | collective-permute-start | bytes 1769480 | tf_op jit(solution)/shard_map/ppermute | solution.py:121
  29.4 2.1 %collective-permute-start.5 = (bf16[64,9216]{1,0:T(8,128)(2,1)S(1)}, bf16[64,9216]{1,0:T(8,128)(2,1)S(1)}, u32[]{:S(2)}, u32[]{:S(2)}) collective-permute-start(bf16[64,9216]{1,0:T(8,128)(2,1)S(1)} %collective-permute-done), channel_id=1, source_target_pairs={{0,1},{1,0},{2,3},{3,2},{4,5},{5,4},{6,7},{7,6},{8,9},{9,8},{10,11... | collective-permute-start | bytes 3538952 | tf_op jit(solution)/shard_map/ppermute | solution.py:125
  31.7 9.4 %collective-permute-done.2 = bf16[32,9216]{1,0:T(8,128)(2,1)S(1)} collective-permute-done((bf16[32,9216]{1,0:T(8,128)(2,1)S(1)}, bf16[32,9216]{1,0:T(8,128)(2,1)S(1)}, u32[]{:S(2)}, u32[]{:S(2)}) %collective-permute-start.2) | collective-permute-done | bytes 589856 | tf_op jit(solution)/shard_map/ppermute | solution.py:121
  41.1 2.5 %collective-permute-start.7 = (bf16[32,9216]{1,0:T(8,128)(2,1)S(1)}, bf16[32,9216]{1,0:T(8,128)(2,1)S(1)}, u32[]{:S(2)}, u32[]{:S(2)}) collective-permute-start(bf16[32,9216]{1,0:T(8,128)(2,1)S(1)} %collective-permute-done.2), channel_id=1, source_target_pairs={{0,1},{1,0},{2,3},{3,2},{4,5},{5,4},{6,7},{7,6},{8,9},{9,8},{10,11... | collective-permute-start | bytes 1769480 | tf_op jit(solution)/shard_map/ppermute | solution.py:125
  43.6 1.3 %collective-permute-start.8 = (bf16[32,9216]{1,0:T(8,128)(2,1)S(1)}, bf16[32,9216]{1,0:T(8,128)(2,1)S(1)}, u32[]{:S(2)}, u32[]{:S(2)}) collective-permute-start(bf16[32,9216]{1,0:T(8,128)(2,1)S(1)} %collective-permute-done.3), channel_id=1, source_target_pairs={{0,1},{1,0},{2,3},{3,2},{4,5},{5,4},{6,7},{7,6},{8,9},{9,8},{10,11... | collective-permute-start | bytes 1769480 | tf_op jit(solution)/shard_map/ppermute | solution.py:125
  44.9 1.3 %constant_dynamic-update-slice_fusion.4 = bf16[512,9216]{1,0:T(8,128)(2,1)S(1)} fusion(bf16[512,9216]{1,0:T(8,128)(2,1)S(1)} %constant_dynamic-update-slice_fusion.5, bf16[64,9216]{1,0:T(8,128)(2,1)} %collective-permute-done.4), kind=kLoop, calls=%fused_computation.17 | loop fusion | bytes 2359296
  46.6 15.2 %fusion.5 = (f32[512]{0:T(512)S(1)}, f32[512,864]{0,1:T(8,128)S(1)}) fusion(f32[864]{0:T(1024)S(1)} %copy-done.4, bf16[512,9216]{1,0:T(8,128)(2,1)S(1)} %constant_dynamic-update-slice_fusion.images_ref, bf16[864,9216]{1,0:T(8,128)(2,1)} %param.8), kind=kOutput, calls=%fused_computation.42 | convolution fusion | flops 8154611200 | bytes 27137408 | tf_op jit(solution)/shard_map/dot_general | solution.py:152
  62.4 1.0 gather_fusion
  63.7 9.2 %all-gather.1 = f32[8,2,512]{2,1,0:T(2,128)S(1)} all-gather(f32[1,2,512]{2,1,0:T(2,128)S(1)} %copy.20), channel_id=2, replica_groups=mesh['img'=4,'ref'=8] {'ref'}, dimensions={0}, use_global_device_ids=true | all-gather | bytes 36864 | tf_op jit(solution)/shard_map/all_gather | solution.py:159
  73.1 1.0 gather_fusion.1
  75.1 1.2 %copy.24 = bf16[36,24,512]{2,1,0:T(8,128)(2,1)} copy(bf16[36,24,512]{2,0,1:T(8,128)(2,1)S(1)} %bitcast.33) | data formatting | bytes 1769472 | tf_op jit(solution)/shard_map/transpose | solution.py:167
  76.3 11.9 %shard_map.69 = (f32[24,2432]{1,0:T(8,128)}, f32[24,2432]{1,0:T(8,128)}, f32[24,2432]{1,0:T(8,128)}) custom-call(s32[1]{0:T(128)} %bitcast.me_ref, bf16[864,512]{1,0:T(8,128)(2,1)} %bitcast.34, bf16[512,9216]{1,0:T(8,128)(2,1)} %copy-done, s32[1,2304]{1,0:T(1,128)} %and_select_fusion.angle_ref), custom_call_target="tpu_custom_call" | custom-call | flops 6115295232 | bytes 8626176 | tf_op jit(solution)/shard_map/pallas_call | solution.py:61
  88.2 1.3 %collective-permute-start.11 = (f32[24,2432]{1,0:T(8,128)}, f32[24,2432]{1,0:T(8,128)S(1)}, u32[]{:S(2)}, u32[]{:S(2)}) collective-permute-start(f32[24,2432]{1,0:T(8,128)} %get-tuple-element.8), channel_id=1, source_target_pairs={{0,8},{8,16},{16,24},{24,0},{1,9},{9,17},{17,25},{25,1},{2,10},{10... | collective-permute-start | bytes 700424 | tf_op jit(solution)/shard_map/ppermute | solution.py:173
  89.5 1.1 collective-permute-start.9
  90.6 5.6 %shard_map.68 = f32[24,2432]{1,0:T(8,128)} custom-call(s32[1]{0:T(128)} %bitcast.me_ref, bf16[864,512]{1,0:T(8,128)(2,1)} %bitcast.35, bf16[512,9216]{1,0:T(8,128)(2,1)} %copy-done, s32[1,2304]{1,0:T(1,128)} %and_select_fusion.angle_ref), custom_call_target="tpu_custom_call" | custom-call | flops 2038431744 | bytes 3465216 | tf_op jit(solution)/shard_map/pallas_call | solution.py:61
  96.2 7.3 %collective-permute-done.10 = f32[24,2432]{1,0:T(8,128)S(1)} collective-permute-done((f32[24,2432]{1,0:T(8,128)}, f32[24,2432]{1,0:T(8,128)S(1)}, u32[]{:S(2)}, u32[]{:S(2)}) %collective-permute-start.10) | collective-permute-done | bytes 233504 | tf_op jit(solution)/shard_map/ppermute | solution.py:173
  103.5 8.4 %collective-permute-done.11 = f32[24,2432]{1,0:T(8,128)S(1)} collective-permute-done((f32[24,2432]{1,0:T(8,128)}, f32[24,2432]{1,0:T(8,128)S(1)}, u32[]{:S(2)}, u32[]{:S(2)}) %collective-permute-start.11) | collective-permute-done | bytes 233504 | tf_op jit(solution)/shard_map/ppermute | solution.py:173
  111.9 1.0 add_add_fusion
  112.9 0.7 slice.43
  113.6 0.6 slice_reduce_fusion.2
  (54 shorter events, 3.3 us)
Async XLA Ops:
  0.6 15.0 %copy-start.1 = (bf16[64,9216]{1,0:T(8,128)(2,1)S(1)}, bf16[64,9216]{1,0:T(8,128)(2,1)}, u32[]{:S(2)}) copy-start(bf16[64,9216]{1,0:T(8,128)(2,1)} %param.7) | copy-start | bytes 3538948
  0.6 27.1 %collective-permute-start = (bf16[64,9216]{1,0:T(8,128)(2,1)}, bf16[64,9216]{1,0:T(8,128)(2,1)S(1)}, u32[]{:S(2)}, u32[]{:S(2)}) collective-permute-start(bf16[64,9216]{1,0:T(8,128)(2,1)} %param.7), channel_id=1, source_target_pairs={{0,2},{1,3},{2,6},{3,7},{4,0},{5,1},{6,4},{7,5},{8,10},{9,11},{10,... | collective-permute-start | bytes 3538952 | tf_op jit(solution)/shard_map/ppermute | solution.py:116
  1.9 27.1 %collective-permute-start.1 = (bf16[64,9216]{1,0:T(8,128)(2,1)}, bf16[64,9216]{1,0:T(8,128)(2,1)S(1)}, u32[]{:S(2)}, u32[]{:S(2)}) collective-permute-start(bf16[64,9216]{1,0:T(8,128)(2,1)} %param.7), channel_id=1, source_target_pairs={{0,4},{1,5},{2,0},{3,1},{4,6},{5,7},{6,2},{7,3},{8,12},{9,13},{10,... | collective-permute-start | bytes 3538952 | tf_op jit(solution)/shard_map/ppermute | solution.py:117
  2.2 42.8 %collective-permute-start.4 = (bf16[64,9216]{1,0:T(8,128)(2,1)}, bf16[64,9216]{1,0:T(8,128)(2,1)}, u32[]{:S(2)}, u32[]{:S(2)}) collective-permute-start(bf16[64,9216]{1,0:T(8,128)(2,1)} %param.7), channel_id=1, source_target_pairs={{0,1},{1,0},{2,3},{3,2},{4,5},{5,4},{6,7},{7,6},{8,9},{9,8},{10,11... | collective-permute-start | bytes 3538952 | tf_op jit(solution)/shard_map/ppermute | solution.py:125
  7.9 7.6 %copy-start.3 = (s32[512]{0:T(512)S(1)}, s32[512]{0:T(512)}, u32[]{:S(2)}) copy-start(s32[512]{0:T(512)} %compare_select_fusion.1) | copy-start | bytes 6148
  7.9 7.6 %copy-start.2 = (s32[512]{0:T(512)S(1)}, s32[512]{0:T(512)}, u32[]{:S(2)}) copy-start(s32[512]{0:T(512)} %compare_select_fusion) | copy-start | bytes 6148
  15.7 30.9 %copy-start.4 = (f32[864]{0:T(1024)S(1)}, f32[864]{0:T(1024)}, u32[]{:S(2)}) copy-start(f32[864]{0:T(1024)} %multiply_subtract_fusion) | copy-start | bytes 10372
  27.8 13.3 %collective-permute-start.2 = (bf16[32,9216]{1,0:T(8,128)(2,1)S(1)}, bf16[32,9216]{1,0:T(8,128)(2,1)S(1)}, u32[]{:S(2)}, u32[]{:S(2)}) collective-permute-start(bf16[32,9216]{1,0:T(8,128)(2,1)S(1)} %slice.37), channel_id=1, source_target_pairs={{0,2},{1,3},{2,6},{3,7},{4,0},{5,1},{6,4},{7,5},{8,10},{9,11},{10,... | collective-permute-start | bytes 1769480 | tf_op jit(solution)/shard_map/ppermute | solution.py:121
  29.1 14.5 %collective-permute-start.3 = (bf16[32,9216]{1,0:T(8,128)(2,1)S(1)}, bf16[32,9216]{1,0:T(8,128)(2,1)S(1)}, u32[]{:S(2)}, u32[]{:S(2)}) collective-permute-start(bf16[32,9216]{1,0:T(8,128)(2,1)S(1)} %slice.38), channel_id=1, source_target_pairs={{0,4},{1,5},{2,0},{3,1},{4,6},{5,7},{6,2},{7,3},{8,12},{9,13},{10,... | collective-permute-start | bytes 1769480 | tf_op jit(solution)/shard_map/ppermute | solution.py:122
  29.4 16.9 %collective-permute-start.5 = (bf16[64,9216]{1,0:T(8,128)(2,1)S(1)}, bf16[64,9216]{1,0:T(8,128)(2,1)S(1)}, u32[]{:S(2)}, u32[]{:S(2)}) collective-permute-start(bf16[64,9216]{1,0:T(8,128)(2,1)S(1)} %collective-permute-done), channel_id=1, source_target_pairs={{0,1},{1,0},{2,3},{3,2},{4,5},{5,4},{6,7},{7,6},{8,9},{9,8},{10,11... | collective-permute-start | bytes 3538952 | tf_op jit(solution)/shard_map/ppermute | solution.py:125
  31.5 14.9 %collective-permute-start.6 = (bf16[64,9216]{1,0:T(8,128)(2,1)S(1)}, bf16[64,9216]{1,0:T(8,128)(2,1)S(1)}, u32[]{:S(2)}, u32[]{:S(2)}) collective-permute-start(bf16[64,9216]{1,0:T(8,128)(2,1)S(1)} %collective-permute-done.1), channel_id=1, source_target_pairs={{0,1},{1,0},{2,3},{3,2},{4,5},{5,4},{6,7},{7,6},{8,9},{9,8},{10,11... | collective-permute-start | bytes 3538952 | tf_op jit(solution)/shard_map/ppermute | solution.py:125
  41.1 5.4 %collective-permute-start.7 = (bf16[32,9216]{1,0:T(8,128)(2,1)S(1)}, bf16[32,9216]{1,0:T(8,128)(2,1)S(1)}, u32[]{:S(2)}, u32[]{:S(2)}) collective-permute-start(bf16[32,9216]{1,0:T(8,128)(2,1)S(1)} %collective-permute-done.2), channel_id=1, source_target_pairs={{0,1},{1,0},{2,3},{3,2},{4,5},{5,4},{6,7},{7,6},{8,9},{9,8},{10,11... | collective-permute-start | bytes 1769480 | tf_op jit(solution)/shard_map/ppermute | solution.py:125
  43.6 2.9 %collective-permute-start.8 = (bf16[32,9216]{1,0:T(8,128)(2,1)S(1)}, bf16[32,9216]{1,0:T(8,128)(2,1)S(1)}, u32[]{:S(2)}, u32[]{:S(2)}) collective-permute-start(bf16[32,9216]{1,0:T(8,128)(2,1)S(1)} %collective-permute-done.3), channel_id=1, source_target_pairs={{0,1},{1,0},{2,3},{3,2},{4,5},{5,4},{6,7},{7,6},{8,9},{9,8},{10,11... | collective-permute-start | bytes 1769480 | tf_op jit(solution)/shard_map/ppermute | solution.py:125
  46.6 15.3 %copy-start = (bf16[512,9216]{1,0:T(8,128)(2,1)}, bf16[512,9216]{1,0:T(8,128)(2,1)S(1)}, u32[]{:S(2)}) copy-start(bf16[512,9216]{1,0:T(8,128)(2,1)S(1)} %constant_dynamic-update-slice_fusion.images_ref) | copy-start | bytes 28311556
  46.6 16.8 %copy-start.6 = (pred[512]{0:T(512)(128)(4,1)S(1)}, pred[512]{0:T(512)(128)(4,1)}, u32[]{:S(2)}) copy-start(pred[512]{0:T(512)(128)(4,1)} %compare_and_fusion.1) | copy-start | bytes 1540
  46.6 27.5 %copy-start.5 = (pred[512]{0:T(512)(128)(4,1)S(1)}, pred[512]{0:T(512)(128)(4,1)}, u32[]{:S(2)}) copy-start(pred[512]{0:T(512)(128)(4,1)} %compare_and_fusion) | copy-start | bytes 1540
  88.1 15.3 %collective-permute-start.10 = (f32[24,2432]{1,0:T(8,128)}, f32[24,2432]{1,0:T(8,128)S(1)}, u32[]{:S(2)}, u32[]{:S(2)}) collective-permute-start(f32[24,2432]{1,0:T(8,128)} %get-tuple-element.7), channel_id=1, source_target_pairs={{0,16},{8,24},{16,0},{24,8},{1,17},{9,25},{17,1},{25,9},{2,18},{10... | collective-permute-start | bytes 700424 | tf_op jit(solution)/shard_map/ppermute | solution.py:173
  88.2 23.7 %collective-permute-start.11 = (f32[24,2432]{1,0:T(8,128)}, f32[24,2432]{1,0:T(8,128)S(1)}, u32[]{:S(2)}, u32[]{:S(2)}) collective-permute-start(f32[24,2432]{1,0:T(8,128)} %get-tuple-element.8), channel_id=1, source_target_pairs={{0,8},{8,16},{16,24},{24,0},{1,9},{9,17},{17,25},{25,1},{2,10},{10... | collective-permute-start | bytes 700424 | tf_op jit(solution)/shard_map/ppermute | solution.py:173
  89.5 22.4 %collective-permute-start.9 = (f32[24,2432]{1,0:T(8,128)}, f32[24,2432]{1,0:T(8,128)S(1)}, u32[]{:S(2)}, u32[]{:S(2)}) collective-permute-start(f32[24,2432]{1,0:T(8,128)} %get-tuple-element.6), channel_id=1, source_target_pairs={{0,24},{8,0},{16,8},{24,16},{1,25},{9,1},{17,9},{25,17},{2,26},{10... | collective-permute-start | bytes 700424 | tf_op jit(solution)/shard_map/ppermute | solution.py:173

commit v17 on v16

--- a/solution.py
+++ b/solution.py
@@ -49,14 +49,15 @@
             target[...] = out_ref[...]
 
 
-def turn_and_sum(by_turn, gathered, classes_here, rotations, chunks, me, first, count):
+def turn_and_sum(by_turn, gathered, classes_here, rotations, chunks, chunk_ids):
     local_refs, n = by_turn.shape
     pixels = gathered.shape[1]
     width = pixels // chunks
+    count = chunk_ids.shape[0]
     angle = (jnp.arange(width, dtype=jnp.int32) % ANG).reshape(1, width)
 
-    def chunk_of(t, me_ref):
-        return (0, (me_ref[0] + first + t) % chunks)
+    def chunk_of(t, ids_ref):
+        return (0, ids_ref[t])
 
     return pl.pallas_call(
         functools.partial(turn_sum_kernel, classes_here, rotations, count),
@@ -86,7 +87,7 @@
             bytes_accessed=2 * local_refs * n + 2 * n * width * count + 4 * classes_here * width * count,
             transcendentals=0,
         ),
-    )(jnp.reshape(me, (1,)).astype(jnp.int32), by_turn, gathered, angle)
+    )(chunk_ids.astype(jnp.int32), by_turn, gathered, angle)
 
 def ring_order(chips):
     if chips == 4:
@@ -168,12 +169,16 @@
     me = lax.axis_index("img")
     received = []
     if chunks > 1:
-        outgoing = turn_and_sum(by_turn, gathered, classes_here, rotations, chunks, me, 1, chunks - 1)
-        received = [
-            lax.ppermute(outgoing[step - 1], "img", [(src, (src + step) % chunks) for src in range(chunks)])
-            for step in reversed(range(1, chunks))
-        ]
-    total = turn_and_sum(by_turn, gathered, classes_here, rotations, chunks, me, 0, 1)[0]
+        order = [chunks // 2] + [step for step in range(1, chunks) if step != chunks // 2]
+        for steps in (order[:1], order[1:]):
+            if not steps:
+                continue
+            ids = (me + jnp.array(steps, jnp.int32)) % chunks
+            parts = turn_and_sum(by_turn, gathered, classes_here, rotations, chunks, ids)
+            for step, part in zip(steps, parts):
+                perm = [(src, (src + step) % chunks) for src in range(chunks)]
+                received.append(lax.ppermute(part, "img", perm))
+    total = turn_and_sum(by_turn, gathered, classes_here, rotations, chunks, jnp.reshape(me, (1,)))[0]
     for part in received:
         total = total + part
     width = pixels // chunks

time: 115 us -> 112 us (0.974)
  the two profiles are of different devices: /device:TPU:17 before, /device:TPU:0 now
where the time goes in v17:
time: 112 us; the launch traced here: 111 us
  waiting for transfers between devices  31.2 us (28%)
  Pallas kernels  20.5 us (18%)
  matrix products  15.2 us (14%)
  other arithmetic  13.1 us (12%)
  starting transfers between devices  12.1 us (11%)
  blocking collectives  9.26 us (8%)
  local copies, waits for them, and re-layouts  9 us (8%)
    pallas_call x3, Pallas kernels, turn_and_sum(): pl.pallas_call(functools.partial(turn_sum_kernel, classes_here, rotations...  20.5 us
    dot_general x1, matrix products, per_device(): lax.dot_general(gathered, references, (((1,), (1,)), ((), ())), preferred...  15.2 us
    ppermute x1, waiting for transfers between devices, ring_gather(): from_prev = lax.ppermute(from_prev, 'ref', to_next)  13.2 us
    ppermute x1, waiting for transfers between devices, ring_gather(): top = lax.ppermute(from_prev[:half], 'ref', to_next)  11.7 us
    all_gather x1, blocking collectives, per_device(): stats = lax.all_gather(in_group_order, 'ref', axis=0)  9.26 us
    dot_general x1, other arithmetic, per_device(): jnp.einsum('jp,jp->j', references, references, preferred_element_type=jnp...  7 us
    ppermute x3, starting transfers between devices, per_device(): received.append(lax.ppermute(part, 'img', perm))  6.41 us
    ppermute x3, waiting for transfers between devices, per_device(): received.append(lax.ppermute(part, 'img', perm))  4.76 us
  transfers between devices with their start and end apart: 12, of which 6 were waited for; matrix products, arithmetic and copies ran while one was open for 13% of the time, Pallas kernels for 13%

profile of v17, /device:TPU:0, one launch (start us, length us, event | category | flops | bytes accessed | tf_op | source)
XLA Modules:
  0.0 111.4 jit_solution(13274595076550824319)
XLA Ops:
  0.6 3.0 %collective-permute-start = (bf16[64,9216]{1,0:T(8,128)(2,1)}, bf16[64,9216]{1,0:T(8,128)(2,1)S(1)}, u32[]{:S(2)}, u32[]{:S(2)}) collective-permute-start(bf16[64,9216]{1,0:T(8,128)(2,1)} %param.9), channel_id=1, source_target_pairs={{0,2},{1,3},{2,6},{3,7},{4,0},{5,1},{6,4},{7,5},{8,10},{9,11},{10,... | collective-permute-start | bytes 3538952 | tf_op jit(solution)/shard_map/ppermute | solution.py:117
  3.7 0.7 constant_dynamic-slice_fusion
  4.5 0.6 compare_select_fusion.1
  5.0 0.6 compare_and_fusion.1
  5.6 0.6 compare_select_fusion
  6.2 0.6 compare_and_fusion
  6.8 0.6 and_select_fusion.angle_ref
  7.4 0.7 log.3
  8.2 7.0 %fusion = f32[864]{0:T(1024)S(1)} fusion(bf16[864,9216]{1,0:T(8,128)(2,1)} %param.10), kind=kLoop, calls=%fused_computation.3 | loop fusion | flops 23887008 | bytes 15928704 | tf_op jit(solution)/shard_map/jp,jp->j/dot_general | solution.py:144
  15.3 1.2 %and_select_fusion.1.me_ref = s32[2]{0:T(128)} fusion(s32[2]{0:T(128)} %constant.85.clone, s32[]{:T(128)} %axis_index.27), kind=kLoop, calls=%fused_computation.41 | loop fusion | flops 24 | bytes 20 | tf_op jit(solution)/shard_map/jit(remainder)/select_n | solution.py:176
  16.6 13.2 %collective-permute-done = bf16[64,9216]{1,0:T(8,128)(2,1)S(1)} collective-permute-done((bf16[64,9216]{1,0:T(8,128)(2,1)}, bf16[64,9216]{1,0:T(8,128)(2,1)S(1)}, u32[]{:S(2)}, u32[]{:S(2)}) %collective-permute-start) | collective-permute-done | bytes 1179680 | tf_op jit(solution)/shard_map/ppermute | solution.py:117
  29.9 1.8 %collective-permute-start.2 = (bf16[32,9216]{1,0:T(8,128)(2,1)S(1)}, bf16[32,9216]{1,0:T(8,128)(2,1)S(1)}, u32[]{:S(2)}, u32[]{:S(2)}) collective-permute-start(bf16[32,9216]{1,0:T(8,128)(2,1)S(1)} %slice.37), channel_id=1, source_target_pairs={{0,2},{1,3},{2,6},{3,7},{4,0},{5,1},{6,4},{7,5},{8,10},{9,11},{10,... | collective-permute-start | bytes 1769480 | tf_op jit(solution)/shard_map/ppermute | solution.py:122
  32.1 0.5 collective-permute-start.6
  32.7 11.7 %collective-permute-done.2 = bf16[32,9216]{1,0:T(8,128)(2,1)S(1)} collective-permute-done((bf16[32,9216]{1,0:T(8,128)(2,1)S(1)}, bf16[32,9216]{1,0:T(8,128)(2,1)S(1)}, u32[]{:S(2)}, u32[]{:S(2)}) %collective-permute-start.2) | collective-permute-done | bytes 589856 | tf_op jit(solution)/shard_map/ppermute | solution.py:122
  44.5 1.2 %collective-permute-done.3 = bf16[32,9216]{1,0:T(8,128)(2,1)S(1)} collective-permute-done((bf16[32,9216]{1,0:T(8,128)(2,1)S(1)}, bf16[32,9216]{1,0:T(8,128)(2,1)S(1)}, u32[]{:S(2)}, u32[]{:S(2)}) %collective-permute-start.3) | collective-permute-done | bytes 589856 | tf_op jit(solution)/shard_map/ppermute | solution.py:123
  45.7 1.3 %constant_dynamic-update-slice_fusion.4 = bf16[512,9216]{1,0:T(8,128)(2,1)S(1)} fusion(bf16[512,9216]{1,0:T(8,128)(2,1)S(1)} %constant_dynamic-update-slice_fusion.5, bf16[64,9216]{1,0:T(8,128)(2,1)} %collective-permute-done.4), kind=kLoop, calls=%fused_computation.17 | loop fusion | bytes 2359296
  47.7 15.2 %fusion.6 = (f32[512]{0:T(512)S(1)}, f32[512,864]{0,1:T(8,128)S(1)}) fusion(f32[864]{0:T(1024)S(1)} %multiply_subtract_fusion, bf16[512,9216]{1,0:T(8,128)(2,1)S(1)} %constant_dynamic-update-slice_fusion.images_ref, bf16[864,9216]{1,0:T(8,128)(2,1)} %param.10), kind=kOutput, calls=%fused_computation.46 | convolution fusion | flops 8154611200 | bytes 27137408 | tf_op jit(solution)/shard_map/dot_general | solution.py:153
  63.5 1.0 gather_fusion
  64.8 9.3 %all-gather.1 = f32[8,2,512]{2,1,0:T(2,128)S(1)} all-gather(f32[1,2,512]{2,1,0:T(2,128)S(1)} %copy.22), channel_id=2, replica_groups=mesh['img'=4,'ref'=8] {'ref'}, dimensions={0}, use_global_device_ids=true | all-gather | bytes 36864 | tf_op jit(solution)/shard_map/all_gather | solution.py:160
  74.3 1.0 gather_fusion.1
  76.2 1.2 %copy.26 = bf16[36,24,512]{2,1,0:T(8,128)(2,1)} copy(bf16[36,24,512]{2,0,1:T(8,128)(2,1)S(1)} %bitcast.36) | data formatting | bytes 1769472 | tf_op jit(solution)/shard_map/transpose | solution.py:168
  77.4 5.6 %shard_map.87 = f32[24,2432]{1,0:T(8,128)} custom-call(s32[1]{0:T(128)S(6)} %select_n.47.me_ref, bf16[864,512]{1,0:T(8,128)(2,1)} %bitcast.33, bf16[512,9216]{1,0:T(8,128)(2,1)} %copy-done, s32[1,2304]{1,0:T(1,128)} %and_select_fusion.angle_ref), custom_call_target="tpu_custom_call" | custom-call | flops 2038431744 | bytes 3465216 | tf_op jit(solution)/shard_map/pallas_call | solution.py:62
  83.0 2.6 %collective-permute-start.9 = (f32[24,2432]{1,0:T(8,128)}, f32[24,2432]{1,0:T(8,128)S(1)}, u32[]{:S(2)}, u32[]{:S(2)}) collective-permute-start(f32[24,2432]{1,0:T(8,128)} %shard_map.87), channel_id=1, source_target_pairs={{0,16},{8,24},{16,0},{24,8},{1,17},{9,25},{17,1},{25,9},{2,18},{10... | collective-permute-start | bytes 700424 | tf_op jit(solution)/shard_map/ppermute | solution.py:180
  85.5 9.4 %shard_map.88 = (f32[24,2432]{1,0:T(8,128)}, f32[24,2432]{1,0:T(8,128)}) custom-call(s32[2]{0:T(128)} %and_select_fusion.1.me_ref, bf16[864,512]{1,0:T(8,128)(2,1)} %bitcast.34, bf16[512,9216]{1,0:T(8,128)(2,1)} %copy-done, s32[1,2304]{1,0:T(1,128)} %and_select_fusion.angle_ref), custom_call_target="tpu_custom_call" | custom-call | flops 4076863488 | bytes 6045696 | tf_op jit(solution)/shard_map/pallas_call | solution.py:62
  94.9 1.6 %collective-permute-start.10 = (f32[24,2432]{1,0:T(8,128)}, f32[24,2432]{1,0:T(8,128)S(1)}, u32[]{:S(2)}, u32[]{:S(2)}) collective-permute-start(f32[24,2432]{1,0:T(8,128)} %get-tuple-element.5), channel_id=1, source_target_pairs={{0,8},{8,16},{16,24},{24,0},{1,9},{9,17},{17,25},{25,1},{2,10},{10... | collective-permute-start | bytes 700424 | tf_op jit(solution)/shard_map/ppermute | solution.py:180
  96.5 2.2 %collective-permute-start.11 = (f32[24,2432]{1,0:T(8,128)}, f32[24,2432]{1,0:T(8,128)S(1)}, u32[]{:S(2)}, u32[]{:S(2)}) collective-permute-start(f32[24,2432]{1,0:T(8,128)} %get-tuple-element.6), channel_id=1, source_target_pairs={{0,24},{8,0},{16,8},{24,16},{1,25},{9,1},{17,9},{25,17},{2,26},{10... | collective-permute-start | bytes 700424 | tf_op jit(solution)/shard_map/ppermute | solution.py:180
  98.8 5.6 %shard_map.86 = f32[24,2432]{1,0:T(8,128)} custom-call(s32[1]{0:T(128)} %bitcast.me_ref, bf16[864,512]{1,0:T(8,128)(2,1)} %bitcast.35, bf16[512,9216]{1,0:T(8,128)(2,1)} %copy-done, s32[1,2304]{1,0:T(1,128)} %and_select_fusion.angle_ref), custom_call_target="tpu_custom_call" | custom-call | flops 2038431744 | bytes 3465216 | tf_op jit(solution)/shard_map/pallas_call | solution.py:62
  104.3 1.2 %collective-permute-done.10 = f32[24,2432]{1,0:T(8,128)S(1)} collective-permute-done((f32[24,2432]{1,0:T(8,128)}, f32[24,2432]{1,0:T(8,128)S(1)}, u32[]{:S(2)}, u32[]{:S(2)}) %collective-permute-start.10) | collective-permute-done | bytes 233504 | tf_op jit(solution)/shard_map/ppermute | solution.py:180
  105.5 3.5 %collective-permute-done.11 = f32[24,2432]{1,0:T(8,128)S(1)} collective-permute-done((f32[24,2432]{1,0:T(8,128)}, f32[24,2432]{1,0:T(8,128)S(1)}, u32[]{:S(2)}, u32[]{:S(2)}) %collective-permute-start.11) | collective-permute-done | bytes 233504 | tf_op jit(solution)/shard_map/ppermute | solution.py:180
  109.1 1.0 add_add_fusion
  110.1 0.7 slice.43
  110.8 0.6 slice_reduce_fusion.2
  (54 shorter events, 3.5 us)
Async XLA Ops:
  0.6 15.9 %copy-start.1 = (bf16[64,9216]{1,0:T(8,128)(2,1)S(1)}, bf16[64,9216]{1,0:T(8,128)(2,1)}, u32[]{:S(2)}) copy-start(bf16[64,9216]{1,0:T(8,128)(2,1)} %param.9) | copy-start | bytes 3538948
  0.6 29.2 %collective-permute-start = (bf16[64,9216]{1,0:T(8,128)(2,1)}, bf16[64,9216]{1,0:T(8,128)(2,1)S(1)}, u32[]{:S(2)}, u32[]{:S(2)}) collective-permute-start(bf16[64,9216]{1,0:T(8,128)(2,1)} %param.9), channel_id=1, source_target_pairs={{0,2},{1,3},{2,6},{3,7},{4,0},{5,1},{6,4},{7,5},{8,10},{9,11},{10,... | collective-permute-start | bytes 3538952 | tf_op jit(solution)/shard_map/ppermute | solution.py:117
  3.6 28.0 %collective-permute-start.1 = (bf16[64,9216]{1,0:T(8,128)(2,1)}, bf16[64,9216]{1,0:T(8,128)(2,1)S(1)}, u32[]{:S(2)}, u32[]{:S(2)}) collective-permute-start(bf16[64,9216]{1,0:T(8,128)(2,1)} %param.9), channel_id=1, source_target_pairs={{0,4},{1,5},{2,0},{3,1},{4,6},{5,7},{6,2},{7,3},{8,12},{9,13},{10,... | collective-permute-start | bytes 3538952 | tf_op jit(solution)/shard_map/ppermute | solution.py:118
  3.7 42.0 %collective-permute-start.4 = (bf16[64,9216]{1,0:T(8,128)(2,1)}, bf16[64,9216]{1,0:T(8,128)(2,1)}, u32[]{:S(2)}, u32[]{:S(2)}) collective-permute-start(bf16[64,9216]{1,0:T(8,128)(2,1)} %param.9), channel_id=1, source_target_pairs={{0,1},{1,0},{2,3},{3,2},{4,5},{5,4},{6,7},{7,6},{8,9},{9,8},{10,11... | collective-permute-start | bytes 3538952 | tf_op jit(solution)/shard_map/ppermute | solution.py:126
  8.2 8.2 %copy-start.3 = (s32[512]{0:T(512)S(1)}, s32[512]{0:T(512)}, u32[]{:S(2)}) copy-start(s32[512]{0:T(512)} %compare_select_fusion.1) | copy-start | bytes 6148
  8.2 8.3 %copy-start.2 = (s32[512]{0:T(512)S(1)}, s32[512]{0:T(512)}, u32[]{:S(2)}) copy-start(s32[512]{0:T(512)} %compare_select_fusion) | copy-start | bytes 6148
  29.9 14.6 %collective-permute-start.2 = (bf16[32,9216]{1,0:T(8,128)(2,1)S(1)}, bf16[32,9216]{1,0:T(8,128)(2,1)S(1)}, u32[]{:S(2)}, u32[]{:S(2)}) collective-permute-start(bf16[32,9216]{1,0:T(8,128)(2,1)S(1)} %slice.37), channel_id=1, source_target_pairs={{0,2},{1,3},{2,6},{3,7},{4,0},{5,1},{6,4},{7,5},{8,10},{9,11},{10,... | collective-permute-start | bytes 1769480 | tf_op jit(solution)/shard_map/ppermute | solution.py:122
  31.7 14.0 %collective-permute-start.3 = (bf16[32,9216]{1,0:T(8,128)(2,1)S(1)}, bf16[32,9216]{1,0:T(8,128)(2,1)S(1)}, u32[]{:S(2)}, u32[]{:S(2)}) collective-permute-start(bf16[32,9216]{1,0:T(8,128)(2,1)S(1)} %slice.38), channel_id=1, source_target_pairs={{0,4},{1,5},{2,0},{3,1},{4,6},{5,7},{6,2},{7,3},{8,12},{9,13},{10,... | collective-permute-start | bytes 1769480 | tf_op jit(solution)/shard_map/ppermute | solution.py:123
  32.1 15.0 %collective-permute-start.5 = (bf16[64,9216]{1,0:T(8,128)(2,1)S(1)}, bf16[64,9216]{1,0:T(8,128)(2,1)S(1)}, u32[]{:S(2)}, u32[]{:S(2)}) collective-permute-start(bf16[64,9216]{1,0:T(8,128)(2,1)S(1)} %collective-permute-done), channel_id=1, source_target_pairs={{0,1},{1,0},{2,3},{3,2},{4,5},{5,4},{6,7},{7,6},{8,9},{9,8},{10,11... | collective-permute-start | bytes 3538952 | tf_op jit(solution)/shard_map/ppermute | solution.py:126
  32.1 15.1 %collective-permute-start.6 = (bf16[64,9216]{1,0:T(8,128)(2,1)S(1)}, bf16[64,9216]{1,0:T(8,128)(2,1)S(1)}, u32[]{:S(2)}, u32[]{:S(2)}) collective-permute-start(bf16[64,9216]{1,0:T(8,128)(2,1)S(1)} %collective-permute-done.1), channel_id=1, source_target_pairs={{0,1},{1,0},{2,3},{3,2},{4,5},{5,4},{6,7},{7,6},{8,9},{9,8},{10,11... | collective-permute-start | bytes 3538952 | tf_op jit(solution)/shard_map/ppermute | solution.py:126
  44.5 2.8 %collective-permute-start.7 = (bf16[32,9216]{1,0:T(8,128)(2,1)S(1)}, bf16[32,9216]{1,0:T(8,128)(2,1)S(1)}, u32[]{:S(2)}, u32[]{:S(2)}) collective-permute-start(bf16[32,9216]{1,0:T(8,128)(2,1)S(1)} %collective-permute-done.2), channel_id=1, source_target_pairs={{0,1},{1,0},{2,3},{3,2},{4,5},{5,4},{6,7},{7,6},{8,9},{9,8},{10,11... | collective-permute-start | bytes 1769480 | tf_op jit(solution)/shard_map/ppermute | solution.py:126
  45.7 2.0 %collective-permute-start.8 = (bf16[32,9216]{1,0:T(8,128)(2,1)S(1)}, bf16[32,9216]{1,0:T(8,128)(2,1)S(1)}, u32[]{:S(2)}, u32[]{:S(2)}) collective-permute-start(bf16[32,9216]{1,0:T(8,128)(2,1)S(1)} %collective-permute-done.3), channel_id=1, source_target_pairs={{0,1},{1,0},{2,3},{3,2},{4,5},{5,4},{6,7},{7,6},{8,9},{9,8},{10,11... | collective-permute-start | bytes 1769480 | tf_op jit(solution)/shard_map/ppermute | solution.py:126
  47.7 15.3 %copy-start = (bf16[512,9216]{1,0:T(8,128)(2,1)}, bf16[512,9216]{1,0:T(8,128)(2,1)S(1)}, u32[]{:S(2)}) copy-start(bf16[512,9216]{1,0:T(8,128)(2,1)S(1)} %constant_dynamic-update-slice_fusion.images_ref) | copy-start | bytes 28311556
  47.7 16.8 %copy-start.5 = (pred[512]{0:T(512)(128)(4,1)S(1)}, pred[512]{0:T(512)(128)(4,1)}, u32[]{:S(2)}) copy-start(pred[512]{0:T(512)(128)(4,1)} %compare_and_fusion.1) | copy-start | bytes 1540
  47.7 27.6 %copy-start.4 = (pred[512]{0:T(512)(128)(4,1)S(1)}, pred[512]{0:T(512)(128)(4,1)}, u32[]{:S(2)}) copy-start(pred[512]{0:T(512)(128)(4,1)} %compare_and_fusion) | copy-start | bytes 1540
  83.0 21.4 %collective-permute-start.9 = (f32[24,2432]{1,0:T(8,128)}, f32[24,2432]{1,0:T(8,128)S(1)}, u32[]{:S(2)}, u32[]{:S(2)}) collective-permute-start(f32[24,2432]{1,0:T(8,128)} %shard_map.87), channel_id=1, source_target_pairs={{0,16},{8,24},{16,0},{24,8},{1,17},{9,25},{17,1},{25,9},{2,18},{10... | collective-permute-start | bytes 700424 | tf_op jit(solution)/shard_map/ppermute | solution.py:180
  94.9 10.6 %collective-permute-start.10 = (f32[24,2432]{1,0:T(8,128)}, f32[24,2432]{1,0:T(8,128)S(1)}, u32[]{:S(2)}, u32[]{:S(2)}) collective-permute-start(f32[24,2432]{1,0:T(8,128)} %get-tuple-element.5), channel_id=1, source_target_pairs={{0,8},{8,16},{16,24},{24,0},{1,9},{9,17},{17,25},{25,1},{2,10},{10... | collective-permute-start | bytes 700424 | tf_op jit(solution)/shard_map/ppermute | solution.py:180
  96.5 12.6 %collective-permute-start.11 = (f32[24,2432]{1,0:T(8,128)}, f32[24,2432]{1,0:T(8,128)S(1)}, u32[]{:S(2)}, u32[]{:S(2)}) collective-permute-start(f32[24,2432]{1,0:T(8,128)} %get-tuple-element.6), channel_id=1, source_target_pairs={{0,24},{8,0},{16,8},{24,16},{1,25},{9,1},{17,9},{25,17},{2,26},{10... | collective-permute-start | bytes 700424 | tf_op jit(solution)/shard_map/ppermute | solution.py:180

commit v18 on v17

--- a/solution.py
+++ b/solution.py
@@ -170,7 +170,7 @@
     received = []
     if chunks > 1:
         order = [chunks // 2] + [step for step in range(1, chunks) if step != chunks // 2]
-        for steps in (order[:1], order[1:]):
+        for steps in [[step] for step in order]:
             if not steps:
                 continue
             ids = (me + jnp.array(steps, jnp.int32)) % chunks

time: 112 us -> 110 us (0.982)
  waiting for transfers between devices: 31.2 us -> 28 us
  Pallas kernels: 20.5 us -> 22.2 us
    ppermute x3, waiting for transfers between devices: 4.76 us -> 0.96 us  [per_device(): received.append(lax.ppermute(part, 'img', perm))]
    pallas_call x3 -> x4, Pallas kernels: 20.5 us -> 22.2 us  [turn_and_sum(): pl.pallas_call(functools.partial(turn_sum_kernel, classes_here, rotations...]
    select_n x1 -> x0, other arithmetic: 1.21 us -> none  [per_device(): ids = (me + jnp.array(steps, jnp.int32)) % chunks]
  transfers between devices with their start and end apart: 12 -> 12, of which waited for: 6 -> 5; matrix products, arithmetic and copies ran while one was open for 13% -> 13% of each run, Pallas kernels for 13% -> 15%
where the time goes in v18:
time: 110 us; the launch traced here: 109 us
  waiting for transfers between devices  28 us (25%)
  Pallas kernels  22.2 us (20%)
  matrix products  15.2 us (14%)
  other arithmetic  12.5 us (11%)
  starting transfers between devices  12.1 us (11%)
  blocking collectives  9.26 us (8%)
  local copies, waits for them, and re-layouts  9 us (8%)
    pallas_call x4, Pallas kernels, turn_and_sum(): pl.pallas_call(functools.partial(turn_sum_kernel, classes_here, rotations...  22.2 us
    dot_general x1, matrix products, per_device(): lax.dot_general(gathered, references, (((1,), (1,)), ((), ())), preferred...  15.2 us
    ppermute x1, waiting for transfers between devices, ring_gather(): from_prev = lax.ppermute(from_prev, 'ref', to_next)  13.8 us
    ppermute x1, waiting for transfers between devices, ring_gather(): top = lax.ppermute(from_prev[:half], 'ref', to_next)  11.7 us
    all_gather x1, blocking collectives, per_device(): stats = lax.all_gather(in_group_order, 'ref', axis=0)  9.26 us
    dot_general x1, other arithmetic, per_device(): jnp.einsum('jp,jp->j', references, references, preferred_element_type=jnp...  7 us
    ppermute x3, starting transfers between devices, per_device(): received.append(lax.ppermute(part, 'img', perm))  6.42 us
    ppermute x1, starting transfers between devices, ring_gather(): from_prev = lax.ppermute(from_prev, 'ref', to_next)  2.99 us
  transfers between devices with their start and end apart: 12, of which 5 were waited for; matrix products, arithmetic and copies ran while one was open for 13% of the time, Pallas kernels for 15%

profile of v18, /device:TPU:0, one launch (start us, length us, event | category | flops | bytes accessed | tf_op | source)
XLA Modules:
  0.0 109.3 jit_solution(10442411530467124977)
XLA Ops:
  0.6 3.0 %collective-permute-start = (bf16[64,9216]{1,0:T(8,128)(2,1)}, bf16[64,9216]{1,0:T(8,128)(2,1)S(1)}, u32[]{:S(2)}, u32[]{:S(2)}) collective-permute-start(bf16[64,9216]{1,0:T(8,128)(2,1)} %param.10), channel_id=1, source_target_pairs={{0,2},{1,3},{2,6},{3,7},{4,0},{5,1},{6,4},{7,5},{8,10},{9,11},{10,... | collective-permute-start | bytes 3538952 | tf_op jit(solution)/shard_map/ppermute | solution.py:117
  3.7 0.7 constant_dynamic-slice_fusion
  4.5 0.6 compare_select_fusion.1
  5.0 0.6 compare_and_fusion.1
  5.6 0.6 compare_select_fusion
  6.2 0.6 compare_and_fusion
  6.8 0.6 and_select_fusion.angle_ref
  7.4 0.7 log.3
  8.2 7.0 %fusion = f32[864]{0:T(1024)S(1)} fusion(bf16[864,9216]{1,0:T(8,128)(2,1)} %param.11), kind=kLoop, calls=%fused_computation.3 | loop fusion | flops 23887008 | bytes 15928704 | tf_op jit(solution)/shard_map/jp,jp->j/dot_general | solution.py:144
  15.2 0.6 multiply_subtract_fusion
  16.0 13.8 %collective-permute-done = bf16[64,9216]{1,0:T(8,128)(2,1)S(1)} collective-permute-done((bf16[64,9216]{1,0:T(8,128)(2,1)}, bf16[64,9216]{1,0:T(8,128)(2,1)S(1)}, u32[]{:S(2)}, u32[]{:S(2)}) %collective-permute-start) | collective-permute-done | bytes 1179680 | tf_op jit(solution)/shard_map/ppermute | solution.py:117
  29.9 1.8 %collective-permute-start.2 = (bf16[32,9216]{1,0:T(8,128)(2,1)S(1)}, bf16[32,9216]{1,0:T(8,128)(2,1)S(1)}, u32[]{:S(2)}, u32[]{:S(2)}) collective-permute-start(bf16[32,9216]{1,0:T(8,128)(2,1)S(1)} %slice.37), channel_id=1, source_target_pairs={{0,2},{1,3},{2,6},{3,7},{4,0},{5,1},{6,4},{7,5},{8,10},{9,11},{10,... | collective-permute-start | bytes 1769480 | tf_op jit(solution)/shard_map/ppermute | solution.py:122
  32.1 0.5 collective-permute-start.6
  32.7 11.7 %collective-permute-done.2 = bf16[32,9216]{1,0:T(8,128)(2,1)S(1)} collective-permute-done((bf16[32,9216]{1,0:T(8,128)(2,1)S(1)}, bf16[32,9216]{1,0:T(8,128)(2,1)S(1)}, u32[]{:S(2)}, u32[]{:S(2)}) %collective-permute-start.2) | collective-permute-done | bytes 589856 | tf_op jit(solution)/shard_map/ppermute | solution.py:122
  44.5 1.2 %collective-permute-done.3 = bf16[32,9216]{1,0:T(8,128)(2,1)S(1)} collective-permute-done((bf16[32,9216]{1,0:T(8,128)(2,1)S(1)}, bf16[32,9216]{1,0:T(8,128)(2,1)S(1)}, u32[]{:S(2)}, u32[]{:S(2)}) %collective-permute-start.3) | collective-permute-done | bytes 589856 | tf_op jit(solution)/shard_map/ppermute | solution.py:123
  45.7 1.3 %constant_dynamic-update-slice_fusion.4 = bf16[512,9216]{1,0:T(8,128)(2,1)S(1)} fusion(bf16[512,9216]{1,0:T(8,128)(2,1)S(1)} %constant_dynamic-update-slice_fusion.5, bf16[64,9216]{1,0:T(8,128)(2,1)} %collective-permute-done.4), kind=kLoop, calls=%fused_computation.17 | loop fusion | bytes 2359296
  47.7 15.2 %fusion.5 = (f32[512]{0:T(512)S(1)}, f32[512,864]{0,1:T(8,128)S(1)}) fusion(f32[864]{0:T(1024)S(1)} %copy-done.4, bf16[512,9216]{1,0:T(8,128)(2,1)S(1)} %constant_dynamic-update-slice_fusion.images_ref, bf16[864,9216]{1,0:T(8,128)(2,1)} %param.11), kind=kOutput, calls=%fused_computation.42 | convolution fusion | flops 8154611200 | bytes 27137408 | tf_op jit(solution)/shard_map/dot_general | solution.py:153
  63.5 1.0 gather_fusion
  64.8 9.3 %all-gather.1 = f32[8,2,512]{2,1,0:T(2,128)S(1)} all-gather(f32[1,2,512]{2,1,0:T(2,128)S(1)} %copy.23), channel_id=2, replica_groups=mesh['img'=4,'ref'=8] {'ref'}, dimensions={0}, use_global_device_ids=true | all-gather | bytes 36864 | tf_op jit(solution)/shard_map/all_gather | solution.py:160
  74.3 1.0 gather_fusion.1
  76.2 1.2 %copy.27 = bf16[36,24,512]{2,1,0:T(8,128)(2,1)} copy(bf16[36,24,512]{2,0,1:T(8,128)(2,1)S(1)} %bitcast.37) | data formatting | bytes 1769472 | tf_op jit(solution)/shard_map/transpose | solution.py:168
  77.4 5.6 %shard_map.96 = f32[24,2432]{1,0:T(8,128)} custom-call(s32[1]{0:T(128)S(6)} %select_n.53.me_ref, bf16[864,512]{1,0:T(8,128)(2,1)} %bitcast.33, bf16[512,9216]{1,0:T(8,128)(2,1)} %copy-done, s32[1,2304]{1,0:T(1,128)} %and_select_fusion.angle_ref), custom_call_target="tpu_custom_call" | custom-call | flops 2038431744 | bytes 3465216 | tf_op jit(solution)/shard_map/pallas_call | solution.py:62
  83.0 2.6 %collective-permute-start.9 = (f32[24,2432]{1,0:T(8,128)}, f32[24,2432]{1,0:T(8,128)S(1)}, u32[]{:S(2)}, u32[]{:S(2)}) collective-permute-start(f32[24,2432]{1,0:T(8,128)} %shard_map.96), channel_id=1, source_target_pairs={{0,16},{8,24},{16,0},{24,8},{1,17},{9,25},{17,1},{25,9},{2,18},{10... | collective-permute-start | bytes 700424 | tf_op jit(solution)/shard_map/ppermute | solution.py:180
  85.6 5.6 %shard_map.97 = f32[24,2432]{1,0:T(8,128)} custom-call(s32[1]{0:T(128)S(6)} %select_n.54.me_ref, bf16[864,512]{1,0:T(8,128)(2,1)} %bitcast.34, bf16[512,9216]{1,0:T(8,128)(2,1)} %copy-done, s32[1,2304]{1,0:T(1,128)} %and_select_fusion.angle_ref), custom_call_target="tpu_custom_call" | custom-call | flops 2038431744 | bytes 3465216 | tf_op jit(solution)/shard_map/pallas_call | solution.py:62
  91.1 1.6 %collective-permute-start.10 = (f32[24,2432]{1,0:T(8,128)}, f32[24,2432]{1,0:T(8,128)S(1)}, u32[]{:S(2)}, u32[]{:S(2)}) collective-permute-start(f32[24,2432]{1,0:T(8,128)} %shard_map.97), channel_id=1, source_target_pairs={{0,8},{8,16},{16,24},{24,0},{1,9},{9,17},{17,25},{25,1},{2,10},{10... | collective-permute-start | bytes 700424 | tf_op jit(solution)/shard_map/ppermute | solution.py:180
  92.7 5.5 %shard_map.98 = f32[24,2432]{1,0:T(8,128)} custom-call(s32[1]{0:T(128)S(6)} %select_n.55.me_ref, bf16[864,512]{1,0:T(8,128)(2,1)} %bitcast.35, bf16[512,9216]{1,0:T(8,128)(2,1)} %copy-done, s32[1,2304]{1,0:T(1,128)} %and_select_fusion.angle_ref), custom_call_target="tpu_custom_call" | custom-call | flops 2038431744 | bytes 3465216 | tf_op jit(solution)/shard_map/pallas_call | solution.py:62
  98.2 2.2 %collective-permute-start.11 = (f32[24,2432]{1,0:T(8,128)}, f32[24,2432]{1,0:T(8,128)S(1)}, u32[]{:S(2)}, u32[]{:S(2)}) collective-permute-start(f32[24,2432]{1,0:T(8,128)} %shard_map.98), channel_id=1, source_target_pairs={{0,24},{8,0},{16,8},{24,16},{1,25},{9,1},{17,9},{25,17},{2,26},{10... | collective-permute-start | bytes 700424 | tf_op jit(solution)/shard_map/ppermute | solution.py:180
  100.5 5.6 %shard_map.95 = f32[24,2432]{1,0:T(8,128)} custom-call(s32[1]{0:T(128)} %bitcast.me_ref, bf16[864,512]{1,0:T(8,128)(2,1)} %bitcast.36, bf16[512,9216]{1,0:T(8,128)(2,1)} %copy-done, s32[1,2304]{1,0:T(1,128)} %and_select_fusion.angle_ref), custom_call_target="tpu_custom_call" | custom-call | flops 2038431744 | bytes 3465216 | tf_op jit(solution)/shard_map/pallas_call | solution.py:62
  106.0 1.0 collective-permute-done.11
  107.0 1.0 add_add_fusion
  108.0 0.7 slice.43
  108.7 0.6 slice_reduce_fusion.2
  (56 shorter events, 3.5 us)
Async XLA Ops:
  0.6 15.3 %copy-start.1 = (bf16[64,9216]{1,0:T(8,128)(2,1)S(1)}, bf16[64,9216]{1,0:T(8,128)(2,1)}, u32[]{:S(2)}) copy-start(bf16[64,9216]{1,0:T(8,128)(2,1)} %param.10) | copy-start | bytes 3538948
  0.6 29.2 %collective-permute-start = (bf16[64,9216]{1,0:T(8,128)(2,1)}, bf16[64,9216]{1,0:T(8,128)(2,1)S(1)}, u32[]{:S(2)}, u32[]{:S(2)}) collective-permute-start(bf16[64,9216]{1,0:T(8,128)(2,1)} %param.10), channel_id=1, source_target_pairs={{0,2},{1,3},{2,6},{3,7},{4,0},{5,1},{6,4},{7,5},{8,10},{9,11},{10,... | collective-permute-start | bytes 3538952 | tf_op jit(solution)/shard_map/ppermute | solution.py:117
  3.6 28.0 %collective-permute-start.1 = (bf16[64,9216]{1,0:T(8,128)(2,1)}, bf16[64,9216]{1,0:T(8,128)(2,1)S(1)}, u32[]{:S(2)}, u32[]{:S(2)}) collective-permute-start(bf16[64,9216]{1,0:T(8,128)(2,1)} %param.10), channel_id=1, source_target_pairs={{0,4},{1,5},{2,0},{3,1},{4,6},{5,7},{6,2},{7,3},{8,12},{9,13},{10,... | collective-permute-start | bytes 3538952 | tf_op jit(solution)/shard_map/ppermute | solution.py:118
  3.7 42.0 %collective-permute-start.4 = (bf16[64,9216]{1,0:T(8,128)(2,1)}, bf16[64,9216]{1,0:T(8,128)(2,1)}, u32[]{:S(2)}, u32[]{:S(2)}) collective-permute-start(bf16[64,9216]{1,0:T(8,128)(2,1)} %param.10), channel_id=1, source_target_pairs={{0,1},{1,0},{2,3},{3,2},{4,5},{5,4},{6,7},{7,6},{8,9},{9,8},{10,11... | collective-permute-start | bytes 3538952 | tf_op jit(solution)/shard_map/ppermute | solution.py:126
  8.2 7.6 %copy-start.3 = (s32[512]{0:T(512)S(1)}, s32[512]{0:T(512)}, u32[]{:S(2)}) copy-start(s32[512]{0:T(512)} %compare_select_fusion.1) | copy-start | bytes 6148
  8.2 7.6 %copy-start.2 = (s32[512]{0:T(512)S(1)}, s32[512]{0:T(512)}, u32[]{:S(2)}) copy-start(s32[512]{0:T(512)} %compare_select_fusion) | copy-start | bytes 6148
  16.0 31.7 %copy-start.4 = (f32[864]{0:T(1024)S(1)}, f32[864]{0:T(1024)}, u32[]{:S(2)}) copy-start(f32[864]{0:T(1024)} %multiply_subtract_fusion) | copy-start | bytes 10372
  29.9 14.6 %collective-permute-start.2 = (bf16[32,9216]{1,0:T(8,128)(2,1)S(1)}, bf16[32,9216]{1,0:T(8,128)(2,1)S(1)}, u32[]{:S(2)}, u32[]{:S(2)}) collective-permute-start(bf16[32,9216]{1,0:T(8,128)(2,1)S(1)} %slice.37), channel_id=1, source_target_pairs={{0,2},{1,3},{2,6},{3,7},{4,0},{5,1},{6,4},{7,5},{8,10},{9,11},{10,... | collective-permute-start | bytes 1769480 | tf_op jit(solution)/shard_map/ppermute | solution.py:122
  31.7 14.0 %collective-permute-start.3 = (bf16[32,9216]{1,0:T(8,128)(2,1)S(1)}, bf16[32,9216]{1,0:T(8,128)(2,1)S(1)}, u32[]{:S(2)}, u32[]{:S(2)}) collective-permute-start(bf16[32,9216]{1,0:T(8,128)(2,1)S(1)} %slice.38), channel_id=1, source_target_pairs={{0,4},{1,5},{2,0},{3,1},{4,6},{5,7},{6,2},{7,3},{8,12},{9,13},{10,... | collective-permute-start | bytes 1769480 | tf_op jit(solution)/shard_map/ppermute | solution.py:123
  32.1 15.0 %collective-permute-start.5 = (bf16[64,9216]{1,0:T(8,128)(2,1)S(1)}, bf16[64,9216]{1,0:T(8,128)(2,1)S(1)}, u32[]{:S(2)}, u32[]{:S(2)}) collective-permute-start(bf16[64,9216]{1,0:T(8,128)(2,1)S(1)} %collective-permute-done), channel_id=1, source_target_pairs={{0,1},{1,0},{2,3},{3,2},{4,5},{5,4},{6,7},{7,6},{8,9},{9,8},{10,11... | collective-permute-start | bytes 3538952 | tf_op jit(solution)/shard_map/ppermute | solution.py:126
  32.1 15.1 %collective-permute-start.6 = (bf16[64,9216]{1,0:T(8,128)(2,1)S(1)}, bf16[64,9216]{1,0:T(8,128)(2,1)S(1)}, u32[]{:S(2)}, u32[]{:S(2)}) collective-permute-start(bf16[64,9216]{1,0:T(8,128)(2,1)S(1)} %collective-permute-done.1), channel_id=1, source_target_pairs={{0,1},{1,0},{2,3},{3,2},{4,5},{5,4},{6,7},{7,6},{8,9},{9,8},{10,11... | collective-permute-start | bytes 3538952 | tf_op jit(solution)/shard_map/ppermute | solution.py:126
  44.5 2.8 %collective-permute-start.7 = (bf16[32,9216]{1,0:T(8,128)(2,1)S(1)}, bf16[32,9216]{1,0:T(8,128)(2,1)S(1)}, u32[]{:S(2)}, u32[]{:S(2)}) collective-permute-start(bf16[32,9216]{1,0:T(8,128)(2,1)S(1)} %collective-permute-done.2), channel_id=1, source_target_pairs={{0,1},{1,0},{2,3},{3,2},{4,5},{5,4},{6,7},{7,6},{8,9},{9,8},{10,11... | collective-permute-start | bytes 1769480 | tf_op jit(solution)/shard_map/ppermute | solution.py:126
  45.7 2.0 %collective-permute-start.8 = (bf16[32,9216]{1,0:T(8,128)(2,1)S(1)}, bf16[32,9216]{1,0:T(8,128)(2,1)S(1)}, u32[]{:S(2)}, u32[]{:S(2)}) collective-permute-start(bf16[32,9216]{1,0:T(8,128)(2,1)S(1)} %collective-permute-done.3), channel_id=1, source_target_pairs={{0,1},{1,0},{2,3},{3,2},{4,5},{5,4},{6,7},{7,6},{8,9},{9,8},{10,11... | collective-permute-start | bytes 1769480 | tf_op jit(solution)/shard_map/ppermute | solution.py:126
  47.7 15.3 %copy-start = (bf16[512,9216]{1,0:T(8,128)(2,1)}, bf16[512,9216]{1,0:T(8,128)(2,1)S(1)}, u32[]{:S(2)}) copy-start(bf16[512,9216]{1,0:T(8,128)(2,1)S(1)} %constant_dynamic-update-slice_fusion.images_ref) | copy-start | bytes 28311556
  47.7 16.8 %copy-start.6 = (pred[512]{0:T(512)(128)(4,1)S(1)}, pred[512]{0:T(512)(128)(4,1)}, u32[]{:S(2)}) copy-start(pred[512]{0:T(512)(128)(4,1)} %compare_and_fusion.1) | copy-start | bytes 1540
  47.7 27.6 %copy-start.5 = (pred[512]{0:T(512)(128)(4,1)S(1)}, pred[512]{0:T(512)(128)(4,1)}, u32[]{:S(2)}) copy-start(pred[512]{0:T(512)(128)(4,1)} %compare_and_fusion) | copy-start | bytes 1540
  83.0 23.1 %collective-permute-start.9 = (f32[24,2432]{1,0:T(8,128)}, f32[24,2432]{1,0:T(8,128)S(1)}, u32[]{:S(2)}, u32[]{:S(2)}) collective-permute-start(f32[24,2432]{1,0:T(8,128)} %shard_map.96), channel_id=1, source_target_pairs={{0,16},{8,24},{16,0},{24,8},{1,17},{9,25},{17,1},{25,9},{2,18},{10... | collective-permute-start | bytes 700424 | tf_op jit(solution)/shard_map/ppermute | solution.py:180
  91.1 14.9 %collective-permute-start.10 = (f32[24,2432]{1,0:T(8,128)}, f32[24,2432]{1,0:T(8,128)S(1)}, u32[]{:S(2)}, u32[]{:S(2)}) collective-permute-start(f32[24,2432]{1,0:T(8,128)} %shard_map.97), channel_id=1, source_target_pairs={{0,8},{8,16},{16,24},{24,0},{1,9},{9,17},{17,25},{25,1},{2,10},{10... | collective-permute-start | bytes 700424 | tf_op jit(solution)/shard_map/ppermute | solution.py:180
  98.2 8.8 %collective-permute-start.11 = (f32[24,2432]{1,0:T(8,128)}, f32[24,2432]{1,0:T(8,128)S(1)}, u32[]{:S(2)}, u32[]{:S(2)}) collective-permute-start(f32[24,2432]{1,0:T(8,128)} %shard_map.98), channel_id=1, source_target_pairs={{0,24},{8,0},{16,8},{24,16},{1,25},{9,1},{17,9},{25,17},{2,26},{10... | collective-permute-start | bytes 700424 | tf_op jit(solution)/shard_map/ppermute | solution.py:180
